TPU v7x, 512 devices: a whole 4x4x16 slice. The times are simulated.
512 devices in a mesh: grp: 16 (over x, y), clu: 32 (over z, core).
Axes of the slice: x: 4, y: 4, z: 16, core: 2. Of those that a mesh axis runs over, the one named last changes fastest.
Arguments:
- lower_inverse: bfloat16 [32, 2, 512, 512], P('clu', None, 'grp'), as said below
- upper_inverse: bfloat16 [32, 2, 512, 512], P('clu', None, 'grp'), as said below
- lower_factors: bfloat16 [32, 128, 2, 48, 512], P('clu', 'grp'), may hold values from -1.2578125 to 1.2578125
- upper_factors: bfloat16 [32, 128, 2, 48, 512], P('clu', 'grp'), may hold values from -1.2578125 to 1.2578125
- lower_ranks: int32 [32, 128], P('clu', 'grp'), may hold values from 16 to 48
- upper_ranks: int32 [32, 128], P('clu', 'grp'), may hold values from 16 to 48
- pivots: int32 [32, 512], P('clu'), may hold values from 0 to 511, each once within a row
- pair_lower: int32 [32, 512], P('clu', 'grp'), may hold values from 0 to 7
- pair_upper: int32 [32, 512], P('clu', 'grp'), may hold values from 0 to 7
- pair_owner: int32 [32, 512, 1], P('clu', 'grp'), may hold values from 0 to 31; in each aligned block of 32 rows (0 to 31, 32 to 63, ..., all dimensions but the last counted through in order) at most 2 rows name the same one
Outputs:
- lower_solved: bfloat16 [32, 128, 2, 48, 512], P('clu', 'grp')
- upper_solved: bfloat16 [32, 128, 2, 48, 512], P('clu', 'grp')
- arrived: bfloat16 [32, 16, 32, 2, 2, 2304], P('clu', 'grp')
Inputs may be any that keep to these rules, and one draw needn't show every extreme that they name: `lower_inverse`: each cluster's matrix is unit lower triangular: zeros above the diagonal, one on the real part's diagonal and zero on the imaginary part's. `upper_inverse`: each cluster's matrix is upper triangular: zeros below the diagonal in both parts. `pair_owner`: among the 32 pairs of one share, at most 2 name the same owner, and some share reaches it.
All inputs are finite; a program needn't handle non-finite values.
Results may differ from a plain program's by a relative error of at most 0.0058.
Values may be sent and summed in bfloat16 or wider, within the bound.
No kernel may reach another device: no remote copies, remote signals or barrier semaphores. Data moves between devices by JAX's collectives and lax.ppermute only.
A program may use at most 64 MiB of HBM per device.

v0:
```python
import jax
import jax.numpy as jnp
from jax import lax
from jax.sharding import PartitionSpec as P

SEND_CAP = 2


def mask_rows(factors, block_ranks):
    rank_width = factors.shape[2]
    row_index = lax.broadcasted_iota(jnp.int32, (factors.shape[0], rank_width), 1)
    row_mask = row_index < block_ranks[:, None]
    return jnp.where(row_mask[:, None, :, None], factors, jnp.zeros((), factors.dtype))


def product(left, right):
    return jnp.einsum("prb,psb->prs", left, right, preferred_element_type=jnp.float32)


def per_device(
    lower_inverse,
    upper_inverse,
    lower_factors,
    upper_factors,
    lower_ranks,
    upper_ranks,
    pivots,
    pair_lower,
    pair_upper,
    pair_owner,
):
    lower_masked = mask_rows(lower_factors[0], lower_ranks[0])
    upper_masked = mask_rows(upper_factors[0], upper_ranks[0])
    upper_pivoted = jnp.take(upper_masked, pivots[0], axis=3)
    block_count = lower_masked.shape[0]
    rank_width = lower_masked.shape[2]
    panel_count = lower_masked.shape[3]
    lower_real = lower_masked[:, 0].reshape(block_count * rank_width, panel_count)
    lower_imag = lower_masked[:, 1].reshape(block_count * rank_width, panel_count)
    upper_real = upper_pivoted[:, 0].reshape(block_count * rank_width, panel_count)
    upper_imag = upper_pivoted[:, 1].reshape(block_count * rank_width, panel_count)
    contract_last = (((1,), (1,)), ((), ()))
    lower_piece = lax.all_gather(lower_inverse, "grp", axis=2, tiled=True)
    upper_piece = lax.all_gather(upper_inverse, "grp", axis=2, tiled=True)
    piece_real = upper_piece[0, 0]
    piece_imag = upper_piece[0, 1]
    real_part = jnp.dot(lower_real, piece_real, preferred_element_type=jnp.float32) - jnp.dot(
        lower_imag, piece_imag, preferred_element_type=jnp.float32
    )
    imag_part = jnp.dot(lower_real, piece_imag, preferred_element_type=jnp.float32) + jnp.dot(
        lower_imag, piece_real, preferred_element_type=jnp.float32
    )
    lower_totals = jnp.stack([real_part, imag_part], 0)
    piece_real = lower_piece[0, 0]
    piece_imag = lower_piece[0, 1]
    real_part = lax.dot_general(
        upper_real, piece_real, contract_last, preferred_element_type=jnp.float32
    ) - lax.dot_general(upper_imag, piece_imag, contract_last, preferred_element_type=jnp.float32)
    imag_part = lax.dot_general(
        upper_real, piece_imag, contract_last, preferred_element_type=jnp.float32
    ) + lax.dot_general(upper_imag, piece_real, contract_last, preferred_element_type=jnp.float32)
    upper_totals = jnp.stack([real_part, imag_part], 0)
    lower_solved = jnp.transpose(
        lower_totals.astype(jnp.bfloat16).reshape(2, block_count, rank_width, panel_count),
        (1, 0, 2, 3),
    )
    upper_solved = jnp.transpose(
        upper_totals.astype(jnp.bfloat16).reshape(2, block_count, rank_width, panel_count),
        (1, 0, 2, 3),
    )
    left_blocks = lower_solved[pair_lower[0]]
    right_blocks = upper_solved[pair_upper[0]]
    pair_count = left_blocks.shape[0]
    real_part = product(left_blocks[:, 0], right_blocks[:, 0]) - product(
        left_blocks[:, 1], right_blocks[:, 1]
    )
    imag_part = product(left_blocks[:, 0], right_blocks[:, 1]) + product(
        left_blocks[:, 1], right_blocks[:, 0]
    )
    cores = (
        jnp.stack([real_part, imag_part], 1)
        .reshape(pair_count, 2 * rank_width * rank_width)
        .astype(jnp.bfloat16)
    )
    owners = pair_owner[0, :, 0]
    pair_ids = lax.broadcasted_iota(jnp.int32, (pair_count,), 0)
    same_owner = (owners[:, None] == owners[None, :]) & (pair_ids[None, :] < pair_ids[:, None])
    slots = jnp.sum(same_owner.astype(jnp.int32), axis=1)
    clusters = lax.axis_size("clu")
    target_slot = owners * SEND_CAP + slots
    slot_ids = lax.broadcasted_iota(jnp.int32, (clusters * SEND_CAP, pair_count), 0)
    one_hot = (slot_ids == target_slot[None, :]).astype(jnp.bfloat16)
    buffer = jnp.dot(one_hot, cores, preferred_element_type=jnp.float32).astype(jnp.bfloat16)
    buffer = buffer.reshape(clusters, SEND_CAP, 2, rank_width * rank_width)
    arrived = lax.all_to_all(buffer, "clu", split_axis=0, concat_axis=0, tiled=True)
    return (lower_solved[None], upper_solved[None], arrived[None, None])


def solution(mesh):
    in_specs = (
        P("clu", None, "grp", None),
        P("clu", None, "grp", None),
        P("clu", "grp", None, None, None),
        P("clu", "grp", None, None, None),
        P("clu", "grp"),
        P("clu", "grp"),
        P("clu", None),
        P("clu", "grp"),
        P("clu", "grp"),
        P("clu", "grp", None),
    )
    out_specs = (
        P("clu", "grp", None, None, None),
        P("clu", "grp", None, None, None),
        P("clu", "grp", None, None, None, None),
    )
    return jax.shard_map(
        per_device, mesh=mesh, in_specs=in_specs, out_specs=out_specs, check_vma=False
    )
```

profile of v0, /device:TPU:1, one launch (start us, length us, event | category | flops | bytes accessed | tf_op | source)
XLA Modules:
  0.0 210.7 jit_solution(4374763556248300210)
XLA Ops:
  7.2 0.0 all-gather.5.cloned.1.call-start
  7.2 0.7 all-gather.5.cloned.1.call-update
  7.9 0.0 all-gather.3.cloned.1.call-start
  8.0 0.7 all-gather.3.cloned.1.call-update
  8.7 2.6 %copy.48 = bf16[1,8,2,48,512]{3,1,4,2,0:T(8,128)(2,1)S(1)} copy(bf16[1,8,2,48,512]{4,3,2,1,0:T(8,128)(2,1)} %param.13) | data formatting | bytes 1572864 | tf_op args[3]
  11.3 0.0 copy-start.11
  11.3 0.1 iota_compare_fusion.3
  11.4 2.5 %copy.43 = bf16[1,8,2,48,512]{3,1,4,2,0:T(8,128)(2,1)} copy(bf16[1,8,2,48,512]{4,3,2,1,0:T(8,128)(2,1)S(1)} %copy-done.8) | data formatting | bytes 1572864 | tf_op args[2]
  13.9 0.1 iota_compare_fusion.4
  14.0 1.4 bitcast_select_fusion
  15.4 3.0 %gather_fusion = bf16[512,8,2,48]{3,1,2,0:T(8,128)(2,1)S(1)} fusion(bf16[8,2,48,512]{2,0,3,1:T(8,128)(2,1)} %bitcast_select_fusion, s32[1024]{0:T(1024)S(1)} %pad_clamp_fusion.2), kind=kCustom, calls=%fused_computation | custom fusion | bytes 1574912 | tf_op jit(solution)/shard_map/jit(_take)/gather | solution.py:34
  18.4 1.8 select_bitcast_fusion
  20.2 0.1 bitcast_select_fusion.1
  20.3 1.1 fusion.26
  21.4 2.6 %copy.49 = bf16[8,1,48,512]{3,2,0,1:T(8,128)(2,1)} copy(bf16[8,1,48,512]{2,0,1,3:T(8,128)(2,1)} %get-tuple-element.4) | data formatting | bytes 786432 | tf_op jit(solution)/shard_map/slice | solution.py:40
  24.0 0.7 copy.50
  24.8 1.1 fusion.27
  25.9 2.7 %copy.44 = bf16[8,1,48,512]{3,2,0,1:T(8,128)(2,1)} copy(bf16[8,1,48,512]{2,0,3,1:T(8,128)(2,1)} %get-tuple-element.6) | data formatting | bytes 786432 | tf_op jit(solution)/shard_map/slice | solution.py:38
  28.5 0.7 copy.45
  29.3 0.0 copy-start.4
  29.4 0.2 convert_reduce_fusion
  29.5 42.9 %all-gather.5.cloned.1.call-done = bf16[1,2,512,512]{3,2,1,0:T(8,128)(2,1)} async-done(((bf16[1,2,32,512]{3,2,1,0:T(8,128)(2,1)}), bf16[1,2,512,512]{3,2,1,0:T(8,128)(2,1)}) %all-gather.5.cloned.1.call-update) | async-done | bytes 1048592 | tf_op jit(solution)/shard_map/all_gather | solution.py:43
  72.4 2.3 %fusion.21 = f32[384,512]{1,0:T(8,128)} fusion(bf16[384,512]{1,0:T(8,128)(2,1)S(1)} %bitcast.132, bf16[1,2,512,512]{3,2,1,0:T(8,128)(2,1)} %all-gather.5.cloned.1.call-done), kind=kOutput, calls=%fused_computation.43 | convolution fusion | flops 201326592 | bytes 1703936 | tf_op jit(solution)/shard_map/dot_general | solution.py:59
  74.7 1.4 fusion.20
  76.2 56.5 %all-gather.3.cloned.1.call-done = bf16[1,2,512,512]{3,2,1,0:T(8,128)(2,1)} async-done(((bf16[1,2,32,512]{3,2,1,0:T(8,128)(2,1)}), bf16[1,2,512,512]{3,2,1,0:T(8,128)(2,1)}) %all-gather.3.cloned.1.call-update) | async-done | bytes 1048592 | tf_op jit(solution)/shard_map/all_gather | solution.py:44
  132.7 1.5 fusion.19
  134.2 1.4 fusion.18
  135.6 0.4 fusion.9
  136.0 0.4 fusion.8
  136.5 0.4 copy-done.2
  136.9 0.4 fusion.7
  137.2 0.4 fusion.6
  137.6 1.3 fusion.15
  138.9 2.4 %gather_fusion.1 = bf16[32,2,48,512]{3,2,1,0:T(8,128)(2,1)} fusion(bf16[8,2,48,512]{3,2,1,0:T(8,128)(2,1)S(1)} %get-tuple-element.12, s32[1024]{0:T(1024)S(1)} %pad_clamp_fusion.1), kind=kCustom, calls=%fused_computation.1 | custom fusion | bytes 6291584 | tf_op jit(solution)/shard_map/gather | solution.py:71
  141.3 2.4 %gather_fusion.2 = bf16[32,2,48,512]{3,2,1,0:T(8,128)(2,1)} fusion(bf16[8,2,48,512]{3,2,1,0:T(8,128)(2,1)S(1)} %get-tuple-element.7, s32[1024]{0:T(1024)S(1)} %pad_clamp_fusion), kind=kCustom, calls=%fused_computation.2 | custom fusion | bytes 6291584 | tf_op jit(solution)/shard_map/gather | solution.py:72
  143.8 2.6 %fusion = f32[32,48,48]{2,1,0:T(8,128)S(1)} fusion(bf16[32,2,48,512]{3,2,1,0:T(8,128)(2,1)} %gather_fusion.1, bf16[32,2,48,512]{3,2,1,0:T(8,128)(2,1)} %gather_fusion.2), kind=kOutput, calls=%fused_computation.11 | convolution fusion | flops 75497472 | bytes 3440640 | tf_op jit(solution)/shard_map/prb,psb->prs/dot_general | solution.py:17
  146.3 0.3 copy-done.5
  146.6 2.1 fusion.1
  148.7 0.3 copy-done.6
  149.0 0.6 fusion.13
  149.5 0.5 fusion.12
  150.1 0.2 pad_maximum_fusion.2
  150.3 0.1 copy.57
  150.3 1.4 convert_element_type.16
  151.7 0.3 convolution_convert_fusion
  152.0 0.1 reshape.167
  152.2 50.9 %all_to_all.5 = bf16[32,2,2,2304]{3,2,1,0:T(2,128)(2,1)S(1)} all-to-all(bf16[32,2,2,2304]{3,2,1,0:T(2,128)(2,1)S(1)} %reshape.167), channel_id=1, replica_groups=mesh['grp'=16,'clu'=32] {'clu'}, dimensions={0} | all-to-all | bytes 1179648 | tf_op jit(solution)/shard_map/all_to_all | solution.py:95
  203.0 0.8 copy.63
  (33 shorter events, 0.1 us)
Async XLA Ops:
  7.2 4.1 %copy-start.10 = (s32[1,8]{1,0:T(1,128)S(1)}, s32[1,8]{1,0:T(1,128)}, u32[]{:S(2)}) copy-start(s32[1,8]{1,0:T(1,128)} %param.15) | copy-start | bytes 100
  7.2 4.2 %copy-start.9 = (s32[1,512]{1,0:T(1,128)S(1)}, s32[1,512]{1,0:T(1,128)}, u32[]{:S(2)}) copy-start(s32[1,512]{1,0:T(1,128)} %param.16) | copy-start | bytes 6148
  7.2 4.2 %copy-start.8 = (bf16[1,8,2,48,512]{4,3,2,1,0:T(8,128)(2,1)S(1)}, bf16[1,8,2,48,512]{4,3,2,1,0:T(8,128)(2,1)}, u32[]{:S(2)}) copy-start(bf16[1,8,2,48,512]{4,3,2,1,0:T(8,128)(2,1)} %param.12) | copy-start | bytes 2359300
  7.2 65.2 %all-gather.5.cloned.1.call-start = ((), (), s32[]{:S(2)}) async-start(), calls=%async_computation.2 | async-start | bytes 1114112 | tf_op jit(solution)/shard_map/all_gather | solution.py:43
  7.9 124.8 %all-gather.3.cloned.1.call-start = ((), (), s32[]{:S(2)}) async-start(), calls=%async_computation.1 | async-start | bytes 1114112 | tf_op jit(solution)/shard_map/all_gather | solution.py:44
  11.3 2.6 %copy-start.11 = (s32[1,8]{1,0:T(1,128)S(1)}, s32[1,8]{1,0:T(1,128)}, u32[]{:S(2)}) copy-start(s32[1,8]{1,0:T(1,128)} %param.14) | copy-start | bytes 100
  18.4 1.8 copy-start
  25.9 3.4 %copy-start.12 = (s32[1,32]{1,0:T(1,128)S(1)}, s32[1,32]{1,0:T(1,128)}, u32[]{:S(2)}) copy-start(s32[1,32]{1,0:T(1,128)} %param.17) | copy-start | bytes 388
  25.9 3.4 %copy-start.13 = (s32[1,32]{1,0:T(1,128)S(1)}, s32[1,32]{1,0:T(1,128)}, u32[]{:S(2)}) copy-start(s32[1,32]{1,0:T(1,128)} %param.18) | copy-start | bytes 388
  25.9 3.5 %copy-start.14 = (s32[1,32,1]{1,2,0:T(1,128)S(1)}, s32[1,32,1]{1,2,0:T(1,128)}, u32[]{:S(2)}) copy-start(s32[1,32,1]{1,2,0:T(1,128)} %param.19) | copy-start | bytes 388
  25.9 46.5 %copy-start.3 = (bf16[8,1,48,512]{3,2,0,1:T(8,128)(2,1)S(1)}, bf16[8,1,48,512]{3,2,0,1:T(8,128)(2,1)}, u32[]{:S(2)}) copy-start(bf16[8,1,48,512]{3,2,0,1:T(8,128)(2,1)} %copy.49) | copy-start | bytes 1179652
  29.3 103.4 %copy-start.4 = (bf16[8,1,48,512]{3,2,0,1:T(8,128)(2,1)S(1)}, bf16[8,1,48,512]{3,2,0,1:T(8,128)(2,1)}, u32[]{:S(2)}) copy-start(bf16[8,1,48,512]{3,2,0,1:T(8,128)(2,1)} %copy.44) | copy-start | bytes 1179652
  76.2 59.4 %copy-start.1 = (bf16[1,2,512,512]{3,2,1,0:T(8,128)(2,1)S(1)}, bf16[1,2,512,512]{3,2,1,0:T(8,128)(2,1)}, u32[]{:S(2)}) copy-start(bf16[1,2,512,512]{3,2,1,0:T(8,128)(2,1)} %all-gather.5.cloned.1.call-done) | copy-start | bytes 3145732
  132.7 2.9 %copy-start.7 = (f32[384,512]{1,0:T(8,128)S(1)}, f32[384,512]{1,0:T(8,128)}, u32[]{:S(2)}) copy-start(f32[384,512]{1,0:T(8,128)} %fusion.21) | copy-start | bytes 2359300
  135.6 1.2 copy-start.2
  143.8 2.8 %copy-start.5 = (bf16[32,2,48,512]{3,2,1,0:T(8,128)(2,1)S(1)}, bf16[32,2,48,512]{3,2,1,0:T(8,128)(2,1)}, u32[]{:S(2)}) copy-start(bf16[32,2,48,512]{3,2,1,0:T(8,128)(2,1)} %gather_fusion.1) | copy-start | bytes 9437188
  146.6 2.4 %copy-start.6 = (bf16[32,2,48,512]{3,2,1,0:T(8,128)(2,1)S(1)}, bf16[32,2,48,512]{3,2,1,0:T(8,128)(2,1)}, u32[]{:S(2)}) copy-start(bf16[32,2,48,512]{3,2,1,0:T(8,128)(2,1)} %gather_fusion.2) | copy-start | bytes 9437188
Sparse Core Ops, SparseCore 0:
  11.1 61.2 all-gather.4
  75.5 57.1 all-gather.2
where the time goes:
time: 211 us
  waiting for transfers between devices  101 us (48%)
  blocking collectives  50.9 us (24%)
  local copies, waits for them, and re-layouts  25.2 us (12%)
  between operations  14.4 us (7%)
  matrix products  14.2 us (7%)
  other arithmetic  5.23 us (2%)
    all_gather x1, waiting for transfers between devices, per_device(): upper_piece = lax.all_gather(upper_inverse, 'grp', axis=2, tiled=True)  56.5 us
    all_to_all x1, blocking collectives, per_device(): lax.all_to_all(buffer, 'clu', split_axis=0, concat_axis=0, tiled=True)  50.9 us
    all_gather x1, waiting for transfers between devices, per_device(): lower_piece = lax.all_gather(lower_inverse, 'grp', axis=2, tiled=True)  42.9 us
    unnamed x33, local copies, waits for them, and re-layouts  6.88 us
    dot_general x4, matrix products, product(): jnp.einsum('prb,psb->prs', left, right, preferred_element_type=jnp.float32)  5.78 us
  transfers between devices with their start and end apart: 2, of which 2 were waited for; matrix products, arithmetic and copies ran while one was open for 12% of the time, Pallas kernels for 0%

commit v1 on v0

--- a/solution.py
+++ b/solution.py
@@ -15,6 +15,25 @@
 
 def product(left, right):
     return jnp.einsum("prb,psb->prs", left, right, preferred_element_type=jnp.float32)
+
+
+def gather_inverses(lower_rows, upper_rows):
+    groups = lax.axis_size("grp")
+    rows = lower_rows.shape[1]
+    width = lower_rows.shape[2]
+    span = width + rows
+    start = lax.axis_index("grp") * rows
+    both = jnp.concatenate([upper_rows, lower_rows], axis=-1)
+    packed = lax.dynamic_slice_in_dim(both, start, span, axis=2)
+    copies = jnp.broadcast_to(packed[None], (groups,) + packed.shape)
+    blocks = lax.all_to_all(copies, "grp", split_axis=0, concat_axis=0, tiled=True)
+    upper_blocks, lower_blocks = [], []
+    for source in range(groups):
+        block = blocks[source]
+        cut = width - source * rows
+        upper_blocks.append(jnp.pad(block[..., :cut], ((0, 0), (0, 0), (source * rows, 0))))
+        lower_blocks.append(jnp.pad(block[..., cut:], ((0, 0), (0, 0), (0, cut - rows))))
+    return jnp.concatenate(lower_blocks, axis=1), jnp.concatenate(upper_blocks, axis=1)
 
 
 def per_device(
@@ -40,10 +59,9 @@
     upper_real = upper_pivoted[:, 0].reshape(block_count * rank_width, panel_count)
     upper_imag = upper_pivoted[:, 1].reshape(block_count * rank_width, panel_count)
     contract_last = (((1,), (1,)), ((), ()))
-    lower_piece = lax.all_gather(lower_inverse, "grp", axis=2, tiled=True)
-    upper_piece = lax.all_gather(upper_inverse, "grp", axis=2, tiled=True)
-    piece_real = upper_piece[0, 0]
-    piece_imag = upper_piece[0, 1]
+    lower_piece, upper_piece = gather_inverses(lower_inverse[0], upper_inverse[0])
+    piece_real = upper_piece[0]
+    piece_imag = upper_piece[1]
     real_part = jnp.dot(lower_real, piece_real, preferred_element_type=jnp.float32) - jnp.dot(
         lower_imag, piece_imag, preferred_element_type=jnp.float32
     )
@@ -51,8 +69,8 @@
         lower_imag, piece_real, preferred_element_type=jnp.float32
     )
     lower_totals = jnp.stack([real_part, imag_part], 0)
-    piece_real = lower_piece[0, 0]
-    piece_imag = lower_piece[0, 1]
+    piece_real = lower_piece[0]
+    piece_imag = lower_piece[1]
     real_part = lax.dot_general(
         upper_real, piece_real, contract_last, preferred_element_type=jnp.float32
     ) - lax.dot_general(upper_imag, piece_imag, contract_last, preferred_element_type=jnp.float32)

time: 211 us -> 106 us (0.50)
  waiting for transfers between devices: 101 us -> 0.01 us
  between operations: 14.4 us -> 1.31 us
  starting transfers between devices: 0.08 us -> 7.59 us
  matrix products: 14.2 us -> 9.12 us
  blocking collectives: 50.9 us -> 55.4 us
    all_gather x2 -> x0, waiting for transfers between devices: 99.4 us -> none  [the longest x1 56.5 us: per_device(): upper_piece = lax.all_gather(upper_inverse, 'grp', axis=2, tiled=True)]
    all_to_all x0 -> x1, starting transfers between devices: none -> 7.59 us  [gather_inverses(): lax.all_to_all(copies, 'grp', split_axis=0, concat_axis=0, tiled=True)]
    all_to_all x1, blocking collectives: 50.9 us -> 55.4 us  [per_device(): lax.all_to_all(buffer, 'clu', split_axis=0, concat_axis=0, tiled=True)]
    unnamed x33 -> x54, local copies, waits for them, and re-layouts: 6.88 us -> 7.83 us
  transfers between devices with their start and end apart: 2 -> 1, of which waited for: 2 -> 0; matrix products, arithmetic and copies ran while one was open for 12% -> 17% of each run, Pallas kernels for 0% -> 0%
where the time goes in v1:
time: 106 us
  blocking collectives  55.4 us (52%)
  local copies, waits for them, and re-layouts  25.1 us (24%)
  matrix products  9.12 us (9%)
  starting transfers between devices  7.59 us (7%)
  other arithmetic  7.03 us (7%)
  between operations  1.31 us (1%)
    all_to_all x1, blocking collectives, per_device(): lax.all_to_all(buffer, 'clu', split_axis=0, concat_axis=0, tiled=True)  55.4 us
    unnamed x54, local copies, waits for them, and re-layouts  7.83 us
    all_to_all x1, starting transfers between devices, gather_inverses(): lax.all_to_all(copies, 'grp', split_axis=0, concat_axis=0, tiled=True)  7.59 us
    dot_general x4, matrix products, product(): jnp.einsum('prb,psb->prs', left, right, preferred_element_type=jnp.float32)  5.77 us
    gather x1, local copies, waits for them, and re-layouts, per_device(): upper_pivoted = jnp.take(upper_masked, pivots[0], axis=3)  2.95 us
    gather x1, local copies, waits for them, and re-layouts, per_device(): right_blocks = upper_solved[pair_upper[0]]  2.43 us
    gather x1, local copies, waits for them, and re-layouts, per_device(): left_blocks = lower_solved[pair_lower[0]]  2.4 us
  transfers between devices with their start and end apart: 1, of which 0 were waited for; matrix products, arithmetic and copies ran while one was open for 17% of the time, Pallas kernels for 0%

profile of v1, /device:TPU:1, one launch (start us, length us, event | category | flops | bytes accessed | tf_op | source)
XLA Modules:
  0.0 105.5 jit_solution(6272850492318778729)
XLA Ops:
  0.6 1.0 fusion.22
  1.6 1.2 %broadcast_in_dim.52 = bf16[16,2,32,544]{3,2,1,0:T(8,128)(2,1)} broadcast(bf16[2,32,544]{2,1,0:T(8,128)(2,1)S(1)} %fusion.22), dimensions={1,2,3} | broadcast | bytes 1183744 | tf_op jit(solution)/shard_map/broadcast_in_dim | solution.py:28
  2.8 7.6 %all-to-all-start = ((bf16[16,2,32,544]{3,2,1,0:T(8,128)(2,1)}), bf16[16,2,32,544]{3,2,1,0:T(8,128)(2,1)S(1)}, u32[]{:S(2)}, u32[]{:S(2)}) async-start(bf16[16,2,32,544]{3,2,1,0:T(8,128)(2,1)} %broadcast_in_dim.52), calls=%async_computation | async-start | bytes 2621440 | tf_op jit(solution)/shard_map/all_to_all | solution.py:29
  10.4 2.6 %copy.43 = bf16[1,8,2,48,512]{3,1,4,2,0:T(8,128)(2,1)S(1)} copy(bf16[1,8,2,48,512]{4,3,2,1,0:T(8,128)(2,1)} %param.12) | data formatting | bytes 1572864 | tf_op args[2]
  13.1 0.1 bitcast_select_fusion.1
  13.3 0.1 fusion.28
  13.4 1.5 %copy.44 = bf16[8,1,48,512]{3,2,0,1:T(8,128)(2,1)} copy(bf16[8,1,48,512]{2,0,3,1:T(8,128)(2,1)S(1)} %get-tuple-element.6) | data formatting | bytes 786432 | tf_op jit(solution)/shard_map/slice | solution.py:57
  14.9 1.5 %copy.45 = bf16[8,1,48,512]{3,2,0,1:T(8,128)(2,1)} copy(bf16[8,1,48,512]{2,0,3,1:T(8,128)(2,1)S(1)} %get-tuple-element.5) | data formatting | bytes 786432 | tf_op jit(solution)/shard_map/slice | solution.py:58
  16.4 2.6 %copy.48 = bf16[1,8,2,48,512]{3,1,4,2,0:T(8,128)(2,1)S(1)} copy(bf16[1,8,2,48,512]{4,3,2,1,0:T(8,128)(2,1)} %param.13) | data formatting | bytes 1572864 | tf_op args[3]
  19.1 1.5 %bitcast_select_fusion = bf16[8,2,48,512]{2,0,3,1:T(8,128)(2,1)} fusion(bf16[1,8,2,48,512]{3,1,4,2,0:T(8,128)(2,1)S(1)} %copy.48, pred[8,48]{1,0:T(8,128)(4,1)S(1)} %iota_compare_fusion.3), kind=kLoop, calls=%fused_computation.4 | loop fusion | flops 393216 | bytes 1573248 | tf_op jit(solution)/shard_map/jit(_where)/select_n | solution.py:13
  20.6 3.0 %gather_fusion = bf16[512,8,2,48]{3,1,2,0:T(8,128)(2,1)S(1)} fusion(bf16[8,2,48,512]{2,0,3,1:T(8,128)(2,1)} %bitcast_select_fusion, s32[1024]{0:T(1024)S(1)} %pad_clamp_fusion.2), kind=kCustom, calls=%fused_computation | custom fusion | bytes 1574912 | tf_op jit(solution)/shard_map/jit(_take)/gather | solution.py:53
  23.5 1.9 %select_bitcast_fusion = bf16[8,2,48,512]{2,0,1,3:T(8,128)(2,1)S(1)} fusion(bf16[512,8,2,48]{3,1,2,0:T(8,128)(2,1)S(1)} %gather_fusion, pred[512]{0:T(512)(128)(4,1)S(1)} %compare_and_fusion), kind=kLoop, calls=%fused_computation.6 | loop fusion | flops 393216 | bytes 1573376 | tf_op jit(solution)/shard_map/jit(_take)/select_n | solution.py:53
  25.5 0.1 fusion.27
  25.6 1.5 %copy.49 = bf16[8,1,48,512]{3,2,0,1:T(8,128)(2,1)} copy(bf16[8,1,48,512]{2,0,1,3:T(8,128)(2,1)S(1)} %get-tuple-element.4) | data formatting | bytes 786432 | tf_op jit(solution)/shard_map/slice | solution.py:59
  27.1 0.7 copy.50
  27.9 0.2 convert_reduce_fusion
  28.1 0.1 slice_bitcast_fusion.48
  29.2 0.1 slice.300
  29.3 0.1 slice.301
  29.6 0.1 slice_dynamic-update-slice_fusion
  29.7 0.1 constant_dynamic-update-slice_fusion.14
  29.8 0.1 constant_dynamic-update-slice_fusion.13
  29.9 0.1 constant_dynamic-update-slice_fusion.12
  30.8 0.4 fusion.19
  31.2 0.4 fusion.18
  31.6 0.4 fusion.21
  32.0 0.4 fusion.20
  32.4 0.2 copy-done
  32.6 0.4 fusion.7
  32.9 0.4 fusion.6
  33.3 0.4 fusion.9
  33.7 0.4 fusion.8
  34.1 1.0 fusion.17
  35.1 1.0 fusion.15
  36.1 2.4 %gather_fusion.1 = bf16[32,2,48,512]{3,2,1,0:T(8,128)(2,1)} fusion(bf16[8,2,48,512]{3,2,1,0:T(8,128)(2,1)S(1)} %get-tuple-element.25, s32[1024]{0:T(1024)S(1)} %pad_clamp_fusion.1), kind=kCustom, calls=%fused_computation.1 | custom fusion | bytes 6291584 | tf_op jit(solution)/shard_map/gather | solution.py:89
  38.5 2.4 %gather_fusion.2 = bf16[32,2,48,512]{3,2,1,0:T(8,128)(2,1)} fusion(bf16[8,2,48,512]{3,2,1,0:T(8,128)(2,1)S(1)} %get-tuple-element.23, s32[1024]{0:T(1024)S(1)} %pad_clamp_fusion), kind=kCustom, calls=%fused_computation.2 | custom fusion | bytes 6291584 | tf_op jit(solution)/shard_map/gather | solution.py:90
  40.9 2.6 %fusion = f32[32,48,48]{2,1,0:T(8,128)S(1)} fusion(bf16[32,2,48,512]{3,2,1,0:T(8,128)(2,1)} %gather_fusion.1, bf16[32,2,48,512]{3,2,1,0:T(8,128)(2,1)} %gather_fusion.2), kind=kOutput, calls=%fused_computation.11 | convolution fusion | flops 75497472 | bytes 3440640 | tf_op jit(solution)/shard_map/prb,psb->prs/dot_general | solution.py:17
  43.5 0.3 copy-done.3
  43.8 2.1 %fusion.1 = f32[32,48,48]{2,1,0:T(8,128)S(1)} fusion(bf16[32,2,48,512]{3,2,1,0:T(8,128)(2,1)S(1)} %copy-done.3, bf16[32,2,48,512]{3,2,1,0:T(8,128)(2,1)} %gather_fusion.2), kind=kOutput, calls=%fused_computation.12 | convolution fusion | flops 75497472 | bytes 3440640 | tf_op jit(solution)/shard_map/prb,psb->prs/dot_general | solution.py:17
  45.9 0.3 copy-done.4
  46.1 0.5 fusion.13
  46.7 0.6 fusion.12
  47.2 0.2 pad_maximum_fusion.2
  47.5 1.4 %convert_element_type.76 = bf16[32,4608]{1,0:T(8,128)(2,1)S(1)} reshape(bf16[32,2,48,48]{3,2,1,0:T(8,128)(2,1)S(1)} %copy.57) | data formatting | bytes 589824 | tf_op jit(solution)/shard_map/convert_element_type | solution.py:101
  48.9 0.3 convolution_convert_fusion
  49.2 0.1 reshape.168
  49.3 55.4 %all_to_all.10 = bf16[32,2,2,2304]{3,2,1,0:T(2,128)(2,1)S(1)} all-to-all(bf16[32,2,2,2304]{3,2,1,0:T(2,128)(2,1)S(1)} %reshape.168), channel_id=1, replica_groups=mesh['grp'=16,'clu'=32] {'clu'}, dimensions={0} | all-to-all | bytes 1179648 | tf_op jit(solution)/shard_map/all_to_all | solution.py:113
  104.7 0.8 copy.93
  (85 shorter events, 2.0 us)
Async XLA Ops:
  2.8 25.2 %all-to-all-start = ((bf16[16,2,32,544]{3,2,1,0:T(8,128)(2,1)}), bf16[16,2,32,544]{3,2,1,0:T(8,128)(2,1)S(1)}, u32[]{:S(2)}, u32[]{:S(2)}) async-start(bf16[16,2,32,544]{3,2,1,0:T(8,128)(2,1)} %broadcast_in_dim.52), calls=%async_computation | async-start | bytes 2621440 | tf_op jit(solution)/shard_map/all_to_all | solution.py:29
  10.4 2.6 %copy-start.8 = (s32[1,8]{1,0:T(1,128)S(1)}, s32[1,8]{1,0:T(1,128)}, u32[]{:S(2)}) copy-start(s32[1,8]{1,0:T(1,128)} %param.14) | copy-start | bytes 100
  14.9 4.1 %copy-start.9 = (s32[1,8]{1,0:T(1,128)S(1)}, s32[1,8]{1,0:T(1,128)}, u32[]{:S(2)}) copy-start(s32[1,8]{1,0:T(1,128)} %param.15) | copy-start | bytes 100
  14.9 4.2 %copy-start.5 = (s32[1,512]{1,0:T(1,128)S(1)}, s32[1,512]{1,0:T(1,128)}, u32[]{:S(2)}) copy-start(s32[1,512]{1,0:T(1,128)} %param.16) | copy-start | bytes 6148
  25.6 2.2 %copy-start.6 = (s32[1,32]{1,0:T(1,128)S(1)}, s32[1,32]{1,0:T(1,128)}, u32[]{:S(2)}) copy-start(s32[1,32]{1,0:T(1,128)} %param.17) | copy-start | bytes 388
  25.6 2.2 %copy-start.7 = (s32[1,32]{1,0:T(1,128)S(1)}, s32[1,32]{1,0:T(1,128)}, u32[]{:S(2)}) copy-start(s32[1,32]{1,0:T(1,128)} %param.18) | copy-start | bytes 388
  25.6 2.3 %copy-start.10 = (s32[1,32,1]{1,2,0:T(1,128)S(1)}, s32[1,32,1]{1,2,0:T(1,128)}, u32[]{:S(2)}) copy-start(s32[1,32,1]{1,2,0:T(1,128)} %param.19) | copy-start | bytes 388
  29.0 1.8 %copy-start.1 = (bf16[8,1,48,512]{3,2,0,1:T(8,128)(2,1)S(1)}, bf16[8,1,48,512]{3,2,0,1:T(8,128)(2,1)}, u32[]{:S(2)}) copy-start(bf16[8,1,48,512]{3,2,0,1:T(8,128)(2,1)} %copy.44) | copy-start | bytes 1179652
  30.2 1.4 %copy-start.2 = (bf16[8,1,48,512]{3,2,0,1:T(8,128)(2,1)S(1)}, bf16[8,1,48,512]{3,2,0,1:T(8,128)(2,1)}, u32[]{:S(2)}) copy-start(bf16[8,1,48,512]{3,2,0,1:T(8,128)(2,1)} %copy.49) | copy-start | bytes 1179652
  31.6 1.0 copy-start
  40.9 2.8 %copy-start.3 = (bf16[32,2,48,512]{3,2,1,0:T(8,128)(2,1)S(1)}, bf16[32,2,48,512]{3,2,1,0:T(8,128)(2,1)}, u32[]{:S(2)}) copy-start(bf16[32,2,48,512]{3,2,1,0:T(8,128)(2,1)} %gather_fusion.1) | copy-start | bytes 9437188
  43.8 2.4 %copy-start.4 = (bf16[32,2,48,512]{3,2,1,0:T(8,128)(2,1)S(1)}, bf16[32,2,48,512]{3,2,1,0:T(8,128)(2,1)}, u32[]{:S(2)}) copy-start(bf16[32,2,48,512]{3,2,1,0:T(8,128)(2,1)} %gather_fusion.2) | copy-start | bytes 9437188

commit v2 on v1

v2 whole, which is shorter than its diff:
```python
import jax
import jax.numpy as jnp
from jax import lax
from jax.sharding import PartitionSpec as P

SEND_CAP = 2


def mask_rows(factors, block_ranks):
    rank_width = factors.shape[2]
    row_index = lax.broadcasted_iota(jnp.int32, (factors.shape[0], rank_width), 1)
    row_mask = row_index < block_ranks[:, None]
    return jnp.where(row_mask[:, None, :, None], factors, jnp.zeros((), factors.dtype))


def product(left, right):
    return jnp.einsum("prb,psb->prs", left, right, preferred_element_type=jnp.float32)


def gather_inverses(lower_rows, upper_rows):
    groups = lax.axis_size("grp")
    rows = lower_rows.shape[1]
    width = lower_rows.shape[2]
    span = width + rows
    start = lax.axis_index("grp") * rows
    both = jnp.concatenate([upper_rows, lower_rows], axis=-1)
    packed = lax.dynamic_slice_in_dim(both, start, span, axis=2)
    copies = jnp.broadcast_to(packed[None], (groups,) + packed.shape)
    blocks = lax.all_to_all(copies, "grp", split_axis=0, concat_axis=0, tiled=True)
    upper_blocks, lower_blocks = [], []
    for source in range(groups):
        block = blocks[source]
        cut = width - source * rows
        upper_blocks.append(jnp.pad(block[..., :cut], ((0, 0), (0, 0), (source * rows, 0))))
        lower_blocks.append(jnp.pad(block[..., cut:], ((0, 0), (0, 0), (0, cut - rows))))
    return jnp.concatenate(lower_blocks, axis=1), jnp.concatenate(upper_blocks, axis=1)


def solve_rows(rows, right, contract):
    block_count, _, rank_width, panel_count = rows.shape
    flat = rows.reshape(block_count * 2 * rank_width, panel_count)
    totals = lax.dot_general(flat, right, contract, preferred_element_type=jnp.float32)
    totals = totals.reshape(block_count, 2, rank_width, 2 * panel_count)
    real_part = totals[:, 0, :, :panel_count] - totals[:, 1, :, panel_count:]
    imag_part = totals[:, 0, :, panel_count:] + totals[:, 1, :, :panel_count]
    return jnp.stack([real_part, imag_part], 1).astype(jnp.bfloat16)


def per_device(
    lower_inverse,
    upper_inverse,
    lower_factors,
    upper_factors,
    lower_ranks,
    upper_ranks,
    pivots,
    pair_lower,
    pair_upper,
    pair_owner,
):
    lower_masked = mask_rows(lower_factors[0], lower_ranks[0])
    upper_masked = mask_rows(upper_factors[0], upper_ranks[0])
    block_count, _, rank_width, panel_count = lower_masked.shape
    panel_ids = lax.broadcasted_iota(jnp.int32, (panel_count, panel_count), 0)
    pivot_matrix = (panel_ids == pivots[0][None, :]).astype(jnp.bfloat16)
    upper_pivoted = jnp.dot(
        upper_masked.reshape(-1, panel_count), pivot_matrix, preferred_element_type=jnp.float32
    ).astype(jnp.bfloat16).reshape(upper_masked.shape)
    lower_piece, upper_piece = gather_inverses(lower_inverse[0], upper_inverse[0])
    contract_first = (((1,), (0,)), ((), ()))
    contract_last = (((1,), (1,)), ((), ()))
    upper_right = jnp.concatenate([upper_piece[0], upper_piece[1]], axis=1)
    lower_right = jnp.concatenate([lower_piece[0], lower_piece[1]], axis=0)
    lower_solved = solve_rows(lower_masked, upper_right, contract_first)
    upper_solved = solve_rows(upper_pivoted, lower_right, contract_last)
    side = block_count * 2 * rank_width
    grams = lax.dot_general(
        lower_solved.reshape(side, panel_count),
        upper_solved.reshape(side, panel_count),
        contract_last,
        preferred_element_type=jnp.float32,
    ).reshape(block_count, 2, rank_width, block_count, 2, rank_width)
    real_part = grams[:, 0, :, :, 0, :] - grams[:, 1, :, :, 1, :]
    imag_part = grams[:, 0, :, :, 1, :] + grams[:, 1, :, :, 0, :]
    all_cores = (
        jnp.transpose(jnp.stack([real_part, imag_part], 0), (1, 3, 0, 2, 4))
        .reshape(block_count * block_count, 2 * rank_width * rank_width)
        .astype(jnp.bfloat16)
    )
    owners = pair_owner[0, :, 0]
    pair_count = owners.shape[0]
    pair_ids = lax.broadcasted_iota(jnp.int32, (pair_count,), 0)
    same_owner = (owners[:, None] == owners[None, :]) & (pair_ids[None, :] < pair_ids[:, None])
    slots = jnp.sum(same_owner.astype(jnp.int32), axis=1)
    clusters = lax.axis_size("clu")
    target_slot = owners * SEND_CAP + slots
    slot_ids = lax.broadcasted_iota(jnp.int32, (clusters * SEND_CAP, pair_count), 0)
    one_hot = (slot_ids == target_slot[None, :]).astype(jnp.float32)
    pair_block = pair_lower[0] * block_count + pair_upper[0]
    block_ids = lax.broadcasted_iota(jnp.int32, (pair_count, block_count * block_count), 1)
    pick = (block_ids == pair_block[:, None]).astype(jnp.float32)
    chooser = jnp.dot(one_hot, pick, preferred_element_type=jnp.float32).astype(jnp.bfloat16)
    buffer = jnp.dot(chooser, all_cores, preferred_element_type=jnp.float32).astype(jnp.bfloat16)
    buffer = buffer.reshape(clusters, SEND_CAP, 2, rank_width * rank_width)
    arrived = lax.all_to_all(buffer, "clu", split_axis=0, concat_axis=0, tiled=True)
    return (lower_solved[None], upper_solved[None], arrived[None, None])


def solution(mesh):
    in_specs = (
        P("clu", None, "grp", None),
        P("clu", None, "grp", None),
        P("clu", "grp", None, None, None),
        P("clu", "grp", None, None, None),
        P("clu", "grp"),
        P("clu", "grp"),
        P("clu", None),
        P("clu", "grp"),
        P("clu", "grp"),
        P("clu", "grp", None),
    )
    out_specs = (
        P("clu", "grp", None, None, None),
        P("clu", "grp", None, None, None),
        P("clu", "grp", None, None, None, None),
    )
    return jax.shard_map(
        per_device, mesh=mesh, in_specs=in_specs, out_specs=out_specs, check_vma=False
    )
```

time: 106 us -> 114 us (1.075)
  blocking collectives: 55.4 us -> 0 us
  waiting for transfers between devices: 0.01 us -> 46.7 us
  starting transfers between devices: 7.59 us -> 28 us
  local copies, waits for them, and re-layouts: 25.1 us -> 22.8 us
    all_to_all x1 -> x0, blocking collectives: 55.4 us -> none  [per_device(): lax.all_to_all(buffer, 'clu', split_axis=0, concat_axis=0, tiled=True)]
    all_to_all x0 -> x1, waiting for transfers between devices: none -> 33.1 us  [per_device(): lax.all_to_all(buffer, 'clu', split_axis=0, concat_axis=0, tiled=True)]
    all_to_all x0 -> x1, starting transfers between devices: none -> 20.2 us  [per_device(): lax.all_to_all(buffer, 'clu', split_axis=0, concat_axis=0, tiled=True)]
    all_to_all x1, waiting for transfers between devices: 0.01 us -> 13.6 us  [gather_inverses(): lax.all_to_all(copies, 'grp', split_axis=0, concat_axis=0, tiled=True)]
    gather x3 -> x0, local copies, waits for them, and re-layouts: 7.78 us -> none  [the longest x1 2.95 us: per_device(): upper_pivoted = jnp.take(upper_masked, pivots[0], axis=3)]
    slice x6 -> x0, local copies, waits for them, and re-layouts: 5.38 us -> none  [the longest x2 1.6 us: per_device(): lower_masked[:, 1].reshape(block_count * rank_width, panel_count)]
    convert_element_type x1 -> x2, local copies, waits for them, and re-layouts: 1.39 us -> 5.87 us  [per_device(): all_cores = jnp.transpose(jnp.stack([real_part, imag_part], 0), (1, 3, 0,...]
    slice x15, local copies, waits for them, and re-layouts: 0.07 us -> 4.27 us  [gather_inverses(): block[..., :cut]]
  transfers between devices with their start and end apart: 1 -> 2, of which waited for: 0 -> 2; matrix products, arithmetic and copies ran while one was open for 17% -> 6% of each run, Pallas kernels for 0% -> 0%
where the time goes in v2:
time: 114 us; the launch traced here: 113 us
  waiting for transfers between devices  46.7 us (41%)
  starting transfers between devices  28 us (25%)
  local copies, waits for them, and re-layouts  22.8 us (20%)
  matrix products  8.08 us (7%)
  other arithmetic  6.63 us (6%)
  between operations  1.17 us (1%)
    all_to_all x1, waiting for transfers between devices, per_device(): lax.all_to_all(buffer, 'clu', split_axis=0, concat_axis=0, tiled=True)  33.1 us
    all_to_all x1, starting transfers between devices, per_device(): lax.all_to_all(buffer, 'clu', split_axis=0, concat_axis=0, tiled=True)  20.2 us
    all_to_all x1, waiting for transfers between devices, gather_inverses(): lax.all_to_all(copies, 'grp', split_axis=0, concat_axis=0, tiled=True)  13.6 us
    all_to_all x1, starting transfers between devices, gather_inverses(): lax.all_to_all(copies, 'grp', split_axis=0, concat_axis=0, tiled=True)  7.73 us
    unnamed x71, local copies, waits for them, and re-layouts  7.11 us
    convert_element_type x2, local copies, waits for them, and re-layouts, per_device(): all_cores = jnp.transpose(jnp.stack([real_part, imag_part], 0), (1, 3, 0,...  5.87 us
    slice x15, local copies, waits for them, and re-layouts, gather_inverses(): block[..., :cut]  4.27 us
    dot_general x2, matrix products, solve_rows(): lax.dot_general(flat, right, contract, preferred_element_type=jnp.float32)  3.93 us
  transfers between devices with their start and end apart: 2, of which 2 were waited for; matrix products, arithmetic and copies ran while one was open for 6% of the time, Pallas kernels for 0%

profile of v2, /device:TPU:1, one launch (start us, length us, event | category | flops | bytes accessed | tf_op | source)
XLA Modules:
  0.0 113.3 jit_solution(416232189247537709)
XLA Ops:
  0.6 1.0 fusion.26
  1.6 1.2 %broadcast_in_dim.43 = bf16[16,2,32,544]{3,2,1,0:T(8,128)(2,1)} broadcast(bf16[2,32,544]{2,1,0:T(8,128)(2,1)S(1)} %fusion.26), dimensions={1,2,3} | broadcast | bytes 1183744 | tf_op jit(solution)/shard_map/broadcast_in_dim | solution.py:28
  2.9 7.7 %all-to-all-start = ((bf16[16,2,32,544]{3,2,1,0:T(8,128)(2,1)}), bf16[16,2,32,544]{3,2,1,0:T(8,128)(2,1)S(1)}, u32[]{:S(2)}, u32[]{:S(2)}) async-start(bf16[16,2,32,544]{3,2,1,0:T(8,128)(2,1)} %broadcast_in_dim.43), calls=%async_computation | async-start | bytes 2621440 | tf_op jit(solution)/shard_map/all_to_all | solution.py:29
  10.7 0.1 broadcast_in_dim.45
  10.8 0.2 convert_reduce_fusion
  11.0 0.7 iota_compare_fusion.11
  11.7 0.5 multiply_add_fusion
  12.2 0.6 add_bitcast_fusion
  12.8 1.1 bitcast_select_fusion
  13.8 13.6 %all-to-all-done = bf16[16,2,32,544]{3,2,1,0:T(8,128)(2,1)S(1)} async-done(((bf16[16,2,32,544]{3,2,1,0:T(8,128)(2,1)}), bf16[16,2,32,544]{3,2,1,0:T(8,128)(2,1)S(1)}, u32[]{:S(2)}, u32[]{:S(2)}) %all-to-all-start) | async-done | bytes 1114144 | tf_op jit(solution)/shard_map/all_to_all | solution.py:29
  27.4 0.1 slice_bitcast_fusion.8
  28.1 0.6 slice.273
  28.8 0.6 slice.275
  29.5 0.6 slice.277
  30.2 0.6 slice.279
  30.8 0.1 slice.307
  30.9 0.6 slice.283
  31.5 0.1 slice.308
  31.6 0.6 slice.285
  32.2 0.6 slice.287
  33.1 0.6 constant_dynamic-update-slice_fusion.15
  33.7 1.0 slice_bitcast_fusion.5
  34.7 2.9 %fusion.3 = f32[768,1024]{1,0:T(8,128)S(1)} fusion(bf16[768,512]{1,0:T(8,128)(2,1)} %bitcast_select_fusion, bf16[512,512]{1,0:T(8,128)(2,1)} %get-tuple-element.31, bf16[512,512]{1,0:T(8,128)(2,1)} %get-tuple-element.30, s32[512]{0:T(512)} %bitcast.129), kind=kOutput, calls=%fused_computation.9 | convolution fusion | flops 1210712064 | bytes 4982784 | tf_op jit(solution)/shard_map/dot_general | solution.py:42
  37.6 0.1 fusion.12
  37.8 0.1 fusion.38
  37.9 0.9 copy-done.1
  38.9 0.1 constant_dynamic-update-slice_fusion.14
  38.9 0.1 constant_dynamic-update-slice_fusion.13
  39.0 0.1 constant_dynamic-update-slice_fusion.12
  40.1 0.2 copy-done.12
  40.3 1.0 fusion.4
  41.3 0.3 fusion.16
  41.6 1.8 %fusion.17 = f32[8,2,48,8,2,48]{5,2,4,3,1,0:T(8,128)S(1)} fusion(bf16[8,1,48,512]{3,2,1,0:T(8,128)(2,1)S(1)} %get-tuple-element.13, bf16[8,1,48,512]{3,2,1,0:T(8,128)(2,1)S(1)} %get-tuple-element.12, bf16[8,1,48,512]{3,2,1,0:T(8,128)(2,1)S(1)} %fusion.12, bf16[8,1,48,512]{3,2,1,0:T(8,128)(2,1)S(1)} %fusion.38), kind=kOutput, calls=%fused_computation.34 | convolution fusion | flops 607125504 | bytes 3932160 | tf_op jit(solution)/shard_map/dot_general | solution.py:77
  43.4 0.2 fusion.11
  43.6 0.2 fusion.10
  43.8 0.4 maximum_bitcast_fusion
  44.2 1.3 %copy.33 = bf16[8,8,2,48,48]{4,3,2,1,0:T(8,128)(2,1)} copy(bf16[8,8,2,48,48]{4,3,1,0,2:T(8,128)(2,1)S(1)} %maximum_bitcast_fusion) | data formatting | bytes 1179648 | tf_op jit(solution)/shard_map/convert_element_type | solution.py:88
  45.5 4.6 %convert_element_type.106 = bf16[64,4608]{1,0:T(8,128)(2,1)} reshape(bf16[8,8,2,48,48]{4,3,2,1,0:T(8,128)(2,1)} %copy.33) | data formatting | bytes 1179648 | tf_op jit(solution)/shard_map/convert_element_type | solution.py:88
  50.1 2.3 %convolution_convert_fusion = bf16[64,4608]{1,0:T(8,128)(2,1)} fusion(bf16[64,4608]{1,0:T(8,128)(2,1)} %convert_element_type.106, s32[32]{0:T(128)S(1)} %copy-done.10, s32[32]{0:T(128)S(1)} %copy-done.11), kind=kOutput, calls=%fused_computation | convolution fusion | flops 38313984 | bytes 1179904 | tf_op jit(solution)/shard_map/dot_general | solution.py:103
  52.4 2.0 %reshape.202 = bf16[32,2,2,2304]{3,2,1,0:T(2,128)(2,1)} reshape(bf16[64,4608]{1,0:T(8,128)(2,1)} %convolution_convert_fusion) | data formatting | bytes 1179648 | tf_op jit(solution)/shard_map/reshape | solution.py:104
  54.4 20.2 %all-to-all-start.1 = ((bf16[32,2,2,2304]{3,2,1,0:T(2,128)(2,1)}), bf16[32,2,2,2304]{3,2,1,0:T(2,128)(2,1)}, u32[]{:S(2)}, u32[]{:S(2)}) async-start(bf16[32,2,2,2304]{3,2,1,0:T(2,128)(2,1)} %reshape.202), calls=%async_computation.1 | async-start | bytes 1179648 | tf_op jit(solution)/shard_map/all_to_all | solution.py:105
  74.7 1.1 pad_maximum_fusion
  75.8 0.9 copy.34
  76.7 0.1 fusion.40
  76.8 0.1 fusion.39
  77.0 0.9 copy.35
  78.0 33.1 %all-to-all-done.1 = bf16[32,2,2,2304]{3,2,1,0:T(2,128)(2,1)} async-done(((bf16[32,2,2,2304]{3,2,1,0:T(2,128)(2,1)}), bf16[32,2,2,2304]{3,2,1,0:T(2,128)(2,1)}, u32[]{:S(2)}, u32[]{:S(2)}) %all-to-all-start.1) | async-done | bytes 589856 | tf_op jit(solution)/shard_map/all_to_all | solution.py:105
  111.0 2.3 %copy.74 = bf16[1,1,32,2,2,2304]{5,4,3,2,1,0:T(2,128)(2,1)} copy(bf16[1,1,32,2,2,2304]{5,4,3,2,1,0:T(2,128)(2,1)} %bitcast.44) | data formatting | bytes 1179648
  (88 shorter events, 2.0 us)
Async XLA Ops:
  2.8 7.8 %copy-start.13 = (s32[1,8]{1,0:T(1,128)S(1)}, s32[1,8]{1,0:T(1,128)}, u32[]{:S(2)}) copy-start(s32[1,8]{1,0:T(1,128)} %param.15) | copy-start | bytes 100
  2.8 8.0 %copy-start.15 = (s32[1,32,1]{1,2,0:T(1,128)S(1)}, s32[1,32,1]{1,2,0:T(1,128)}, u32[]{:S(2)}) copy-start(s32[1,32,1]{1,2,0:T(1,128)} %param.19) | copy-start | bytes 388
  2.8 8.1 %copy-start.14 = (s32[1,8]{1,0:T(1,128)S(1)}, s32[1,8]{1,0:T(1,128)}, u32[]{:S(2)}) copy-start(s32[1,8]{1,0:T(1,128)} %param.14) | copy-start | bytes 100
  2.8 9.4 %copy-start.16 = (s32[1,32]{1,0:T(1,128)S(1)}, s32[1,32]{1,0:T(1,128)}, u32[]{:S(2)}) copy-start(s32[1,32]{1,0:T(1,128)} %param.18) | copy-start | bytes 388
  2.9 9.4 %copy-start.17 = (s32[1,32]{1,0:T(1,128)S(1)}, s32[1,32]{1,0:T(1,128)}, u32[]{:S(2)}) copy-start(s32[1,32]{1,0:T(1,128)} %param.17) | copy-start | bytes 388
  2.9 9.9 %copy-start.2 = (bf16[1,8,2,48,512]{4,3,2,1,0:T(8,128)(2,1)S(1)}, bf16[1,8,2,48,512]{4,3,2,1,0:T(8,128)(2,1)}, u32[]{:S(2)}) copy-start(bf16[1,8,2,48,512]{4,3,2,1,0:T(8,128)(2,1)} %param.13) | copy-start | bytes 2359300
  2.9 24.5 %all-to-all-start = ((bf16[16,2,32,544]{3,2,1,0:T(8,128)(2,1)}), bf16[16,2,32,544]{3,2,1,0:T(8,128)(2,1)S(1)}, u32[]{:S(2)}, u32[]{:S(2)}) async-start(bf16[16,2,32,544]{3,2,1,0:T(8,128)(2,1)} %broadcast_in_dim.43), calls=%async_computation | async-start | bytes 2621440 | tf_op jit(solution)/shard_map/all_to_all | solution.py:29
  37.6 1.2 %copy-start.1 = (bf16[2,512,512]{2,1,0:T(8,128)(2,1)S(1)}, bf16[2,512,512]{2,1,0:T(8,128)(2,1)}, u32[]{:S(2)}) copy-start(bf16[2,512,512]{2,1,0:T(8,128)(2,1)} %get-tuple-element.34) | copy-start | bytes 3145732
  37.8 1.7 %copy-start.3 = (bf16[2,32,256]{2,1,0:T(8,128)(2,1)S(1)}, bf16[2,32,256]{2,1,0:T(8,128)(2,1)}, u32[]{:S(2)}) copy-start(bf16[2,32,256]{2,1,0:T(8,128)(2,1)} %slice.273) | copy-start | bytes 98308
  37.8 1.7 %copy-start.4 = (bf16[2,32,224]{2,1,0:T(8,128)(2,1)S(1)}, bf16[2,32,224]{2,1,0:T(8,128)(2,1)}, u32[]{:S(2)}) copy-start(bf16[2,32,224]{2,1,0:T(8,128)(2,1)} %slice.275) | copy-start | bytes 86020
  37.8 1.8 %copy-start.5 = (bf16[2,32,192]{2,1,0:T(8,128)(2,1)S(1)}, bf16[2,32,192]{2,1,0:T(8,128)(2,1)}, u32[]{:S(2)}) copy-start(bf16[2,32,192]{2,1,0:T(8,128)(2,1)} %slice.277) | copy-start | bytes 73732
  37.8 1.9 %copy-start.6 = (bf16[2,32,160]{2,1,0:T(8,128)(2,1)S(1)}, bf16[2,32,160]{2,1,0:T(8,128)(2,1)}, u32[]{:S(2)}) copy-start(bf16[2,32,160]{2,1,0:T(8,128)(2,1)} %slice.279) | copy-start | bytes 61444
  37.8 1.9 %copy-start.7 = (bf16[2,32,96]{2,1,0:T(8,128)(2,1)S(1)}, bf16[2,32,96]{2,1,0:T(8,128)(2,1)}, u32[]{:S(2)}) copy-start(bf16[2,32,96]{2,1,0:T(8,128)(2,1)} %slice.283) | copy-start | bytes 36868
  37.8 2.0 %copy-start.8 = (bf16[2,32,64]{2,1,0:T(8,128)(2,1)S(1)}, bf16[2,32,64]{2,1,0:T(8,128)(2,1)}, u32[]{:S(2)}) copy-start(bf16[2,32,64]{2,1,0:T(8,128)(2,1)} %slice.285) | copy-start | bytes 24580
  37.8 2.1 %copy-start.9 = (bf16[2,32,32]{2,1,0:T(8,128)(2,1)S(1)}, bf16[2,32,32]{2,1,0:T(8,128)(2,1)}, u32[]{:S(2)}) copy-start(bf16[2,32,32]{2,1,0:T(8,128)(2,1)} %slice.287) | copy-start | bytes 12292
  39.2 1.1 %copy-start.12 = (bf16[1,8,2,48,512]{4,3,2,1,0:T(8,128)(2,1)S(1)}, bf16[1,8,2,48,512]{4,3,2,1,0:T(8,128)(2,1)}, u32[]{:S(2)}) copy-start(bf16[1,8,2,48,512]{4,3,2,1,0:T(8,128)(2,1)} %param.12) | copy-start | bytes 2359300
  39.2 1.1 copy-start.18
  41.6 1.8 %copy-start = (bf16[8,1,48,512]{3,2,1,0:T(8,128)(2,1)}, bf16[8,1,48,512]{3,2,1,0:T(8,128)(2,1)S(1)}, u32[]{:S(2)}) copy-start(bf16[8,1,48,512]{3,2,1,0:T(8,128)(2,1)S(1)} %get-tuple-element.13) | copy-start | bytes 1179652
  45.5 4.6 %copy-start.10 = (s32[32]{0:T(128)S(1)}, s32[32]{0:T(128)}, u32[]{:S(2)}) copy-start(s32[32]{0:T(128)} %multiply_add_fusion) | copy-start | bytes 388
  45.5 4.6 %copy-start.11 = (s32[32]{0:T(128)S(1)}, s32[32]{0:T(128)}, u32[]{:S(2)}) copy-start(s32[32]{0:T(128)} %add_bitcast_fusion) | copy-start | bytes 388
  54.4 56.6 %all-to-all-start.1 = ((bf16[32,2,2,2304]{3,2,1,0:T(2,128)(2,1)}), bf16[32,2,2,2304]{3,2,1,0:T(2,128)(2,1)}, u32[]{:S(2)}, u32[]{:S(2)}) async-start(bf16[32,2,2,2304]{3,2,1,0:T(2,128)(2,1)} %reshape.202), calls=%async_computation.1 | async-start | bytes 1179648 | tf_op jit(solution)/shard_map/all_to_all | solution.py:105

commit v3 on v1

--- a/solution.py
+++ b/solution.py
@@ -78,28 +78,27 @@
         upper_real, piece_imag, contract_last, preferred_element_type=jnp.float32
     ) + lax.dot_general(upper_imag, piece_real, contract_last, preferred_element_type=jnp.float32)
     upper_totals = jnp.stack([real_part, imag_part], 0)
+    lower_totals = lower_totals.astype(jnp.bfloat16)
+    upper_totals = upper_totals.astype(jnp.bfloat16)
     lower_solved = jnp.transpose(
-        lower_totals.astype(jnp.bfloat16).reshape(2, block_count, rank_width, panel_count),
-        (1, 0, 2, 3),
+        lower_totals.reshape(2, block_count, rank_width, panel_count), (1, 0, 2, 3)
     )
     upper_solved = jnp.transpose(
-        upper_totals.astype(jnp.bfloat16).reshape(2, block_count, rank_width, panel_count),
-        (1, 0, 2, 3),
+        upper_totals.reshape(2, block_count, rank_width, panel_count), (1, 0, 2, 3)
     )
-    left_blocks = lower_solved[pair_lower[0]]
-    right_blocks = upper_solved[pair_upper[0]]
-    pair_count = left_blocks.shape[0]
-    real_part = product(left_blocks[:, 0], right_blocks[:, 0]) - product(
-        left_blocks[:, 1], right_blocks[:, 1]
+    real_part = lax.dot_general(
+        lower_totals[0], upper_totals[0], contract_last, preferred_element_type=jnp.float32
+    ) - lax.dot_general(lower_totals[1], upper_totals[1], contract_last, preferred_element_type=jnp.float32)
+    imag_part = lax.dot_general(
+        lower_totals[0], upper_totals[1], contract_last, preferred_element_type=jnp.float32
+    ) + lax.dot_general(lower_totals[1], upper_totals[0], contract_last, preferred_element_type=jnp.float32)
+    grid = jnp.stack([real_part, imag_part], 0).reshape(2, block_count, rank_width, block_count, rank_width)
+    grid = jnp.transpose(grid, (1, 3, 0, 2, 4)).reshape(
+        block_count * block_count, 2, rank_width, rank_width
     )
-    imag_part = product(left_blocks[:, 0], right_blocks[:, 1]) + product(
-        left_blocks[:, 1], right_blocks[:, 0]
-    )
-    cores = (
-        jnp.stack([real_part, imag_part], 1)
-        .reshape(pair_count, 2 * rank_width * rank_width)
-        .astype(jnp.bfloat16)
-    )
+    pair_count = pair_lower.shape[1]
+    picked = jnp.take(grid, pair_lower[0] * block_count + pair_upper[0], axis=0)
+    cores = picked.reshape(pair_count, 2 * rank_width * rank_width).astype(jnp.bfloat16)
     owners = pair_owner[0, :, 0]
     pair_ids = lax.broadcasted_iota(jnp.int32, (pair_count,), 0)
     same_owner = (owners[:, None] == owners[None, :]) & (pair_ids[None, :] < pair_ids[:, None])

time: 106 us -> 102 us (0.962)
  blocking collectives: 55.4 us -> 0 us
  waiting for transfers between devices: 0.01 us -> 34.4 us
  starting transfers between devices: 7.59 us -> 27 us
  matrix products: 9.12 us -> 4.96 us
  local copies, waits for them, and re-layouts: 25.1 us -> 26.6 us
    all_to_all x1 -> x0, blocking collectives: 55.4 us -> none  [per_device(): lax.all_to_all(buffer, 'clu', split_axis=0, concat_axis=0, tiled=True)]
    all_to_all x0 -> x1, waiting for transfers between devices: none -> 34.4 us  [per_device(): lax.all_to_all(buffer, 'clu', split_axis=0, concat_axis=0, tiled=True)]
    all_to_all x0 -> x1, starting transfers between devices: none -> 19.4 us  [per_device(): lax.all_to_all(buffer, 'clu', split_axis=0, concat_axis=0, tiled=True)]
    dot_general x4, matrix products: 5.77 us -> 1.54 us  [the longest x1 0.39 us: per_device(): lax.dot_general(lower_totals[1], upper_totals[1], contract_last, preferre...]
    another operation x1 -> x4, local copies, waits for them, and re-layouts: 0.05 us -> 2.43 us  [per_device(): jnp.stack([real_part, imag_part], 0)]
    transpose x2 -> x0, other arithmetic: 1.96 us -> none  [the longest x1 0.98 us: per_device(): jnp.transpose(lower_totals.astype(jnp.bfloat16).reshape(2, block_count, r...]
    broadcast_in_dim x0 -> x2, other arithmetic: none -> 1.91 us  [per_device(): return (lower_solved[None], upper_solved[None], arrived[None, None])]
    convert_element_type x1 -> x0, local copies, waits for them, and re-layouts: 1.39 us -> none  [per_device(): cores = jnp.stack([real_part, imag_part], 1).reshape(pair_count, 2 * rank...]
  transfers between devices with their start and end apart: 1 -> 2, of which waited for: 0 -> 1; matrix products, arithmetic and copies ran while one was open for 17% -> 19% of each run, Pallas kernels for 0% -> 0%
where the time goes in v3:
time: 102 us; the launch traced here: 101 us
  waiting for transfers between devices  34.4 us (34%)
  starting transfers between devices  27 us (26%)
  local copies, waits for them, and re-layouts  26.6 us (26%)
  other arithmetic  7.09 us (7%)
  matrix products  4.96 us (5%)
  between operations  1.31 us (1%)
    all_to_all x1, waiting for transfers between devices, per_device(): lax.all_to_all(buffer, 'clu', split_axis=0, concat_axis=0, tiled=True)  34.4 us
    all_to_all x1, starting transfers between devices, per_device(): lax.all_to_all(buffer, 'clu', split_axis=0, concat_axis=0, tiled=True)  19.4 us
    unnamed x52, local copies, waits for them, and re-layouts  8.3 us
    all_to_all x1, starting transfers between devices, gather_inverses(): lax.all_to_all(copies, 'grp', split_axis=0, concat_axis=0, tiled=True)  7.59 us
    gather x2, local copies, waits for them, and re-layouts, per_device(): picked = jnp.take(grid, pair_lower[0] * block_count + pair_upper[0], axis=0)  4.03 us
    gather x1, local copies, waits for them, and re-layouts, per_device(): upper_pivoted = jnp.take(upper_masked, pivots[0], axis=3)  2.95 us
    another operation x4, local copies, waits for them, and re-layouts, per_device(): jnp.stack([real_part, imag_part], 0)  2.43 us
  transfers between devices with their start and end apart: 2, of which 1 were waited for; matrix products, arithmetic and copies ran while one was open for 19% of the time, Pallas kernels for 0%

profile of v3, /device:TPU:1, one launch (start us, length us, event | category | flops | bytes accessed | tf_op | source)
XLA Modules:
  0.0 101.3 jit_solution(15034870039677209141)
XLA Ops:
  0.6 1.0 fusion.10
  1.6 1.2 %broadcast_in_dim.60 = bf16[16,2,32,544]{3,2,1,0:T(8,128)(2,1)} broadcast(bf16[2,32,544]{2,1,0:T(8,128)(2,1)S(1)} %fusion.10), dimensions={1,2,3} | broadcast | bytes 1183744 | tf_op jit(solution)/shard_map/broadcast_in_dim | solution.py:28
  2.8 7.6 %all-to-all-start = ((bf16[16,2,32,544]{3,2,1,0:T(8,128)(2,1)}), bf16[16,2,32,544]{3,2,1,0:T(8,128)(2,1)S(1)}, u32[]{:S(2)}, u32[]{:S(2)}) async-start(bf16[16,2,32,544]{3,2,1,0:T(8,128)(2,1)} %broadcast_in_dim.60), calls=%async_computation | async-start | bytes 2621440 | tf_op jit(solution)/shard_map/all_to_all | solution.py:29
  10.4 2.6 %copy.37 = bf16[1,8,2,48,512]{3,1,4,2,0:T(8,128)(2,1)S(1)} copy(bf16[1,8,2,48,512]{4,3,2,1,0:T(8,128)(2,1)} %param.12) | data formatting | bytes 1572864 | tf_op args[2]
  13.1 0.1 bitcast_select_fusion.1
  13.3 0.1 fusion.16
  13.4 1.5 %copy.38 = bf16[8,1,48,512]{3,2,0,1:T(8,128)(2,1)} copy(bf16[8,1,48,512]{2,0,3,1:T(8,128)(2,1)S(1)} %get-tuple-element.6) | data formatting | bytes 786432 | tf_op jit(solution)/shard_map/slice | solution.py:57
  14.9 1.5 %copy.39 = bf16[8,1,48,512]{3,2,0,1:T(8,128)(2,1)} copy(bf16[8,1,48,512]{2,0,3,1:T(8,128)(2,1)S(1)} %get-tuple-element.5) | data formatting | bytes 786432 | tf_op jit(solution)/shard_map/slice | solution.py:58
  16.4 2.6 %copy.42 = bf16[1,8,2,48,512]{3,1,4,2,0:T(8,128)(2,1)S(1)} copy(bf16[1,8,2,48,512]{4,3,2,1,0:T(8,128)(2,1)} %param.13) | data formatting | bytes 1572864 | tf_op args[3]
  19.1 1.5 %bitcast_select_fusion = bf16[8,2,48,512]{2,0,3,1:T(8,128)(2,1)} fusion(bf16[1,8,2,48,512]{3,1,4,2,0:T(8,128)(2,1)S(1)} %copy.42, pred[8,48]{1,0:T(8,128)(4,1)S(1)} %iota_compare_fusion.3), kind=kLoop, calls=%fused_computation.4 | loop fusion | flops 393216 | bytes 1573248 | tf_op jit(solution)/shard_map/jit(_where)/select_n | solution.py:13
  20.6 3.0 %gather_fusion = bf16[512,8,2,48]{3,1,2,0:T(8,128)(2,1)S(1)} fusion(bf16[8,2,48,512]{2,0,3,1:T(8,128)(2,1)} %bitcast_select_fusion, s32[1024]{0:T(1024)S(1)} %get-tuple-element.26), kind=kCustom, calls=%fused_computation | custom fusion | bytes 1574912 | tf_op jit(solution)/shard_map/jit(_take)/gather | solution.py:53
  23.5 1.9 %select_bitcast_fusion = bf16[8,2,48,512]{2,0,1,3:T(8,128)(2,1)S(1)} fusion(bf16[512,8,2,48]{3,1,2,0:T(8,128)(2,1)S(1)} %gather_fusion, pred[512]{0:T(512)(128)(4,1)S(1)} %compare_and_fusion.1), kind=kLoop, calls=%fused_computation.6 | loop fusion | flops 393216 | bytes 1573376 | tf_op jit(solution)/shard_map/jit(_take)/select_n | solution.py:53
  25.5 0.1 fusion.15
  25.6 1.5 %copy.43 = bf16[8,1,48,512]{3,2,0,1:T(8,128)(2,1)} copy(bf16[8,1,48,512]{2,0,1,3:T(8,128)(2,1)S(1)} %get-tuple-element.4) | data formatting | bytes 786432 | tf_op jit(solution)/shard_map/slice | solution.py:59
  27.1 0.7 copy.44
  27.8 0.2 convert_reduce_fusion
  28.1 0.1 slice_bitcast_fusion.12
  29.7 0.1 constant_dynamic-update-slice_fusion.14
  29.8 0.1 constant_dynamic-update-slice_fusion.13
  29.9 0.1 constant_dynamic-update-slice_fusion.12
  30.8 0.4 fusion.5
  31.2 0.4 fusion.4
  31.6 0.4 fusion.7
  32.0 0.4 fusion.6
  32.4 0.2 copy-done
  32.5 0.4 fusion.1
  32.9 0.4 fusion
  33.3 0.4 fusion.3
  33.7 0.4 fusion.2
  34.1 0.4 fusion.18
  34.5 0.4 fusion.17
  34.9 0.4 convolution_add_fusion.2
  35.3 0.7 stack.40
  35.9 1.0 copy.48
  36.9 0.4 convolution_subtract_fusion.2
  37.3 0.7 stack.39
  38.0 0.1 copy.47
  38.1 1.0 copy-done.3
  39.1 0.3 pad_maximum_fusion
  39.4 1.5 %gather_fusion.1 = bf16[32,2,48,48]{3,2,1,0:T(8,128)(2,1)} fusion(bf16[64,2,48,48]{3,2,1,0:T(8,128)(2,1)S(1)} %bitcast.124, s32[1024]{0:T(1024)S(1)} %get-tuple-element.25), kind=kCustom, calls=%fused_computation.1 | custom fusion | bytes 589952 | tf_op jit(solution)/shard_map/jit(_take)/gather | solution.py:100
  41.0 2.5 %gather.12 = bf16[32,4608]{1,0:T(8,128)(2,1)S(1)} reshape(bf16[32,2,48,48]{3,2,1,0:T(8,128)(2,1)} %gather_fusion.1) | data formatting | bytes 589824 | tf_op jit(solution)/shard_map/jit(_take)/gather | solution.py:100
  43.5 0.4 convolution_convert_fusion
  43.8 0.9 reshape.168
  44.8 19.4 %all-to-all-start.1 = ((bf16[32,2,2,2304]{3,2,1,0:T(2,128)(2,1)}), bf16[32,2,2,2304]{3,2,1,0:T(2,128)(2,1)S(1)}, u32[]{:S(2)}, u32[]{:S(2)}) async-start(bf16[32,2,2,2304]{3,2,1,0:T(2,128)(2,1)} %reshape.168), calls=%async_computation.1 | async-start | bytes 1179648 | tf_op jit(solution)/shard_map/all_to_all | solution.py:112
  64.2 1.0 maximum_bitcast_fusion
  65.1 1.0 maximum_bitcast_fusion.1
  66.1 34.4 %all-to-all-done.1 = bf16[32,2,2,2304]{3,2,1,0:T(2,128)(2,1)S(1)} async-done(((bf16[32,2,2,2304]{3,2,1,0:T(2,128)(2,1)}), bf16[32,2,2,2304]{3,2,1,0:T(2,128)(2,1)S(1)}, u32[]{:S(2)}, u32[]{:S(2)}) %all-to-all-start.1) | async-done | bytes 589856 | tf_op jit(solution)/shard_map/all_to_all | solution.py:112
  100.5 0.8 copy.80
  (85 shorter events, 2.2 us)
Async XLA Ops:
  2.8 25.2 %all-to-all-start = ((bf16[16,2,32,544]{3,2,1,0:T(8,128)(2,1)}), bf16[16,2,32,544]{3,2,1,0:T(8,128)(2,1)S(1)}, u32[]{:S(2)}, u32[]{:S(2)}) async-start(bf16[16,2,32,544]{3,2,1,0:T(8,128)(2,1)} %broadcast_in_dim.60), calls=%async_computation | async-start | bytes 2621440 | tf_op jit(solution)/shard_map/all_to_all | solution.py:29
  10.4 2.6 %copy-start.5 = (s32[1,8]{1,0:T(1,128)S(1)}, s32[1,8]{1,0:T(1,128)}, u32[]{:S(2)}) copy-start(s32[1,8]{1,0:T(1,128)} %param.14) | copy-start | bytes 100
  14.9 4.1 %copy-start.6 = (s32[1,8]{1,0:T(1,128)S(1)}, s32[1,8]{1,0:T(1,128)}, u32[]{:S(2)}) copy-start(s32[1,8]{1,0:T(1,128)} %param.15) | copy-start | bytes 100
  14.9 4.2 %copy-start.4 = (s32[1,512]{1,0:T(1,128)S(1)}, s32[1,512]{1,0:T(1,128)}, u32[]{:S(2)}) copy-start(s32[1,512]{1,0:T(1,128)} %param.16) | copy-start | bytes 6148
  19.1 1.5 %copy-start.7 = (s32[1,32]{1,0:T(1,128)S(1)}, s32[1,32]{1,0:T(1,128)}, u32[]{:S(2)}) copy-start(s32[1,32]{1,0:T(1,128)} %param.18) | copy-start | bytes 388
  19.1 1.5 %copy-start.8 = (s32[1,32]{1,0:T(1,128)S(1)}, s32[1,32]{1,0:T(1,128)}, u32[]{:S(2)}) copy-start(s32[1,32]{1,0:T(1,128)} %param.17) | copy-start | bytes 388
  25.6 2.2 %copy-start.9 = (s32[1,32,1]{1,2,0:T(1,128)S(1)}, s32[1,32,1]{1,2,0:T(1,128)}, u32[]{:S(2)}) copy-start(s32[1,32,1]{1,2,0:T(1,128)} %param.19) | copy-start | bytes 388
  29.0 1.8 %copy-start.1 = (bf16[8,1,48,512]{3,2,0,1:T(8,128)(2,1)S(1)}, bf16[8,1,48,512]{3,2,0,1:T(8,128)(2,1)}, u32[]{:S(2)}) copy-start(bf16[8,1,48,512]{3,2,0,1:T(8,128)(2,1)} %copy.38) | copy-start | bytes 1179652
  30.2 1.4 %copy-start.2 = (bf16[8,1,48,512]{3,2,0,1:T(8,128)(2,1)S(1)}, bf16[8,1,48,512]{3,2,0,1:T(8,128)(2,1)}, u32[]{:S(2)}) copy-start(bf16[8,1,48,512]{3,2,0,1:T(8,128)(2,1)} %copy.43) | copy-start | bytes 1179652
  31.5 1.0 copy-start
  38.0 1.1 %copy-start.3 = (bf16[1,8,48,8,48]{4,2,0,3,1:T(8,128)(2,1)S(1)}, bf16[1,8,48,8,48]{4,2,0,3,1:T(8,128)(2,1)}, u32[]{:S(2)}) copy-start(bf16[1,8,48,8,48]{4,2,0,3,1:T(8,128)(2,1)} %copy.48) | copy-start | bytes 884740
  44.8 55.7 %all-to-all-start.1 = ((bf16[32,2,2,2304]{3,2,1,0:T(2,128)(2,1)}), bf16[32,2,2,2304]{3,2,1,0:T(2,128)(2,1)S(1)}, u32[]{:S(2)}, u32[]{:S(2)}) async-start(bf16[32,2,2,2304]{3,2,1,0:T(2,128)(2,1)} %reshape.168), calls=%async_computation.1 | async-start | bytes 1179648 | tf_op jit(solution)/shard_map/all_to_all | solution.py:112

commit v4 on v3

--- a/solution.py
+++ b/solution.py
@@ -18,15 +18,19 @@
 
 
 def gather_inverses(lower_rows, upper_rows):
-    groups = lax.axis_size("grp")
+    groups = lax.axis_size("x") * lax.axis_size("y")
     rows = lower_rows.shape[1]
     width = lower_rows.shape[2]
     span = width + rows
-    start = lax.axis_index("grp") * rows
+    start = (lax.axis_index("x") * lax.axis_size("y") + lax.axis_index("y")) * rows
     both = jnp.concatenate([upper_rows, lower_rows], axis=-1)
     packed = lax.dynamic_slice_in_dim(both, start, span, axis=2)
-    copies = jnp.broadcast_to(packed[None], (groups,) + packed.shape)
-    blocks = lax.all_to_all(copies, "grp", split_axis=0, concat_axis=0, tiled=True)
+    near = lax.axis_size("y")
+    copies = jnp.broadcast_to(packed[None], (near,) + packed.shape)
+    blocks = lax.all_to_all(copies, "y", split_axis=0, concat_axis=0, tiled=True)
+    copies = jnp.broadcast_to(blocks[None], (groups // near,) + blocks.shape)
+    blocks = lax.all_to_all(copies, "x", split_axis=0, concat_axis=0, tiled=True)
+    blocks = blocks.reshape((groups,) + packed.shape)
     upper_blocks, lower_blocks = [], []
     for source in range(groups):
         block = blocks[source]
@@ -114,23 +118,29 @@
 
 
 def solution(mesh):
+    grp_size = mesh.shape["grp"]
+    near = 4 if grp_size % 4 == 0 else 1
+    split_mesh = jax.sharding.Mesh(
+        mesh.devices.reshape(grp_size // near, near, mesh.shape["clu"]), ("x", "y", "clu")
+    )
+    grp = ("x", "y")
     in_specs = (
-        P("clu", None, "grp", None),
-        P("clu", None, "grp", None),
-        P("clu", "grp", None, None, None),
-        P("clu", "grp", None, None, None),
-        P("clu", "grp"),
-        P("clu", "grp"),
+        P("clu", None, grp, None),
+        P("clu", None, grp, None),
+        P("clu", grp, None, None, None),
+        P("clu", grp, None, None, None),
+        P("clu", grp),
+        P("clu", grp),
         P("clu", None),
-        P("clu", "grp"),
-        P("clu", "grp"),
-        P("clu", "grp", None),
+        P("clu", grp),
+        P("clu", grp),
+        P("clu", grp, None),
     )
     out_specs = (
-        P("clu", "grp", None, None, None),
-        P("clu", "grp", None, None, None),
-        P("clu", "grp", None, None, None, None),
+        P("clu", grp, None, None, None),
+        P("clu", grp, None, None, None),
+        P("clu", grp, None, None, None, None),
     )
     return jax.shard_map(
-        per_device, mesh=mesh, in_specs=in_specs, out_specs=out_specs, check_vma=False
+        per_device, mesh=split_mesh, in_specs=in_specs, out_specs=out_specs, check_vma=False
     )

time: 102 us -> 118 us (1.16)
  waiting for transfers between devices: 34.4 us -> 42.3 us
  starting transfers between devices: 27 us -> 30.8 us
  local copies, waits for them, and re-layouts: 26.6 us -> 30.3 us
    all_to_all x1 -> x2, waiting for transfers between devices: 0.01 us -> 7.95 us  [the longest x1 7.95 us: gather_inverses(): lax.all_to_all(copies, 'x', split_axis=0, concat_axis=0, tiled=True)]
    all_to_all x1, starting transfers between devices: 19.4 us -> 21.8 us  [per_device(): lax.all_to_all(buffer, 'clu', split_axis=0, concat_axis=0, tiled=True)]
    broadcast_in_dim x1 -> x2, local copies, waits for them, and re-layouts: 1.23 us -> 2.98 us  [the longest x1 2.23 us: gather_inverses(): copies = jnp.broadcast_to(blocks[None], (groups // near,) + blocks.shape)]
    all_to_all x1 -> x2, starting transfers between devices: 7.59 us -> 9.03 us  [the longest x1 5 us: gather_inverses(): lax.all_to_all(copies, 'y', split_axis=0, concat_axis=0, tiled=True)]
    slice x2, local copies, waits for them, and re-layouts: 0.85 us -> 2.16 us  [per_device(): upper_pivoted[:, 1].reshape(block_count * rank_width, panel_count)]
    gather x1, local copies, waits for them, and re-layouts: 2.95 us -> 4.14 us  [per_device(): upper_pivoted = jnp.take(upper_masked, pivots[0], axis=3)]
    unnamed x52 -> x54, local copies, waits for them, and re-layouts: 8.3 us -> 7.37 us
  transfers between devices with their start and end apart: 2 -> 3, of which waited for: 1 -> 2; matrix products, arithmetic and copies ran while one was open for 19% -> 19% of each run, Pallas kernels for 0% -> 0%
where the time goes in v4:
time: 118 us
  waiting for transfers between devices  42.3 us (36%)
  starting transfers between devices  30.8 us (26%)
  local copies, waits for them, and re-layouts  30.3 us (26%)
  other arithmetic  8.04 us (7%)
  matrix products  4.95 us (4%)
  between operations  1.3 us (1%)
    all_to_all x1, waiting for transfers between devices, per_device(): lax.all_to_all(buffer, 'clu', split_axis=0, concat_axis=0, tiled=True)  34.4 us
    all_to_all x1, starting transfers between devices, per_device(): lax.all_to_all(buffer, 'clu', split_axis=0, concat_axis=0, tiled=True)  21.8 us
    all_to_all x1, waiting for transfers between devices, gather_inverses(): lax.all_to_all(copies, 'x', split_axis=0, concat_axis=0, tiled=True)  7.95 us
    unnamed x54, local copies, waits for them, and re-layouts  7.37 us
    all_to_all x1, starting transfers between devices, gather_inverses(): lax.all_to_all(copies, 'y', split_axis=0, concat_axis=0, tiled=True)  5 us
    gather x1, local copies, waits for them, and re-layouts, per_device(): upper_pivoted = jnp.take(upper_masked, pivots[0], axis=3)  4.14 us
    all_to_all x1, starting transfers between devices, gather_inverses(): lax.all_to_all(copies, 'x', split_axis=0, concat_axis=0, tiled=True)  4.03 us
    gather x2, local copies, waits for them, and re-layouts, per_device(): picked = jnp.take(grid, pair_lower[0] * block_count + pair_upper[0], axis=0)  4.03 us
  transfers between devices with their start and end apart: 3, of which 2 were waited for; matrix products, arithmetic and copies ran while one was open for 19% of the time, Pallas kernels for 0%

profile of v4, /device:TPU:1, one launch (start us, length us, event | category | flops | bytes accessed | tf_op | source)
XLA Modules:
  0.0 117.8 jit_solution(15288866740340715628)
XLA Ops:
  0.6 1.0 fusion.10
  1.6 0.8 broadcast_in_dim.66
  2.4 5.0 %all-to-all-start = ((bf16[4,2,32,544]{3,2,1,0:T(8,128)(2,1)}), bf16[4,2,32,544]{3,2,1,0:T(8,128)(2,1)}, u32[]{:S(2)}, u32[]{:S(2)}) async-start(bf16[4,2,32,544]{3,2,1,0:T(8,128)(2,1)} %broadcast_in_dim.66), calls=%async_computation | async-start | bytes 655360 | tf_op jit(solution)/shard_map/all_to_all | solution.py:30
  7.4 2.6 %copy.37 = bf16[1,8,2,48,512]{3,1,4,2,0:T(8,128)(2,1)S(1)} copy(bf16[1,8,2,48,512]{4,3,2,1,0:T(8,128)(2,1)} %param.12) | data formatting | bytes 1572864 | tf_op args[2]
  10.1 0.1 bitcast_select_fusion.1
  10.2 0.1 fusion.16
  10.4 1.5 %copy.38 = bf16[8,1,48,512]{3,2,0,1:T(8,128)(2,1)} copy(bf16[8,1,48,512]{2,0,3,1:T(8,128)(2,1)S(1)} %get-tuple-element.6) | data formatting | bytes 786432 | tf_op jit(solution)/shard_map/slice | solution.py:61
  11.8 1.5 %copy.39 = bf16[8,1,48,512]{3,2,0,1:T(8,128)(2,1)} copy(bf16[8,1,48,512]{2,0,3,1:T(8,128)(2,1)S(1)} %get-tuple-element.5) | data formatting | bytes 786432 | tf_op jit(solution)/shard_map/slice | solution.py:62
  13.3 1.7 %copy.42 = bf16[1,8,2,48,512]{3,1,4,2,0:T(8,128)(2,1)S(1)} copy(bf16[1,8,2,48,512]{4,3,2,1,0:T(8,128)(2,1)S(1)} %copy-done.4) | data formatting | bytes 1572864 | tf_op args[3]
  15.1 1.5 %bitcast_select_fusion = bf16[8,2,48,512]{2,0,3,1:T(8,128)(2,1)} fusion(bf16[1,8,2,48,512]{3,1,4,2,0:T(8,128)(2,1)S(1)} %copy.42, pred[8,48]{1,0:T(8,128)(4,1)S(1)} %iota_compare_fusion.3), kind=kLoop, calls=%fused_computation.4 | loop fusion | flops 393216 | bytes 1573248 | tf_op jit(solution)/shard_map/jit(_where)/select_n | solution.py:13
  16.6 4.1 %gather_fusion = bf16[512,8,2,48]{3,1,2,0:T(8,128)(2,1)} fusion(bf16[8,2,48,512]{2,0,3,1:T(8,128)(2,1)} %bitcast_select_fusion, s32[1024]{0:T(1024)S(1)} %get-tuple-element.26), kind=kCustom, calls=%fused_computation | custom fusion | bytes 1574912 | tf_op jit(solution)/shard_map/jit(_take)/gather | solution.py:57
  20.7 2.9 %select_bitcast_fusion = bf16[8,2,48,512]{2,0,1,3:T(8,128)(2,1)S(1)} fusion(bf16[512,8,2,48]{3,1,2,0:T(8,128)(2,1)} %gather_fusion, pred[512]{0:T(512)(128)(4,1)S(1)} %compare_and_fusion.1), kind=kLoop, calls=%fused_computation.6 | loop fusion | flops 393216 | bytes 1573376 | tf_op jit(solution)/shard_map/jit(_take)/select_n | solution.py:57
  23.6 2.2 %broadcast_in_dim.67 = bf16[4,4,2,32,544]{4,3,2,1,0:T(8,128)(2,1)} broadcast(bf16[4,2,32,544]{3,2,1,0:T(8,128)(2,1)} %all-to-all-done), dimensions={1,2,3,4} | broadcast | bytes 1392640 | tf_op jit(solution)/shard_map/broadcast_in_dim | solution.py:31
  25.9 4.0 %all-to-all-start.1 = ((bf16[4,4,2,32,544]{4,3,2,1,0:T(8,128)(2,1)}), bf16[4,4,2,32,544]{4,3,2,1,0:T(8,128)(2,1)S(1)}, u32[]{:S(2)}, u32[]{:S(2)}) async-start(bf16[4,4,2,32,544]{4,3,2,1,0:T(8,128)(2,1)} %broadcast_in_dim.67), calls=%async_computation.1 | async-start | bytes 2621440 | tf_op jit(solution)/shard_map/all_to_all | solution.py:32
  29.9 1.4 %fusion.15 = (bf16[8,1,48,512]{2,0,1,3:T(8,128)(2,1)}, bf16[8,1,48,512]{2,0,1,3:T(8,128)(2,1)}) fusion(bf16[8,2,48,512]{2,0,1,3:T(8,128)(2,1)S(1)} %select_bitcast_fusion), kind=kLoop, calls=%fused_computation.100 | loop fusion | bytes 1572864 | tf_op jit(solution)/shard_map/slice | solution.py:64
  31.3 1.9 %copy.43 = bf16[8,1,48,512]{3,2,0,1:T(8,128)(2,1)S(1)} copy(bf16[8,1,48,512]{2,0,1,3:T(8,128)(2,1)} %get-tuple-element.4) | data formatting | bytes 786432 | tf_op jit(solution)/shard_map/slice | solution.py:63
  33.3 0.7 copy.44
  34.0 0.2 convert_reduce_fusion
  34.2 7.9 %all-to-all-done.1 = bf16[4,4,2,32,544]{4,3,2,1,0:T(8,128)(2,1)S(1)} async-done(((bf16[4,4,2,32,544]{4,3,2,1,0:T(8,128)(2,1)}), bf16[4,4,2,32,544]{4,3,2,1,0:T(8,128)(2,1)S(1)}, u32[]{:S(2)}, u32[]{:S(2)}) %all-to-all-start.1) | async-done | bytes 1114144 | tf_op jit(solution)/shard_map/all_to_all | solution.py:32
  42.2 0.1 slice_bitcast_fusion.12
  44.9 0.4 fusion.5
  45.3 0.4 fusion.4
  45.6 0.4 fusion.7
  46.0 0.4 fusion.6
  46.4 0.2 copy-done.1
  46.6 0.4 fusion.1
  47.0 0.4 fusion
  47.4 0.4 fusion.3
  47.8 0.4 fusion.2
  48.2 0.4 fusion.18
  48.6 0.4 fusion.17
  49.0 0.4 convolution_add_fusion.2
  49.4 0.7 stack.40
  50.0 1.0 copy.48
  51.0 0.4 convolution_subtract_fusion.2
  51.4 0.7 stack.39
  52.1 0.1 copy.47
  52.2 1.0 copy-done.3
  53.2 0.3 pad_maximum_fusion
  53.5 1.5 %gather_fusion.1 = bf16[32,2,48,48]{3,2,1,0:T(8,128)(2,1)} fusion(bf16[64,2,48,48]{3,2,1,0:T(8,128)(2,1)S(1)} %bitcast.126, s32[1024]{0:T(1024)S(1)} %get-tuple-element.25), kind=kCustom, calls=%fused_computation.1 | custom fusion | bytes 589952 | tf_op jit(solution)/shard_map/jit(_take)/gather | solution.py:104
  55.1 2.5 %gather.12 = bf16[32,4608]{1,0:T(8,128)(2,1)S(1)} reshape(bf16[32,2,48,48]{3,2,1,0:T(8,128)(2,1)} %gather_fusion.1) | data formatting | bytes 589824 | tf_op jit(solution)/shard_map/jit(_take)/gather | solution.py:104
  57.6 0.4 convolution_convert_fusion
  57.9 0.9 reshape.173
  58.9 21.8 %all-to-all-start.2 = ((bf16[32,2,2,2304]{3,2,1,0:T(2,128)(2,1)}), bf16[32,2,2,2304]{3,2,1,0:T(2,128)(2,1)S(1)}, u32[]{:S(2)}, u32[]{:S(2)}) async-start(bf16[32,2,2,2304]{3,2,1,0:T(2,128)(2,1)} %reshape.173), calls=%async_computation.2 | async-start | bytes 1179648 | tf_op jit(solution)/shard_map/all_to_all | solution.py:116
  80.7 1.0 maximum_bitcast_fusion
  81.7 1.0 maximum_bitcast_fusion.1
  82.6 34.4 %all-to-all-done.2 = bf16[32,2,2,2304]{3,2,1,0:T(2,128)(2,1)S(1)} async-done(((bf16[32,2,2,2304]{3,2,1,0:T(2,128)(2,1)}), bf16[32,2,2,2304]{3,2,1,0:T(2,128)(2,1)S(1)}, u32[]{:S(2)}, u32[]{:S(2)}) %all-to-all-start.2) | async-done | bytes 589856 | tf_op jit(solution)/shard_map/all_to_all | solution.py:116
  117.0 0.8 copy.80
  (90 shorter events, 2.5 us)
Async XLA Ops:
  0.6 9.3 %copy-start.6 = (s32[1,8]{1,0:T(1,128)S(1)}, s32[1,8]{1,0:T(1,128)}, u32[]{:S(2)}) copy-start(s32[1,8]{1,0:T(1,128)} %param.14) | copy-start | bytes 100
  2.4 21.3 %all-to-all-start = ((bf16[4,2,32,544]{3,2,1,0:T(8,128)(2,1)}), bf16[4,2,32,544]{3,2,1,0:T(8,128)(2,1)}, u32[]{:S(2)}, u32[]{:S(2)}) async-start(bf16[4,2,32,544]{3,2,1,0:T(8,128)(2,1)} %broadcast_in_dim.66), calls=%async_computation | async-start | bytes 655360 | tf_op jit(solution)/shard_map/all_to_all | solution.py:30
  10.3 3.0 %copy-start.4 = (bf16[1,8,2,48,512]{4,3,2,1,0:T(8,128)(2,1)S(1)}, bf16[1,8,2,48,512]{4,3,2,1,0:T(8,128)(2,1)}, u32[]{:S(2)}) copy-start(bf16[1,8,2,48,512]{4,3,2,1,0:T(8,128)(2,1)} %param.13) | copy-start | bytes 2359300
  11.8 3.1 %copy-start.7 = (s32[1,8]{1,0:T(1,128)S(1)}, s32[1,8]{1,0:T(1,128)}, u32[]{:S(2)}) copy-start(s32[1,8]{1,0:T(1,128)} %param.15) | copy-start | bytes 100
  11.8 3.2 %copy-start.5 = (s32[1,512]{1,0:T(1,128)S(1)}, s32[1,512]{1,0:T(1,128)}, u32[]{:S(2)}) copy-start(s32[1,512]{1,0:T(1,128)} %param.16) | copy-start | bytes 6148
  15.1 1.5 %copy-start.8 = (s32[1,32]{1,0:T(1,128)S(1)}, s32[1,32]{1,0:T(1,128)}, u32[]{:S(2)}) copy-start(s32[1,32]{1,0:T(1,128)} %param.18) | copy-start | bytes 388
  15.1 1.5 %copy-start.9 = (s32[1,32]{1,0:T(1,128)S(1)}, s32[1,32]{1,0:T(1,128)}, u32[]{:S(2)}) copy-start(s32[1,32]{1,0:T(1,128)} %param.17) | copy-start | bytes 388
  25.9 16.3 %all-to-all-start.1 = ((bf16[4,4,2,32,544]{4,3,2,1,0:T(8,128)(2,1)}), bf16[4,4,2,32,544]{4,3,2,1,0:T(8,128)(2,1)S(1)}, u32[]{:S(2)}, u32[]{:S(2)}) async-start(bf16[4,4,2,32,544]{4,3,2,1,0:T(8,128)(2,1)} %broadcast_in_dim.67), calls=%async_computation.1 | async-start | bytes 2621440 | tf_op jit(solution)/shard_map/all_to_all | solution.py:32
  31.3 1.9 %copy-start = (bf16[8,1,48,512]{2,0,1,3:T(8,128)(2,1)S(1)}, bf16[8,1,48,512]{2,0,1,3:T(8,128)(2,1)}, u32[]{:S(2)}) copy-start(bf16[8,1,48,512]{2,0,1,3:T(8,128)(2,1)} %get-tuple-element.3) | copy-start | bytes 1179652
  31.3 2.7 %copy-start.10 = (s32[1,32,1]{1,2,0:T(1,128)S(1)}, s32[1,32,1]{1,2,0:T(1,128)}, u32[]{:S(2)}) copy-start(s32[1,32,1]{1,2,0:T(1,128)} %param.19) | copy-start | bytes 388
  43.1 1.8 %copy-start.2 = (bf16[8,1,48,512]{3,2,0,1:T(8,128)(2,1)S(1)}, bf16[8,1,48,512]{3,2,0,1:T(8,128)(2,1)}, u32[]{:S(2)}) copy-start(bf16[8,1,48,512]{3,2,0,1:T(8,128)(2,1)} %copy.38) | copy-start | bytes 1179652
  45.6 1.0 copy-start.1
  52.1 1.1 copy-start.3
  58.9 58.1 %all-to-all-start.2 = ((bf16[32,2,2,2304]{3,2,1,0:T(2,128)(2,1)}), bf16[32,2,2,2304]{3,2,1,0:T(2,128)(2,1)S(1)}, u32[]{:S(2)}, u32[]{:S(2)}) async-start(bf16[32,2,2,2304]{3,2,1,0:T(2,128)(2,1)} %reshape.173), calls=%async_computation.2 | async-start | bytes 1179648 | tf_op jit(solution)/shard_map/all_to_all | solution.py:116

commit v5 on v3

--- a/solution.py
+++ b/solution.py
@@ -92,12 +92,12 @@
     imag_part = lax.dot_general(
         lower_totals[0], upper_totals[1], contract_last, preferred_element_type=jnp.float32
     ) + lax.dot_general(lower_totals[1], upper_totals[0], contract_last, preferred_element_type=jnp.float32)
-    grid = jnp.stack([real_part, imag_part], 0).reshape(2, block_count, rank_width, block_count, rank_width)
-    grid = jnp.transpose(grid, (1, 3, 0, 2, 4)).reshape(
-        block_count * block_count, 2, rank_width, rank_width
-    )
     pair_count = pair_lower.shape[1]
-    picked = jnp.take(grid, pair_lower[0] * block_count + pair_upper[0], axis=0)
+    picked = [
+        part.reshape(block_count, rank_width, block_count, rank_width)[pair_lower[0], :, pair_upper[0], :]
+        for part in (real_part, imag_part)
+    ]
+    picked = jnp.stack(picked, 1)
     cores = picked.reshape(pair_count, 2 * rank_width * rank_width).astype(jnp.bfloat16)
     owners = pair_owner[0, :, 0]
     pair_ids = lax.broadcasted_iota(jnp.int32, (pair_count,), 0)

time: 102 us -> 103 us (level)
  local copies, waits for them, and re-layouts: 26.6 us -> 27.7 us
    reshape x0 -> x4, local copies, waits for them, and re-layouts: none -> 4.67 us  [per_device(): part.reshape(block_count, rank_width, block_count, rank_width)]
    another operation x4 -> x1, local copies, waits for them, and re-layouts: 2.43 us -> 0.05 us  [per_device(): picked = jnp.stack(picked, 1)]
    gather x2, local copies, waits for them, and re-layouts: 4.03 us -> 2.46 us  [per_device(): part.reshape(block_count, rank_width, block_count, rank_width)]
    convert_element_type x0 -> x1, local copies, waits for them, and re-layouts: none -> 1.39 us  [per_device(): picked.reshape(pair_count, 2 * rank_width * rank_width).astype(jnp.bfloat16)]
where the time goes in v5:
time: 103 us
  waiting for transfers between devices  34.4 us (33%)
  local copies, waits for them, and re-layouts  27.7 us (27%)
  starting transfers between devices  27.1 us (26%)
  other arithmetic  6.78 us (7%)
  matrix products  5.61 us (5%)
  between operations  1.32 us (1%)
    all_to_all x1, waiting for transfers between devices, per_device(): lax.all_to_all(buffer, 'clu', split_axis=0, concat_axis=0, tiled=True)  34.4 us
    all_to_all x1, starting transfers between devices, per_device(): lax.all_to_all(buffer, 'clu', split_axis=0, concat_axis=0, tiled=True)  19.5 us
    all_to_all x1, starting transfers between devices, gather_inverses(): lax.all_to_all(copies, 'grp', split_axis=0, concat_axis=0, tiled=True)  7.59 us
    unnamed x52, local copies, waits for them, and re-layouts  7.3 us
    reshape x4, local copies, waits for them, and re-layouts, per_device(): part.reshape(block_count, rank_width, block_count, rank_width)  4.67 us
    gather x1, local copies, waits for them, and re-layouts, per_device(): upper_pivoted = jnp.take(upper_masked, pivots[0], axis=3)  2.95 us
    gather x2, local copies, waits for them, and re-layouts, per_device(): part.reshape(block_count, rank_width, block_count, rank_width)  2.46 us
  transfers between devices with their start and end apart: 2, of which 1 were waited for; matrix products, arithmetic and copies ran while one was open for 19% of the time, Pallas kernels for 0%

profile of v5, /device:TPU:1, one launch (start us, length us, event | category | flops | bytes accessed | tf_op | source)
XLA Modules:
  0.0 102.9 jit_solution(16343970070799684226)
XLA Ops:
  0.6 1.0 fusion.8
  1.6 1.2 %broadcast_in_dim.54 = bf16[16,2,32,544]{3,2,1,0:T(8,128)(2,1)} broadcast(bf16[2,32,544]{2,1,0:T(8,128)(2,1)S(1)} %fusion.8), dimensions={1,2,3} | broadcast | bytes 1183744 | tf_op jit(solution)/shard_map/broadcast_in_dim | solution.py:28
  2.8 7.6 %all-to-all-start = ((bf16[16,2,32,544]{3,2,1,0:T(8,128)(2,1)}), bf16[16,2,32,544]{3,2,1,0:T(8,128)(2,1)S(1)}, u32[]{:S(2)}, u32[]{:S(2)}) async-start(bf16[16,2,32,544]{3,2,1,0:T(8,128)(2,1)} %broadcast_in_dim.54), calls=%async_computation | async-start | bytes 2621440 | tf_op jit(solution)/shard_map/all_to_all | solution.py:29
  10.5 2.6 %copy.39 = bf16[1,8,2,48,512]{3,1,4,2,0:T(8,128)(2,1)S(1)} copy(bf16[1,8,2,48,512]{4,3,2,1,0:T(8,128)(2,1)} %param.12) | data formatting | bytes 1572864 | tf_op args[2]
  13.1 0.1 bitcast_select_fusion.1
  13.3 0.1 fusion.18
  13.4 1.5 %copy.40 = bf16[8,1,48,512]{3,2,0,1:T(8,128)(2,1)} copy(bf16[8,1,48,512]{2,0,3,1:T(8,128)(2,1)S(1)} %get-tuple-element.6) | data formatting | bytes 786432 | tf_op jit(solution)/shard_map/slice | solution.py:57
  14.9 1.5 %copy.41 = bf16[8,1,48,512]{3,2,0,1:T(8,128)(2,1)} copy(bf16[8,1,48,512]{2,0,3,1:T(8,128)(2,1)S(1)} %get-tuple-element.5) | data formatting | bytes 786432 | tf_op jit(solution)/shard_map/slice | solution.py:58
  16.4 2.6 %copy.44 = bf16[1,8,2,48,512]{3,1,4,2,0:T(8,128)(2,1)S(1)} copy(bf16[1,8,2,48,512]{4,3,2,1,0:T(8,128)(2,1)} %param.13) | data formatting | bytes 1572864 | tf_op args[3]
  19.1 1.5 %bitcast_select_fusion = bf16[8,2,48,512]{2,0,3,1:T(8,128)(2,1)} fusion(bf16[1,8,2,48,512]{3,1,4,2,0:T(8,128)(2,1)S(1)} %copy.44, pred[8,48]{1,0:T(8,128)(4,1)S(1)} %iota_compare_fusion.3), kind=kLoop, calls=%fused_computation.4 | loop fusion | flops 393216 | bytes 1573248 | tf_op jit(solution)/shard_map/jit(_where)/select_n | solution.py:13
  20.6 3.0 %gather_fusion = bf16[512,8,2,48]{3,1,2,0:T(8,128)(2,1)S(1)} fusion(bf16[8,2,48,512]{2,0,3,1:T(8,128)(2,1)} %bitcast_select_fusion, s32[1024]{0:T(1024)S(1)} %pad_clamp_fusion), kind=kCustom, calls=%fused_computation | custom fusion | bytes 1574912 | tf_op jit(solution)/shard_map/jit(_take)/gather | solution.py:53
  23.5 1.8 %select_bitcast_fusion = bf16[8,2,48,512]{2,0,1,3:T(8,128)(2,1)S(1)} fusion(bf16[512,8,2,48]{3,1,2,0:T(8,128)(2,1)S(1)} %gather_fusion, pred[512]{0:T(512)(128)(4,1)S(1)} %compare_and_fusion), kind=kLoop, calls=%fused_computation.6 | loop fusion | flops 393216 | bytes 1573376 | tf_op jit(solution)/shard_map/jit(_take)/select_n | solution.py:53
  25.3 0.1 fusion.17
  25.5 1.5 %copy.45 = bf16[8,1,48,512]{3,2,0,1:T(8,128)(2,1)} copy(bf16[8,1,48,512]{2,0,1,3:T(8,128)(2,1)S(1)} %get-tuple-element.4) | data formatting | bytes 786432 | tf_op jit(solution)/shard_map/slice | solution.py:59
  26.9 0.7 copy.46
  27.7 0.2 convert_reduce_fusion
  27.9 0.1 slice_bitcast_fusion.12
  29.5 0.1 constant_dynamic-update-slice_fusion.14
  29.6 0.1 constant_dynamic-update-slice_fusion.13
  29.7 0.1 constant_dynamic-update-slice_fusion.12
  30.6 0.4 fusion.5
  31.0 0.4 fusion.4
  31.4 0.4 fusion.7
  31.8 0.4 fusion.6
  32.2 0.2 copy-done
  32.4 0.4 fusion.1
  32.7 0.4 fusion
  33.1 0.4 fusion.3
  33.5 0.4 fusion.2
  33.9 0.4 fusion.20
  34.3 0.4 fusion.19
  34.7 0.4 convolution_add_fusion.2
  35.1 0.7 reshape.179
  35.8 1.0 copy.50
  36.8 1.1 %convolution_subtract_fusion.2 = bf16[384,384]{1,0:T(8,128)(2,1)} fusion(f32[384,384]{1,0:T(8,128)S(1)} %fusion.19, bf16[384,512]{1,0:T(8,128)(2,1)S(1)} %fusion.1, bf16[384,512]{1,0:T(8,128)(2,1)S(1)} %fusion.3), kind=kOutput, calls=%fused_computation.16 | convolution fusion | flops 151289856 | bytes 1671168 | tf_op jit(solution)/shard_map/dot_general | solution.py:91
  37.9 2.0 %reshape.178 = bf16[8,48,8,48]{3,2,1,0:T(8,128)(2,1)S(1)} reshape(bf16[384,384]{1,0:T(8,128)(2,1)} %convolution_subtract_fusion.2) | data formatting | bytes 589824 | tf_op jit(solution)/shard_map/reshape | solution.py:97
  39.9 1.0 copy.49
  40.9 0.7 gather_fusion.2
  41.6 1.8 %gather_fusion.1 = bf16[32,48,48]{2,1,0:T(8,128)(2,1)S(1)} fusion(bf16[8,48,8,48]{3,1,2,0:T(8,128)(2,1)} %copy.49, s32[32]{0:T(128)S(1)} %fusion.16), kind=kCustom, calls=%fused_computation.1 | custom fusion | bytes 295168 | tf_op jit(solution)/shard_map/gather | solution.py:97
  43.4 0.2 pad_maximum_fusion
  43.6 1.4 %convert_element_type.76 = bf16[32,4608]{1,0:T(8,128)(2,1)S(1)} reshape(bf16[32,2,48,48]{3,2,1,0:T(8,128)(2,1)S(1)} %copy.51) | data formatting | bytes 589824 | tf_op jit(solution)/shard_map/convert_element_type | solution.py:101
  45.0 0.3 convolution_convert_fusion
  45.3 1.0 reshape.180
  46.2 19.5 %all-to-all-start.1 = ((bf16[32,2,2,2304]{3,2,1,0:T(2,128)(2,1)}), bf16[32,2,2,2304]{3,2,1,0:T(2,128)(2,1)S(1)}, u32[]{:S(2)}, u32[]{:S(2)}) async-start(bf16[32,2,2,2304]{3,2,1,0:T(2,128)(2,1)} %reshape.180), calls=%async_computation.1 | async-start | bytes 1179648 | tf_op jit(solution)/shard_map/all_to_all | solution.py:112
  65.8 1.0 maximum_bitcast_fusion
  66.8 1.0 maximum_bitcast_fusion.1
  67.7 34.4 %all-to-all-done.1 = bf16[32,2,2,2304]{3,2,1,0:T(2,128)(2,1)S(1)} async-done(((bf16[32,2,2,2304]{3,2,1,0:T(2,128)(2,1)}), bf16[32,2,2,2304]{3,2,1,0:T(2,128)(2,1)S(1)}, u32[]{:S(2)}, u32[]{:S(2)}) %all-to-all-start.1) | async-done | bytes 589856 | tf_op jit(solution)/shard_map/all_to_all | solution.py:112
  102.1 0.8 copy.83
  (86 shorter events, 2.3 us)
Async XLA Ops:
  2.8 25.0 %all-to-all-start = ((bf16[16,2,32,544]{3,2,1,0:T(8,128)(2,1)}), bf16[16,2,32,544]{3,2,1,0:T(8,128)(2,1)S(1)}, u32[]{:S(2)}, u32[]{:S(2)}) async-start(bf16[16,2,32,544]{3,2,1,0:T(8,128)(2,1)} %broadcast_in_dim.54), calls=%async_computation | async-start | bytes 2621440 | tf_op jit(solution)/shard_map/all_to_all | solution.py:29
  10.4 2.6 %copy-start.5 = (s32[1,8]{1,0:T(1,128)S(1)}, s32[1,8]{1,0:T(1,128)}, u32[]{:S(2)}) copy-start(s32[1,8]{1,0:T(1,128)} %param.14) | copy-start | bytes 100
  14.9 4.1 %copy-start.6 = (s32[1,8]{1,0:T(1,128)S(1)}, s32[1,8]{1,0:T(1,128)}, u32[]{:S(2)}) copy-start(s32[1,8]{1,0:T(1,128)} %param.15) | copy-start | bytes 100
  14.9 4.2 %copy-start.4 = (s32[1,512]{1,0:T(1,128)S(1)}, s32[1,512]{1,0:T(1,128)}, u32[]{:S(2)}) copy-start(s32[1,512]{1,0:T(1,128)} %param.16) | copy-start | bytes 6148
  25.4 2.2 %copy-start.7 = (s32[1,32,1]{1,2,0:T(1,128)S(1)}, s32[1,32,1]{1,2,0:T(1,128)}, u32[]{:S(2)}) copy-start(s32[1,32,1]{1,2,0:T(1,128)} %param.19) | copy-start | bytes 388
  25.4 2.4 %copy-start.8 = (s32[1,32]{1,0:T(1,128)S(1)}, s32[1,32]{1,0:T(1,128)}, u32[]{:S(2)}) copy-start(s32[1,32]{1,0:T(1,128)} %param.18) | copy-start | bytes 388
  25.4 2.4 %copy-start.9 = (s32[1,32]{1,0:T(1,128)S(1)}, s32[1,32]{1,0:T(1,128)}, u32[]{:S(2)}) copy-start(s32[1,32]{1,0:T(1,128)} %param.17) | copy-start | bytes 388
  28.8 1.8 %copy-start.1 = (bf16[8,1,48,512]{3,2,0,1:T(8,128)(2,1)S(1)}, bf16[8,1,48,512]{3,2,0,1:T(8,128)(2,1)}, u32[]{:S(2)}) copy-start(bf16[8,1,48,512]{3,2,0,1:T(8,128)(2,1)} %copy.40) | copy-start | bytes 1179652
  30.0 1.4 %copy-start.2 = (bf16[8,1,48,512]{3,2,0,1:T(8,128)(2,1)S(1)}, bf16[8,1,48,512]{3,2,0,1:T(8,128)(2,1)}, u32[]{:S(2)}) copy-start(bf16[8,1,48,512]{3,2,0,1:T(8,128)(2,1)} %copy.45) | copy-start | bytes 1179652
  31.4 1.0 copy-start
  37.9 3.0 %copy-start.3 = (bf16[8,48,8,48]{3,1,2,0:T(8,128)(2,1)S(1)}, bf16[8,48,8,48]{3,1,2,0:T(8,128)(2,1)}, u32[]{:S(2)}) copy-start(bf16[8,48,8,48]{3,1,2,0:T(8,128)(2,1)} %copy.50) | copy-start | bytes 884740
  46.2 55.8 %all-to-all-start.1 = ((bf16[32,2,2,2304]{3,2,1,0:T(2,128)(2,1)}), bf16[32,2,2,2304]{3,2,1,0:T(2,128)(2,1)S(1)}, u32[]{:S(2)}, u32[]{:S(2)}) async-start(bf16[32,2,2,2304]{3,2,1,0:T(2,128)(2,1)} %reshape.180), calls=%async_computation.1 | async-start | bytes 1179648 | tf_op jit(solution)/shard_map/all_to_all | solution.py:112

commit v6 on v5

--- a/solution.py
+++ b/solution.py
@@ -93,10 +93,21 @@
         lower_totals[0], upper_totals[1], contract_last, preferred_element_type=jnp.float32
     ) + lax.dot_general(lower_totals[1], upper_totals[0], contract_last, preferred_element_type=jnp.float32)
     pair_count = pair_lower.shape[1]
-    picked = [
-        part.reshape(block_count, rank_width, block_count, rank_width)[pair_lower[0], :, pair_upper[0], :]
-        for part in (real_part, imag_part)
-    ]
+    side = block_count * rank_width
+    line_ids = lax.broadcasted_iota(jnp.int32, (pair_count, rank_width, side), 2)
+    within = lax.broadcasted_iota(jnp.int32, (pair_count, rank_width, side), 1)
+    row_pick = (line_ids == pair_lower[0][:, None, None] * rank_width + within).astype(jnp.bfloat16)
+    col_pick = (line_ids == pair_upper[0][:, None, None] * rank_width + within).astype(jnp.bfloat16)
+    picked = []
+    for part in (real_part, imag_part):
+        rows_of = jnp.dot(
+            row_pick.reshape(pair_count * rank_width, side),
+            part.astype(jnp.bfloat16),
+            preferred_element_type=jnp.float32,
+        ).astype(jnp.bfloat16).reshape(pair_count, rank_width, side)
+        picked.append(
+            jnp.einsum("qrl,qsl->qrs", rows_of, col_pick, preferred_element_type=jnp.float32)
+        )
     picked = jnp.stack(picked, 1)
     cores = picked.reshape(pair_count, 2 * rank_width * rank_width).astype(jnp.bfloat16)
     owners = pair_owner[0, :, 0]

time: 103 us -> 102 us (level)
  matrix products: 5.61 us -> 11.3 us
  local copies, waits for them, and re-layouts: 27.7 us -> 23.8 us
  starting transfers between devices: 27.1 us -> 23.8 us
    dot_general x2 -> x4, matrix products: 1.49 us -> 7.15 us  [the longest x2 4.52 us: per_device(): jnp.dot(row_pick.reshape(pair_count * rank_width, side), part.astype(jnp....]
    reshape x4 -> x0, local copies, waits for them, and re-layouts: 4.67 us -> none  [per_device(): part.reshape(block_count, rank_width, block_count, rank_width)]
    all_to_all x1, starting transfers between devices: 19.5 us -> 16.2 us  [per_device(): lax.all_to_all(buffer, 'clu', split_axis=0, concat_axis=0, tiled=True)]
    gather x2 -> x0, local copies, waits for them, and re-layouts: 2.46 us -> none  [per_device(): part.reshape(block_count, rank_width, block_count, rank_width)]
    slice x2, local copies, waits for them, and re-layouts: 1.6 us -> 2.96 us  [per_device(): lower_masked[:, 1].reshape(block_count * rank_width, panel_count)]
    slice x2, local copies, waits for them, and re-layouts: 0.85 us -> 2.2 us  [per_device(): upper_pivoted[:, 1].reshape(block_count * rank_width, panel_count)]
    unnamed x52 -> x56, local copies, waits for them, and re-layouts: 7.3 us -> 7.42 us
  transfers between devices with their start and end apart: 2 -> 2, of which waited for: 1 -> 1; matrix products, arithmetic and copies ran while one was open for 19% -> 22% of each run, Pallas kernels for 0% -> 0%
where the time goes in v6:
time: 102 us
  waiting for transfers between devices  34.4 us (34%)
  local copies, waits for them, and re-layouts  23.8 us (23%)
  starting transfers between devices  23.8 us (23%)
  matrix products  11.3 us (11%)
  other arithmetic  7.03 us (7%)
  between operations  1.31 us (1%)
    all_to_all x1, waiting for transfers between devices, per_device(): lax.all_to_all(buffer, 'clu', split_axis=0, concat_axis=0, tiled=True)  34.4 us
    all_to_all x1, starting transfers between devices, per_device(): lax.all_to_all(buffer, 'clu', split_axis=0, concat_axis=0, tiled=True)  16.2 us
    all_to_all x1, starting transfers between devices, gather_inverses(): lax.all_to_all(copies, 'grp', split_axis=0, concat_axis=0, tiled=True)  7.59 us
    unnamed x56, local copies, waits for them, and re-layouts  7.42 us
    dot_general x2, matrix products, per_device(): jnp.dot(row_pick.reshape(pair_count * rank_width, side), part.astype(jnp....  4.52 us
    slice x2, local copies, waits for them, and re-layouts, per_device(): lower_masked[:, 1].reshape(block_count * rank_width, panel_count)  2.96 us
    gather x1, local copies, waits for them, and re-layouts, per_device(): upper_pivoted = jnp.take(upper_masked, pivots[0], axis=3)  2.95 us
    dot_general x2, matrix products, per_device(): jnp.einsum('qrl,qsl->qrs', rows_of, col_pick, preferred_element_type=jnp....  2.63 us
  transfers between devices with their start and end apart: 2, of which 1 were waited for; matrix products, arithmetic and copies ran while one was open for 22% of the time, Pallas kernels for 0%

profile of v6, /device:TPU:1, one launch (start us, length us, event | category | flops | bytes accessed | tf_op | source)
XLA Modules:
  0.0 101.6 jit_solution(7354596470809505993)
XLA Ops:
  0.6 1.0 fusion.20
  1.6 1.2 %broadcast_in_dim.50 = bf16[16,2,32,544]{3,2,1,0:T(8,128)(2,1)} broadcast(bf16[2,32,544]{2,1,0:T(8,128)(2,1)S(1)} %fusion.20), dimensions={1,2,3} | broadcast | bytes 1183744 | tf_op jit(solution)/shard_map/broadcast_in_dim | solution.py:28
  2.8 7.6 %all-to-all-start = ((bf16[16,2,32,544]{3,2,1,0:T(8,128)(2,1)}), bf16[16,2,32,544]{3,2,1,0:T(8,128)(2,1)S(1)}, u32[]{:S(2)}, u32[]{:S(2)}) async-start(bf16[16,2,32,544]{3,2,1,0:T(8,128)(2,1)} %broadcast_in_dim.50), calls=%async_computation | async-start | bytes 2621440 | tf_op jit(solution)/shard_map/all_to_all | solution.py:29
  10.4 2.6 %copy.35 = bf16[1,8,2,48,512]{3,1,4,2,0:T(8,128)(2,1)S(1)} copy(bf16[1,8,2,48,512]{4,3,2,1,0:T(8,128)(2,1)} %param.12) | data formatting | bytes 1572864 | tf_op args[2]
  13.1 0.1 bitcast_select_fusion.1
  13.3 1.5 %fusion.24 = (bf16[8,1,48,512]{2,0,3,1:T(8,128)(2,1)}, bf16[8,1,48,512]{2,0,3,1:T(8,128)(2,1)}) fusion(bf16[8,2,48,512]{2,0,3,1:T(8,128)(2,1)S(1)} %bitcast_select_fusion.1), kind=kLoop, calls=%fused_computation.109 | loop fusion | bytes 1572864 | tf_op jit(solution)/shard_map/slice | solution.py:58
  14.8 2.6 %copy.40 = bf16[1,8,2,48,512]{3,1,4,2,0:T(8,128)(2,1)S(1)} copy(bf16[1,8,2,48,512]{4,3,2,1,0:T(8,128)(2,1)} %param.13) | data formatting | bytes 1572864 | tf_op args[3]
  17.5 1.5 %bitcast_select_fusion = bf16[8,2,48,512]{2,0,3,1:T(8,128)(2,1)} fusion(bf16[1,8,2,48,512]{3,1,4,2,0:T(8,128)(2,1)S(1)} %copy.40, pred[8,48]{1,0:T(8,128)(4,1)S(1)} %iota_compare_fusion.6), kind=kLoop, calls=%fused_computation.8 | loop fusion | flops 393216 | bytes 1573248 | tf_op jit(solution)/shard_map/jit(_where)/select_n | solution.py:13
  19.0 3.0 %gather_fusion = bf16[512,8,2,48]{3,1,2,0:T(8,128)(2,1)S(1)} fusion(bf16[8,2,48,512]{2,0,3,1:T(8,128)(2,1)} %bitcast_select_fusion, s32[1024]{0:T(1024)S(1)} %pad_clamp_fusion), kind=kCustom, calls=%fused_computation | custom fusion | bytes 1574912 | tf_op jit(solution)/shard_map/jit(_take)/gather | solution.py:53
  22.0 1.9 %select_bitcast_fusion = bf16[8,2,48,512]{2,0,1,3:T(8,128)(2,1)S(1)} fusion(bf16[512,8,2,48]{3,1,2,0:T(8,128)(2,1)S(1)} %gather_fusion, pred[512]{0:T(512)(128)(4,1)S(1)} %compare_and_fusion), kind=kLoop, calls=%fused_computation.10 | loop fusion | flops 393216 | bytes 1573376 | tf_op jit(solution)/shard_map/jit(_take)/select_n | solution.py:53
  23.9 1.5 %fusion.23 = (bf16[8,1,48,512]{2,0,1,3:T(8,128)(2,1)}, bf16[8,1,48,512]{2,0,1,3:T(8,128)(2,1)}) fusion(bf16[8,2,48,512]{2,0,1,3:T(8,128)(2,1)S(1)} %select_bitcast_fusion), kind=kLoop, calls=%fused_computation.108 | loop fusion | bytes 1572864 | tf_op jit(solution)/shard_map/slice | solution.py:60
  25.5 1.5 %copy.36 = bf16[8,1,48,512]{3,2,0,1:T(8,128)(2,1)} copy(bf16[8,1,48,512]{2,0,3,1:T(8,128)(2,1)S(1)} %copy-done.1) | data formatting | bytes 786432 | tf_op jit(solution)/shard_map/slice | solution.py:57
  27.0 1.5 %copy.37 = bf16[8,1,48,512]{3,2,0,1:T(8,128)(2,1)} copy(bf16[8,1,48,512]{2,0,3,1:T(8,128)(2,1)S(1)} %copy-done) | data formatting | bytes 786432 | tf_op jit(solution)/shard_map/slice | solution.py:58
  28.4 1.8 %copy.41 = bf16[8,1,48,512]{3,2,0,1:T(8,128)(2,1)S(1)} copy(bf16[8,1,48,512]{2,0,1,3:T(8,128)(2,1)} %get-tuple-element.4) | data formatting | bytes 786432 | tf_op jit(solution)/shard_map/slice | solution.py:59
  30.3 0.7 copy.42
  31.2 0.2 convert_reduce_fusion
  31.4 0.1 slice_bitcast_fusion.12
  32.1 0.1 slice.280
  32.5 0.1 slice.284
  32.6 0.1 slice.285
  33.0 0.1 slice_dynamic-update-slice_fusion
  33.1 0.1 constant_dynamic-update-slice_fusion.14
  33.2 0.1 constant_dynamic-update-slice_fusion.13
  33.2 0.1 constant_dynamic-update-slice_fusion.12
  34.1 0.4 fusion.17
  34.5 0.4 fusion.16
  34.9 0.4 fusion.19
  35.3 0.4 fusion.18
  35.7 0.2 copy-done.3
  35.9 0.4 fusion.3
  36.2 0.4 fusion.2
  36.6 0.4 fusion.5
  37.0 0.4 fusion.4
  37.4 0.4 fusion.26
  37.8 0.4 fusion.25
  38.2 2.3 %convolution_convert_fusion.1 = bf16[1536,384]{1,0:T(8,128)(2,1)} fusion(s32[1536]{0:T(1024)S(1)} %add.133, f32[384,384]{1,0:T(8,128)S(1)} %fusion.26, bf16[384,512]{1,0:T(8,128)(2,1)S(1)} %fusion.3, bf16[384,512]{1,0:T(8,128)(2,1)S(1)} %fusion.4), kind=kOutput, calls=%fused_computation.2 | convolution fusion | flops 605454336 | bytes 2562048 | tf_op jit(solution)/shard_map/dot_general | solution.py:103
  40.5 2.2 %convolution_convert_fusion.2 = bf16[1536,384]{1,0:T(8,128)(2,1)} fusion(s32[1536]{0:T(1024)S(1)} %add.133, f32[384,384]{1,0:T(8,128)S(1)} %fusion.25, bf16[384,512]{1,0:T(8,128)(2,1)S(1)} %fusion.3, bf16[384,512]{1,0:T(8,128)(2,1)S(1)} %fusion.5), kind=kOutput, calls=%fused_computation.3 | convolution fusion | flops 605454336 | bytes 2562048 | tf_op jit(solution)/shard_map/dot_general | solution.py:103
  42.7 2.0 %fusion.10 = bf16[32,1,48,48]{3,2,0,1:T(8,128)(2,1)S(1)} fusion(bf16[32,48,384]{2,1,0:T(8,128)(2,1)} %bitcast.141, s32[32]{0:T(128)S(1)} %multiply_bitcast_fusion), kind=kOutput, calls=%fused_computation.25 | convolution fusion | flops 57876480 | bytes 1327232 | tf_op jit(solution)/shard_map/qrl,qsl->qrs/dot_general | solution.py:109
  44.8 0.6 fusion.11
  45.4 0.2 pad_maximum_fusion
  45.6 1.4 %convert_element_type.94 = bf16[32,4608]{1,0:T(8,128)(2,1)S(1)} reshape(bf16[32,2,48,48]{3,2,1,0:T(8,128)(2,1)S(1)} %copy.45) | data formatting | bytes 589824 | tf_op jit(solution)/shard_map/convert_element_type | solution.py:112
  47.0 0.3 convolution_convert_fusion
  47.3 1.0 reshape.148
  48.3 16.2 %all-to-all-start.1 = ((bf16[32,2,2,2304]{3,2,1,0:T(2,128)(2,1)}), bf16[32,2,2,2304]{3,2,1,0:T(2,128)(2,1)S(1)}, u32[]{:S(2)}, u32[]{:S(2)}) async-start(bf16[32,2,2,2304]{3,2,1,0:T(2,128)(2,1)} %reshape.148), calls=%async_computation.1 | async-start | bytes 1179648 | tf_op jit(solution)/shard_map/all_to_all | solution.py:123
  64.5 1.0 maximum_bitcast_fusion
  65.4 1.0 maximum_bitcast_fusion.1
  66.4 34.4 %all-to-all-done.1 = bf16[32,2,2,2304]{3,2,1,0:T(2,128)(2,1)S(1)} async-done(((bf16[32,2,2,2304]{3,2,1,0:T(2,128)(2,1)}), bf16[32,2,2,2304]{3,2,1,0:T(2,128)(2,1)S(1)}, u32[]{:S(2)}, u32[]{:S(2)}) %all-to-all-start.1) | async-done | bytes 589856 | tf_op jit(solution)/shard_map/all_to_all | solution.py:123
  100.8 0.8 copy.77
  (89 shorter events, 2.1 us)
Async XLA Ops:
  2.8 28.6 %all-to-all-start = ((bf16[16,2,32,544]{3,2,1,0:T(8,128)(2,1)}), bf16[16,2,32,544]{3,2,1,0:T(8,128)(2,1)S(1)}, u32[]{:S(2)}, u32[]{:S(2)}) async-start(bf16[16,2,32,544]{3,2,1,0:T(8,128)(2,1)} %broadcast_in_dim.50), calls=%async_computation | async-start | bytes 2621440 | tf_op jit(solution)/shard_map/all_to_all | solution.py:29
  10.4 2.6 %copy-start.6 = (s32[1,8]{1,0:T(1,128)S(1)}, s32[1,8]{1,0:T(1,128)}, u32[]{:S(2)}) copy-start(s32[1,8]{1,0:T(1,128)} %param.14) | copy-start | bytes 100
  14.8 2.6 %copy-start.7 = (s32[1,8]{1,0:T(1,128)S(1)}, s32[1,8]{1,0:T(1,128)}, u32[]{:S(2)}) copy-start(s32[1,8]{1,0:T(1,128)} %param.15) | copy-start | bytes 100
  14.8 2.7 %copy-start.5 = (s32[1,512]{1,0:T(1,128)S(1)}, s32[1,512]{1,0:T(1,128)}, u32[]{:S(2)}) copy-start(s32[1,512]{1,0:T(1,128)} %param.16) | copy-start | bytes 6148
  23.9 1.6 %copy-start.1 = (bf16[8,1,48,512]{2,0,3,1:T(8,128)(2,1)S(1)}, bf16[8,1,48,512]{2,0,3,1:T(8,128)(2,1)}, u32[]{:S(2)}) copy-start(bf16[8,1,48,512]{2,0,3,1:T(8,128)(2,1)} %get-tuple-element.6) | copy-start | bytes 1179652
  23.9 3.0 %copy-start = (bf16[8,1,48,512]{2,0,3,1:T(8,128)(2,1)S(1)}, bf16[8,1,48,512]{2,0,3,1:T(8,128)(2,1)}, u32[]{:S(2)}) copy-start(bf16[8,1,48,512]{2,0,3,1:T(8,128)(2,1)} %get-tuple-element.5) | copy-start | bytes 1179652
  26.9 3.4 %copy-start.2 = (bf16[8,1,48,512]{2,0,1,3:T(8,128)(2,1)S(1)}, bf16[8,1,48,512]{2,0,1,3:T(8,128)(2,1)}, u32[]{:S(2)}) copy-start(bf16[8,1,48,512]{2,0,1,3:T(8,128)(2,1)} %get-tuple-element.3) | copy-start | bytes 1179652
  26.9 4.1 %copy-start.8 = (s32[1,32]{1,0:T(1,128)S(1)}, s32[1,32]{1,0:T(1,128)}, u32[]{:S(2)}) copy-start(s32[1,32]{1,0:T(1,128)} %param.17) | copy-start | bytes 388
  26.9 4.2 %copy-start.10 = (s32[1,32,1]{1,2,0:T(1,128)S(1)}, s32[1,32,1]{1,2,0:T(1,128)}, u32[]{:S(2)}) copy-start(s32[1,32,1]{1,2,0:T(1,128)} %param.19) | copy-start | bytes 388
  26.9 4.4 %copy-start.9 = (s32[1,32]{1,0:T(1,128)S(1)}, s32[1,32]{1,0:T(1,128)}, u32[]{:S(2)}) copy-start(s32[1,32]{1,0:T(1,128)} %param.18) | copy-start | bytes 388
  32.3 1.8 %copy-start.4 = (bf16[8,1,48,512]{3,2,0,1:T(8,128)(2,1)S(1)}, bf16[8,1,48,512]{3,2,0,1:T(8,128)(2,1)}, u32[]{:S(2)}) copy-start(bf16[8,1,48,512]{3,2,0,1:T(8,128)(2,1)} %copy.36) | copy-start | bytes 1179652
  34.9 1.0 copy-start.3
  42.7 2.0 %copy-start.11 = (bf16[1536,384]{1,0:T(8,128)(2,1)S(1)}, bf16[1536,384]{1,0:T(8,128)(2,1)}, u32[]{:S(2)}) copy-start(bf16[1536,384]{1,0:T(8,128)(2,1)} %convolution_convert_fusion.2) | copy-start | bytes 3538948
  48.3 52.5 %all-to-all-start.1 = ((bf16[32,2,2,2304]{3,2,1,0:T(2,128)(2,1)}), bf16[32,2,2,2304]{3,2,1,0:T(2,128)(2,1)S(1)}, u32[]{:S(2)}, u32[]{:S(2)}) async-start(bf16[32,2,2,2304]{3,2,1,0:T(2,128)(2,1)} %reshape.148), calls=%async_computation.1 | async-start | bytes 1179648 | tf_op jit(solution)/shard_map/all_to_all | solution.py:123

commit v7 on v5

--- a/solution.py
+++ b/solution.py
@@ -86,18 +86,20 @@
     upper_solved = jnp.transpose(
         upper_totals.reshape(2, block_count, rank_width, panel_count), (1, 0, 2, 3)
     )
+    lane_tile = 128
+    padded = jnp.pad(
+        upper_totals.reshape(2, block_count, rank_width, panel_count),
+        ((0, 0), (0, 0), (0, lane_tile - rank_width), (0, 0)),
+    ).reshape(2, block_count * lane_tile, panel_count)
     real_part = lax.dot_general(
-        lower_totals[0], upper_totals[0], contract_last, preferred_element_type=jnp.float32
-    ) - lax.dot_general(lower_totals[1], upper_totals[1], contract_last, preferred_element_type=jnp.float32)
+        lower_totals[0], padded[0], contract_last, preferred_element_type=jnp.float32
+    ) - lax.dot_general(lower_totals[1], padded[1], contract_last, preferred_element_type=jnp.float32)
     imag_part = lax.dot_general(
-        lower_totals[0], upper_totals[1], contract_last, preferred_element_type=jnp.float32
-    ) + lax.dot_general(lower_totals[1], upper_totals[0], contract_last, preferred_element_type=jnp.float32)
+        lower_totals[0], padded[1], contract_last, preferred_element_type=jnp.float32
+    ) + lax.dot_general(lower_totals[1], padded[0], contract_last, preferred_element_type=jnp.float32)
+    grid = jnp.stack([real_part, imag_part], 0).reshape(2, block_count, rank_width, block_count, lane_tile)
     pair_count = pair_lower.shape[1]
-    picked = [
-        part.reshape(block_count, rank_width, block_count, rank_width)[pair_lower[0], :, pair_upper[0], :]
-        for part in (real_part, imag_part)
-    ]
-    picked = jnp.stack(picked, 1)
+    picked = grid[:, pair_lower[0], :, pair_upper[0], :][..., :rank_width]
     cores = picked.reshape(pair_count, 2 * rank_width * rank_width).astype(jnp.bfloat16)
     owners = pair_owner[0, :, 0]
     pair_ids = lax.broadcasted_iota(jnp.int32, (pair_count,), 0)

time: 103 us -> 98.8 us (0.959)
  local copies, waits for them, and re-layouts: 27.7 us -> 22 us
    reshape x4 -> x0, local copies, waits for them, and re-layouts: 4.67 us -> none  [per_device(): part.reshape(block_count, rank_width, block_count, rank_width)]
    gather x2 -> x1, local copies, waits for them, and re-layouts: 2.46 us -> 0.71 us  [per_device(): picked = grid[:, pair_lower[0], :, pair_upper[0], :][..., :rank_width]]
where the time goes in v7:
time: 98.8 us; the launch traced here: 98.4 us
  waiting for transfers between devices  35.3 us (36%)
  starting transfers between devices  27 us (27%)
  local copies, waits for them, and re-layouts  22 us (22%)
  other arithmetic  6.95 us (7%)
  matrix products  5.8 us (6%)
  between operations  1.35 us (1%)
    all_to_all x1, waiting for transfers between devices, per_device(): lax.all_to_all(buffer, 'clu', split_axis=0, concat_axis=0, tiled=True)  35.3 us
    all_to_all x1, starting transfers between devices, per_device(): lax.all_to_all(buffer, 'clu', split_axis=0, concat_axis=0, tiled=True)  19.4 us
    unnamed x52, local copies, waits for them, and re-layouts  7.64 us
    all_to_all x1, starting transfers between devices, gather_inverses(): lax.all_to_all(copies, 'grp', split_axis=0, concat_axis=0, tiled=True)  7.59 us
    gather x1, local copies, waits for them, and re-layouts, per_device(): upper_pivoted = jnp.take(upper_masked, pivots[0], axis=3)  2.95 us
  transfers between devices with their start and end apart: 2, of which 1 were waited for; matrix products, arithmetic and copies ran while one was open for 19% of the time, Pallas kernels for 0%

profile of v7, /device:TPU:1, one launch (start us, length us, event | category | flops | bytes accessed | tf_op | source)
XLA Modules:
  0.0 98.4 jit_solution(7072723499108203649)
XLA Ops:
  0.6 1.0 fusion.8
  1.6 1.2 %broadcast_in_dim.52 = bf16[16,2,32,544]{3,2,1,0:T(8,128)(2,1)} broadcast(bf16[2,32,544]{2,1,0:T(8,128)(2,1)S(1)} %fusion.8), dimensions={1,2,3} | broadcast | bytes 1183744 | tf_op jit(solution)/shard_map/broadcast_in_dim | solution.py:28
  2.8 7.6 %all-to-all-start = ((bf16[16,2,32,544]{3,2,1,0:T(8,128)(2,1)}), bf16[16,2,32,544]{3,2,1,0:T(8,128)(2,1)S(1)}, u32[]{:S(2)}, u32[]{:S(2)}) async-start(bf16[16,2,32,544]{3,2,1,0:T(8,128)(2,1)} %broadcast_in_dim.52), calls=%async_computation | async-start | bytes 2621440 | tf_op jit(solution)/shard_map/all_to_all | solution.py:29
  10.4 2.6 %copy.37 = bf16[1,8,2,48,512]{3,1,4,2,0:T(8,128)(2,1)S(1)} copy(bf16[1,8,2,48,512]{4,3,2,1,0:T(8,128)(2,1)} %param.12) | data formatting | bytes 1572864 | tf_op args[2]
  13.1 0.1 bitcast_select_fusion.1
  13.3 0.1 fusion.19
  13.4 1.5 %copy.38 = bf16[8,1,48,512]{3,2,0,1:T(8,128)(2,1)} copy(bf16[8,1,48,512]{2,0,3,1:T(8,128)(2,1)S(1)} %get-tuple-element.6) | data formatting | bytes 786432 | tf_op jit(solution)/shard_map/slice | solution.py:57
  14.9 1.5 %copy.39 = bf16[8,1,48,512]{3,2,0,1:T(8,128)(2,1)} copy(bf16[8,1,48,512]{2,0,3,1:T(8,128)(2,1)S(1)} %get-tuple-element.5) | data formatting | bytes 786432 | tf_op jit(solution)/shard_map/slice | solution.py:58
  16.4 2.6 %copy.42 = bf16[1,8,2,48,512]{3,1,4,2,0:T(8,128)(2,1)S(1)} copy(bf16[1,8,2,48,512]{4,3,2,1,0:T(8,128)(2,1)} %param.13) | data formatting | bytes 1572864 | tf_op args[3]
  19.1 1.5 %bitcast_select_fusion = bf16[8,2,48,512]{2,0,3,1:T(8,128)(2,1)} fusion(bf16[1,8,2,48,512]{3,1,4,2,0:T(8,128)(2,1)S(1)} %copy.42, pred[8,48]{1,0:T(8,128)(4,1)S(1)} %iota_compare_fusion.3), kind=kLoop, calls=%fused_computation.6 | loop fusion | flops 393216 | bytes 1573248 | tf_op jit(solution)/shard_map/jit(_where)/select_n | solution.py:13
  20.6 3.0 %gather_fusion = bf16[512,8,2,48]{3,1,2,0:T(8,128)(2,1)S(1)} fusion(bf16[8,2,48,512]{2,0,3,1:T(8,128)(2,1)} %bitcast_select_fusion, s32[1024]{0:T(1024)S(1)} %pad_clamp_fusion), kind=kCustom, calls=%fused_computation | custom fusion | bytes 1574912 | tf_op jit(solution)/shard_map/jit(_take)/gather | solution.py:53
  23.5 1.9 %select_bitcast_fusion = bf16[8,2,48,512]{2,0,1,3:T(8,128)(2,1)S(1)} fusion(bf16[512,8,2,48]{3,1,2,0:T(8,128)(2,1)S(1)} %gather_fusion, pred[512]{0:T(512)(128)(4,1)S(1)} %compare_and_fusion), kind=kLoop, calls=%fused_computation.8 | loop fusion | flops 393216 | bytes 1573376 | tf_op jit(solution)/shard_map/jit(_take)/select_n | solution.py:53
  25.4 0.1 fusion.18
  25.6 1.5 %copy.43 = bf16[8,1,48,512]{3,2,0,1:T(8,128)(2,1)} copy(bf16[8,1,48,512]{2,0,1,3:T(8,128)(2,1)S(1)} %get-tuple-element.4) | data formatting | bytes 786432 | tf_op jit(solution)/shard_map/slice | solution.py:59
  27.1 0.7 copy.44
  27.8 0.2 convert_reduce_fusion
  28.1 0.1 slice_bitcast_fusion.12
  29.7 0.1 constant_dynamic-update-slice_fusion.14
  29.8 0.1 constant_dynamic-update-slice_fusion.13
  29.9 0.1 constant_dynamic-update-slice_fusion.12
  30.8 0.4 fusion.5
  31.2 0.4 fusion.4
  31.6 0.4 fusion.7
  32.0 0.4 fusion.6
  32.4 0.2 copy-done
  32.5 0.4 fusion.1
  32.9 0.4 fusion
  33.3 0.4 fusion.3
  33.7 0.4 fusion.2
  34.1 1.0 pad_maximum_fusion.1
  35.1 0.2 pad_slice_fusion.1
  35.3 0.6 fusion.21
  35.9 0.6 fusion.20
  36.5 0.6 add_bitcast_fusion
  37.1 0.2 copy.50
  37.3 0.1 copy.48
  37.4 0.6 subtract_bitcast_fusion
  38.1 0.2 copy.49
  38.3 0.1 copy.47
  38.4 0.1 pad_maximum_fusion
  38.5 0.7 gather_fusion.1
  39.3 1.4 %convert_element_type.78 = bf16[32,4608]{1,0:T(8,128)(2,1)S(1)} reshape(bf16[32,2,48,48]{3,2,1,0:T(8,128)(2,1)S(1)} %bitcast.143) | data formatting | bytes 589824 | tf_op jit(solution)/shard_map/convert_element_type | solution.py:103
  40.6 0.3 convolution_convert_fusion
  40.9 1.0 reshape.181
  41.9 19.4 %all-to-all-start.1 = ((bf16[32,2,2,2304]{3,2,1,0:T(2,128)(2,1)}), bf16[32,2,2,2304]{3,2,1,0:T(2,128)(2,1)S(1)}, u32[]{:S(2)}, u32[]{:S(2)}) async-start(bf16[32,2,2,2304]{3,2,1,0:T(2,128)(2,1)} %reshape.181), calls=%async_computation.1 | async-start | bytes 1179648 | tf_op jit(solution)/shard_map/all_to_all | solution.py:114
  61.3 1.0 maximum_bitcast_fusion
  62.2 35.3 %all-to-all-done.1 = bf16[32,2,2,2304]{3,2,1,0:T(2,128)(2,1)S(1)} async-done(((bf16[32,2,2,2304]{3,2,1,0:T(2,128)(2,1)}), bf16[32,2,2,2304]{3,2,1,0:T(2,128)(2,1)S(1)}, u32[]{:S(2)}, u32[]{:S(2)}) %all-to-all-start.1) | async-done | bytes 589856 | tf_op jit(solution)/shard_map/all_to_all | solution.py:114
  97.6 0.8 copy.82
  (83 shorter events, 2.2 us)
Async XLA Ops:
  2.8 25.2 %all-to-all-start = ((bf16[16,2,32,544]{3,2,1,0:T(8,128)(2,1)}), bf16[16,2,32,544]{3,2,1,0:T(8,128)(2,1)S(1)}, u32[]{:S(2)}, u32[]{:S(2)}) async-start(bf16[16,2,32,544]{3,2,1,0:T(8,128)(2,1)} %broadcast_in_dim.52), calls=%async_computation | async-start | bytes 2621440 | tf_op jit(solution)/shard_map/all_to_all | solution.py:29
  10.4 2.6 %copy-start.4 = (s32[1,8]{1,0:T(1,128)S(1)}, s32[1,8]{1,0:T(1,128)}, u32[]{:S(2)}) copy-start(s32[1,8]{1,0:T(1,128)} %param.14) | copy-start | bytes 100
  14.9 4.1 %copy-start.5 = (s32[1,8]{1,0:T(1,128)S(1)}, s32[1,8]{1,0:T(1,128)}, u32[]{:S(2)}) copy-start(s32[1,8]{1,0:T(1,128)} %param.15) | copy-start | bytes 100
  14.9 4.2 %copy-start.3 = (s32[1,512]{1,0:T(1,128)S(1)}, s32[1,512]{1,0:T(1,128)}, u32[]{:S(2)}) copy-start(s32[1,512]{1,0:T(1,128)} %param.16) | copy-start | bytes 6148
  25.6 2.2 %copy-start.6 = (s32[1,32,1]{1,2,0:T(1,128)S(1)}, s32[1,32,1]{1,2,0:T(1,128)}, u32[]{:S(2)}) copy-start(s32[1,32,1]{1,2,0:T(1,128)} %param.19) | copy-start | bytes 388
  25.6 2.4 %copy-start.7 = (s32[1,32]{1,0:T(1,128)S(1)}, s32[1,32]{1,0:T(1,128)}, u32[]{:S(2)}) copy-start(s32[1,32]{1,0:T(1,128)} %param.18) | copy-start | bytes 388
  25.6 2.4 %copy-start.8 = (s32[1,32]{1,0:T(1,128)S(1)}, s32[1,32]{1,0:T(1,128)}, u32[]{:S(2)}) copy-start(s32[1,32]{1,0:T(1,128)} %param.17) | copy-start | bytes 388
  29.0 1.8 %copy-start.1 = (bf16[8,1,48,512]{3,2,0,1:T(8,128)(2,1)S(1)}, bf16[8,1,48,512]{3,2,0,1:T(8,128)(2,1)}, u32[]{:S(2)}) copy-start(bf16[8,1,48,512]{3,2,0,1:T(8,128)(2,1)} %copy.38) | copy-start | bytes 1179652
  30.2 1.4 %copy-start.2 = (bf16[8,1,48,512]{3,2,0,1:T(8,128)(2,1)S(1)}, bf16[8,1,48,512]{3,2,0,1:T(8,128)(2,1)}, u32[]{:S(2)}) copy-start(bf16[8,1,48,512]{3,2,0,1:T(8,128)(2,1)} %copy.43) | copy-start | bytes 1179652
  31.5 1.0 %copy-start = (bf16[8,1,48,512]{3,2,0,1:T(8,128)(2,1)S(1)}, bf16[8,1,48,512]{3,2,0,1:T(8,128)(2,1)}, u32[]{:S(2)}) copy-start(bf16[8,1,48,512]{3,2,0,1:T(8,128)(2,1)} %copy.39) | copy-start | bytes 1179652
  41.9 55.7 %all-to-all-start.1 = ((bf16[32,2,2,2304]{3,2,1,0:T(2,128)(2,1)}), bf16[32,2,2,2304]{3,2,1,0:T(2,128)(2,1)S(1)}, u32[]{:S(2)}, u32[]{:S(2)}) async-start(bf16[32,2,2,2304]{3,2,1,0:T(2,128)(2,1)} %reshape.181), calls=%async_computation.1 | async-start | bytes 1179648 | tf_op jit(solution)/shard_map/all_to_all | solution.py:114

commit v8 on v7

--- a/solution.py
+++ b/solution.py
@@ -100,7 +100,7 @@
     grid = jnp.stack([real_part, imag_part], 0).reshape(2, block_count, rank_width, block_count, lane_tile)
     pair_count = pair_lower.shape[1]
     picked = grid[:, pair_lower[0], :, pair_upper[0], :][..., :rank_width]
-    cores = picked.reshape(pair_count, 2 * rank_width * rank_width).astype(jnp.bfloat16)
+    cores = picked.reshape(pair_count, 2, rank_width * rank_width).astype(jnp.bfloat16)
     owners = pair_owner[0, :, 0]
     pair_ids = lax.broadcasted_iota(jnp.int32, (pair_count,), 0)
     same_owner = (owners[:, None] == owners[None, :]) & (pair_ids[None, :] < pair_ids[:, None])
@@ -108,8 +108,12 @@
     clusters = lax.axis_size("clu")
     target_slot = owners * SEND_CAP + slots
     slot_ids = lax.broadcasted_iota(jnp.int32, (clusters * SEND_CAP, pair_count), 0)
-    one_hot = (slot_ids == target_slot[None, :]).astype(jnp.bfloat16)
-    buffer = jnp.dot(one_hot, cores, preferred_element_type=jnp.float32).astype(jnp.bfloat16)
+    filled = slot_ids == target_slot[None, :]
+    source = jnp.where(
+        jnp.any(filled, axis=1), jnp.argmax(filled, axis=1).astype(jnp.int32), pair_count
+    )
+    cores = jnp.concatenate([cores, jnp.zeros((1,) + cores.shape[1:], cores.dtype)], axis=0)
+    buffer = jnp.take(cores, source, axis=0)
     buffer = buffer.reshape(clusters, SEND_CAP, 2, rank_width * rank_width)
     arrived = lax.all_to_all(buffer, "clu", split_axis=0, concat_axis=0, tiled=True)
     return (lower_solved[None], upper_solved[None], arrived[None, None])

time: 98.8 us -> 101 us (1.022)
  other arithmetic: 6.95 us -> 9.11 us
    gather x0 -> x1, local copies, waits for them, and re-layouts: none -> 1.77 us  [per_device(): buffer = jnp.take(cores, source, axis=0)]
    select_n x0 -> x1, other arithmetic: none -> 1.44 us  [per_device(): buffer = jnp.take(cores, source, axis=0)]
where the time goes in v8:
time: 101 us; the launch traced here: 100 us
  waiting for transfers between devices  35.3 us (35%)
  starting transfers between devices  26.2 us (26%)
  local copies, waits for them, and re-layouts  22.7 us (22%)
  other arithmetic  9.11 us (9%)
  matrix products  5.51 us (5%)
  between operations  1.36 us (1%)
    all_to_all x1, waiting for transfers between devices, per_device(): lax.all_to_all(buffer, 'clu', split_axis=0, concat_axis=0, tiled=True)  35.3 us
    all_to_all x1, starting transfers between devices, per_device(): lax.all_to_all(buffer, 'clu', split_axis=0, concat_axis=0, tiled=True)  18.6 us
    unnamed x52, local copies, waits for them, and re-layouts  7.63 us
    all_to_all x1, starting transfers between devices, gather_inverses(): lax.all_to_all(copies, 'grp', split_axis=0, concat_axis=0, tiled=True)  7.59 us
    gather x1, local copies, waits for them, and re-layouts, per_device(): upper_pivoted = jnp.take(upper_masked, pivots[0], axis=3)  2.95 us
  transfers between devices with their start and end apart: 2, of which 1 were waited for; matrix products, arithmetic and copies ran while one was open for 19% of the time, Pallas kernels for 0%

profile of v8, /device:TPU:1, one launch (start us, length us, event | category | flops | bytes accessed | tf_op | source)
XLA Modules:
  0.0 100.2 jit_solution(16515801593375251119)
XLA Ops:
  0.6 1.0 fusion.8
  1.6 1.2 %broadcast_in_dim.71 = bf16[16,2,32,544]{3,2,1,0:T(8,128)(2,1)} broadcast(bf16[2,32,544]{2,1,0:T(8,128)(2,1)S(1)} %fusion.8), dimensions={1,2,3} | broadcast | bytes 1183744 | tf_op jit(solution)/shard_map/broadcast_in_dim | solution.py:28
  2.8 7.6 %all-to-all-start = ((bf16[16,2,32,544]{3,2,1,0:T(8,128)(2,1)}), bf16[16,2,32,544]{3,2,1,0:T(8,128)(2,1)S(1)}, u32[]{:S(2)}, u32[]{:S(2)}) async-start(bf16[16,2,32,544]{3,2,1,0:T(8,128)(2,1)} %broadcast_in_dim.71), calls=%async_computation | async-start | bytes 2621440 | tf_op jit(solution)/shard_map/all_to_all | solution.py:29
  10.5 0.2 convert_reduce_fusion
  10.7 0.6 iota_reduce_fusion
  11.4 2.6 %copy.41 = bf16[1,8,2,48,512]{3,1,4,2,0:T(8,128)(2,1)S(1)} copy(bf16[1,8,2,48,512]{4,3,2,1,0:T(8,128)(2,1)} %param.12) | data formatting | bytes 1572864 | tf_op args[2]
  14.0 0.1 bitcast_select_fusion.1
  14.2 0.1 fusion.19
  14.3 1.5 %copy.42 = bf16[8,1,48,512]{3,2,0,1:T(8,128)(2,1)} copy(bf16[8,1,48,512]{2,0,3,1:T(8,128)(2,1)S(1)} %get-tuple-element.10) | data formatting | bytes 786432 | tf_op jit(solution)/shard_map/slice | solution.py:57
  15.8 1.5 %copy.43 = bf16[8,1,48,512]{3,2,0,1:T(8,128)(2,1)} copy(bf16[8,1,48,512]{2,0,3,1:T(8,128)(2,1)S(1)} %get-tuple-element.9) | data formatting | bytes 786432 | tf_op jit(solution)/shard_map/slice | solution.py:58
  17.3 2.6 %copy.46 = bf16[1,8,2,48,512]{3,1,4,2,0:T(8,128)(2,1)S(1)} copy(bf16[1,8,2,48,512]{4,3,2,1,0:T(8,128)(2,1)} %param.13) | data formatting | bytes 1572864 | tf_op args[3]
  20.0 1.5 %bitcast_select_fusion = bf16[8,2,48,512]{2,0,3,1:T(8,128)(2,1)} fusion(bf16[1,8,2,48,512]{3,1,4,2,0:T(8,128)(2,1)S(1)} %copy.46, pred[8,48]{1,0:T(8,128)(4,1)S(1)} %iota_compare_fusion.2), kind=kLoop, calls=%fused_computation.6 | loop fusion | flops 393216 | bytes 1573248 | tf_op jit(solution)/shard_map/jit(_where)/select_n | solution.py:13
  21.4 3.0 %gather_fusion = bf16[512,8,2,48]{3,1,2,0:T(8,128)(2,1)S(1)} fusion(bf16[8,2,48,512]{2,0,3,1:T(8,128)(2,1)} %bitcast_select_fusion, s32[1024]{0:T(1024)S(1)} %get-tuple-element.34), kind=kCustom, calls=%fused_computation | custom fusion | bytes 1574912 | tf_op jit(solution)/shard_map/jit(_take)/gather | solution.py:53
  24.4 1.9 %select_bitcast_fusion = bf16[8,2,48,512]{2,0,1,3:T(8,128)(2,1)S(1)} fusion(bf16[512,8,2,48]{3,1,2,0:T(8,128)(2,1)S(1)} %gather_fusion, pred[512]{0:T(512)(128)(4,1)S(1)} %compare_and_fusion.1), kind=kLoop, calls=%fused_computation.8 | loop fusion | flops 393216 | bytes 1573376 | tf_op jit(solution)/shard_map/jit(_take)/select_n | solution.py:53
  26.3 0.1 fusion.18
  26.5 1.5 %copy.47 = bf16[8,1,48,512]{3,2,0,1:T(8,128)(2,1)} copy(bf16[8,1,48,512]{2,0,1,3:T(8,128)(2,1)S(1)} %get-tuple-element.8) | data formatting | bytes 786432 | tf_op jit(solution)/shard_map/slice | solution.py:59
  28.0 0.7 copy.48
  28.7 0.1 broadcast_in_dim.78
  28.9 0.1 slice_bitcast_fusion.12
  31.6 0.4 fusion.5
  32.0 0.4 fusion.4
  32.4 0.4 fusion.7
  32.8 0.4 fusion.6
  33.2 0.2 copy-done
  33.3 0.4 fusion.1
  33.7 0.4 fusion
  34.1 0.4 fusion.3
  34.5 0.4 fusion.2
  34.9 1.0 pad_maximum_fusion.1
  35.9 0.2 pad_slice_fusion.1
  36.1 0.6 fusion.21
  36.7 0.6 fusion.20
  37.3 0.6 add_bitcast_fusion
  38.0 0.2 copy.57
  38.1 0.1 copy.52
  38.3 0.6 subtract_bitcast_fusion
  38.9 0.2 copy.56
  39.1 0.1 copy.51
  39.2 0.1 pad_maximum_fusion
  39.3 0.7 gather_fusion.1
  40.1 1.0 reshape.210
  41.1 0.2 concatenate.24
  41.3 1.8 %gather_fusion.2 = bf16[64,2,2304]{2,1,0:T(2,128)(2,1)S(1)} fusion(bf16[33,2,2304]{2,1,0:T(2,128)(2,1)S(1)} %concatenate.24, s32[1024]{0:T(1024)S(1)} %get-tuple-element.33), kind=kCustom, calls=%fused_computation.2 | custom fusion | bytes 1179904 | tf_op jit(solution)/shard_map/jit(_take)/gather | solution.py:116
  43.1 1.4 %broadcast_select_fusion = bf16[32,2,2,2304]{3,2,1,0:T(2,128)(2,1)} fusion(bf16[32,2,2,2304]{3,2,1,0:T(2,128)(2,1)S(1)} %bitcast.147, pred[32,2]{1,0:T(8,128)(4,1)S(1)} %broadcast_in_dim.78), kind=kLoop, calls=%fused_computation.20 | loop fusion | flops 294912 | bytes 1179712 | tf_op jit(solution)/shard_map/jit(_take)/select_n | solution.py:116
  44.5 18.6 %all-to-all-start.1 = ((bf16[32,2,2,2304]{3,2,1,0:T(2,128)(2,1)}), bf16[32,2,2,2304]{3,2,1,0:T(2,128)(2,1)S(1)}, u32[]{:S(2)}, u32[]{:S(2)}) async-start(bf16[32,2,2,2304]{3,2,1,0:T(2,128)(2,1)} %broadcast_select_fusion), calls=%async_computation.1 | async-start | bytes 1179648 | tf_op jit(solution)/shard_map/all_to_all | solution.py:118
  63.1 1.0 maximum_bitcast_fusion
  64.1 35.3 %all-to-all-done.1 = bf16[32,2,2,2304]{3,2,1,0:T(2,128)(2,1)S(1)} async-done(((bf16[32,2,2,2304]{3,2,1,0:T(2,128)(2,1)}), bf16[32,2,2,2304]{3,2,1,0:T(2,128)(2,1)S(1)}, u32[]{:S(2)}, u32[]{:S(2)}) %all-to-all-start.1) | async-done | bytes 589856 | tf_op jit(solution)/shard_map/all_to_all | solution.py:118
  99.4 0.8 copy.89
  (88 shorter events, 2.6 us)
Async XLA Ops:
  0.6 9.8 %copy-start.4 = (s32[1,32,1]{1,2,0:T(1,128)S(1)}, s32[1,32,1]{1,2,0:T(1,128)}, u32[]{:S(2)}) copy-start(s32[1,32,1]{1,2,0:T(1,128)} %param.19) | copy-start | bytes 388
  2.8 26.0 %all-to-all-start = ((bf16[16,2,32,544]{3,2,1,0:T(8,128)(2,1)}), bf16[16,2,32,544]{3,2,1,0:T(8,128)(2,1)S(1)}, u32[]{:S(2)}, u32[]{:S(2)}) async-start(bf16[16,2,32,544]{3,2,1,0:T(8,128)(2,1)} %broadcast_in_dim.71), calls=%async_computation | async-start | bytes 2621440 | tf_op jit(solution)/shard_map/all_to_all | solution.py:29
  10.4 3.5 %copy-start.5 = (s32[1,8]{1,0:T(1,128)S(1)}, s32[1,8]{1,0:T(1,128)}, u32[]{:S(2)}) copy-start(s32[1,8]{1,0:T(1,128)} %param.14) | copy-start | bytes 100
  15.8 4.1 %copy-start.6 = (s32[1,8]{1,0:T(1,128)S(1)}, s32[1,8]{1,0:T(1,128)}, u32[]{:S(2)}) copy-start(s32[1,8]{1,0:T(1,128)} %param.15) | copy-start | bytes 100
  15.8 4.2 %copy-start.3 = (s32[1,512]{1,0:T(1,128)S(1)}, s32[1,512]{1,0:T(1,128)}, u32[]{:S(2)}) copy-start(s32[1,512]{1,0:T(1,128)} %param.16) | copy-start | bytes 6148
  26.5 2.3 %copy-start.7 = (s32[1,32]{1,0:T(1,128)S(1)}, s32[1,32]{1,0:T(1,128)}, u32[]{:S(2)}) copy-start(s32[1,32]{1,0:T(1,128)} %param.18) | copy-start | bytes 388
  26.5 2.3 %copy-start.8 = (s32[1,32]{1,0:T(1,128)S(1)}, s32[1,32]{1,0:T(1,128)}, u32[]{:S(2)}) copy-start(s32[1,32]{1,0:T(1,128)} %param.17) | copy-start | bytes 388
  29.8 1.8 %copy-start.1 = (bf16[8,1,48,512]{3,2,0,1:T(8,128)(2,1)S(1)}, bf16[8,1,48,512]{3,2,0,1:T(8,128)(2,1)}, u32[]{:S(2)}) copy-start(bf16[8,1,48,512]{3,2,0,1:T(8,128)(2,1)} %copy.42) | copy-start | bytes 1179652
  31.0 1.4 %copy-start.2 = (bf16[8,1,48,512]{3,2,0,1:T(8,128)(2,1)S(1)}, bf16[8,1,48,512]{3,2,0,1:T(8,128)(2,1)}, u32[]{:S(2)}) copy-start(bf16[8,1,48,512]{3,2,0,1:T(8,128)(2,1)} %copy.47) | copy-start | bytes 1179652
  32.3 1.0 copy-start
  44.5 54.9 %all-to-all-start.1 = ((bf16[32,2,2,2304]{3,2,1,0:T(2,128)(2,1)}), bf16[32,2,2,2304]{3,2,1,0:T(2,128)(2,1)S(1)}, u32[]{:S(2)}, u32[]{:S(2)}) async-start(bf16[32,2,2,2304]{3,2,1,0:T(2,128)(2,1)} %broadcast_select_fusion), calls=%async_computation.1 | async-start | bytes 1179648 | tf_op jit(solution)/shard_map/all_to_all | solution.py:118

commit v9 on v7

--- a/solution.py
+++ b/solution.py
@@ -15,6 +15,11 @@
 
 def product(left, right):
     return jnp.einsum("prb,psb->prs", left, right, preferred_element_type=jnp.float32)
+
+
+def combine(by_real, by_imag):
+    half = by_real.shape[0] // 2
+    return jnp.stack([by_real[:half] - by_imag[half:], by_imag[:half] + by_real[half:]], 0)
 
 
 def gather_inverses(lower_rows, upper_rows):
@@ -54,30 +59,22 @@
     block_count = lower_masked.shape[0]
     rank_width = lower_masked.shape[2]
     panel_count = lower_masked.shape[3]
-    lower_real = lower_masked[:, 0].reshape(block_count * rank_width, panel_count)
-    lower_imag = lower_masked[:, 1].reshape(block_count * rank_width, panel_count)
-    upper_real = upper_pivoted[:, 0].reshape(block_count * rank_width, panel_count)
-    upper_imag = upper_pivoted[:, 1].reshape(block_count * rank_width, panel_count)
+    lower_rows = jnp.concatenate(
+        [lower_masked[:, 0].reshape(block_count * rank_width, panel_count),
+         lower_masked[:, 1].reshape(block_count * rank_width, panel_count)], axis=0)
+    upper_rows = jnp.concatenate(
+        [upper_pivoted[:, 0].reshape(block_count * rank_width, panel_count),
+         upper_pivoted[:, 1].reshape(block_count * rank_width, panel_count)], axis=0)
     contract_last = (((1,), (1,)), ((), ()))
     lower_piece, upper_piece = gather_inverses(lower_inverse[0], upper_inverse[0])
-    piece_real = upper_piece[0]
-    piece_imag = upper_piece[1]
-    real_part = jnp.dot(lower_real, piece_real, preferred_element_type=jnp.float32) - jnp.dot(
-        lower_imag, piece_imag, preferred_element_type=jnp.float32
+    lower_totals = combine(
+        jnp.dot(lower_rows, upper_piece[0], preferred_element_type=jnp.float32),
+        jnp.dot(lower_rows, upper_piece[1], preferred_element_type=jnp.float32),
     )
-    imag_part = jnp.dot(lower_real, piece_imag, preferred_element_type=jnp.float32) + jnp.dot(
-        lower_imag, piece_real, preferred_element_type=jnp.float32
+    upper_totals = combine(
+        lax.dot_general(upper_rows, lower_piece[0], contract_last, preferred_element_type=jnp.float32),
+        lax.dot_general(upper_rows, lower_piece[1], contract_last, preferred_element_type=jnp.float32),
     )
-    lower_totals = jnp.stack([real_part, imag_part], 0)
-    piece_real = lower_piece[0]
-    piece_imag = lower_piece[1]
-    real_part = lax.dot_general(
-        upper_real, piece_real, contract_last, preferred_element_type=jnp.float32
-    ) - lax.dot_general(upper_imag, piece_imag, contract_last, preferred_element_type=jnp.float32)
-    imag_part = lax.dot_general(
-        upper_real, piece_imag, contract_last, preferred_element_type=jnp.float32
-    ) + lax.dot_general(upper_imag, piece_real, contract_last, preferred_element_type=jnp.float32)
-    upper_totals = jnp.stack([real_part, imag_part], 0)
     lower_totals = lower_totals.astype(jnp.bfloat16)
     upper_totals = upper_totals.astype(jnp.bfloat16)
     lower_solved = jnp.transpose(
@@ -91,12 +88,11 @@
         upper_totals.reshape(2, block_count, rank_width, panel_count),
         ((0, 0), (0, 0), (0, lane_tile - rank_width), (0, 0)),
     ).reshape(2, block_count * lane_tile, panel_count)
-    real_part = lax.dot_general(
-        lower_totals[0], padded[0], contract_last, preferred_element_type=jnp.float32
-    ) - lax.dot_general(lower_totals[1], padded[1], contract_last, preferred_element_type=jnp.float32)
-    imag_part = lax.dot_general(
-        lower_totals[0], padded[1], contract_last, preferred_element_type=jnp.float32
-    ) + lax.dot_general(lower_totals[1], padded[0], contract_last, preferred_element_type=jnp.float32)
+    both_rows = lower_totals.reshape(2 * block_count * rank_width, panel_count)
+    real_part, imag_part = combine(
+        lax.dot_general(both_rows, padded[0], contract_last, preferred_element_type=jnp.float32),
+        lax.dot_general(both_rows, padded[1], contract_last, preferred_element_type=jnp.float32),
+    )
     grid = jnp.stack([real_part, imag_part], 0).reshape(2, block_count, rank_width, block_count, lane_tile)
     pair_count = pair_lower.shape[1]
     picked = grid[:, pair_lower[0], :, pair_upper[0], :][..., :rank_width]

time: 98.8 us -> 99.5 us (level)
  other arithmetic: 6.95 us -> 8.65 us
  matrix products: 5.8 us -> 4.65 us
    dot_general x12 -> x6, matrix products: 5.51 us -> 4.35 us  [the longest x1 1.01 us: per_device(): lax.dot_general(both_rows, padded[0], contract_last, preferred_element_ty...]
where the time goes in v9:
time: 99.5 us; the launch traced here: 99.1 us
  waiting for transfers between devices  35.3 us (35%)
  starting transfers between devices  26.9 us (27%)
  local copies, waits for them, and re-layouts  22.3 us (22%)
  other arithmetic  8.65 us (9%)
  matrix products  4.65 us (5%)
  between operations  1.3 us (1%)
    all_to_all x1, waiting for transfers between devices, per_device(): lax.all_to_all(buffer, 'clu', split_axis=0, concat_axis=0, tiled=True)  35.3 us
    all_to_all x1, starting transfers between devices, per_device(): lax.all_to_all(buffer, 'clu', split_axis=0, concat_axis=0, tiled=True)  19.3 us
    unnamed x52, local copies, waits for them, and re-layouts  7.92 us
    all_to_all x1, starting transfers between devices, gather_inverses(): lax.all_to_all(copies, 'grp', split_axis=0, concat_axis=0, tiled=True)  7.59 us
    gather x1, local copies, waits for them, and re-layouts, per_device(): upper_pivoted = jnp.take(upper_masked, pivots[0], axis=3)  2.95 us
  transfers between devices with their start and end apart: 2, of which 1 were waited for; matrix products, arithmetic and copies ran while one was open for 19% of the time, Pallas kernels for 0%

profile of v9, /device:TPU:1, one launch (start us, length us, event | category | flops | bytes accessed | tf_op | source)
XLA Modules:
  0.0 99.1 jit_solution(12422381025962937379)
XLA Ops:
  0.6 1.0 fusion.10
  1.6 1.2 %broadcast_in_dim.52 = bf16[16,2,32,544]{3,2,1,0:T(8,128)(2,1)} broadcast(bf16[2,32,544]{2,1,0:T(8,128)(2,1)S(1)} %fusion.10), dimensions={1,2,3} | broadcast | bytes 1183744 | tf_op jit(solution)/shard_map/broadcast_in_dim | solution.py:33
  2.8 7.6 %all-to-all-start = ((bf16[16,2,32,544]{3,2,1,0:T(8,128)(2,1)}), bf16[16,2,32,544]{3,2,1,0:T(8,128)(2,1)S(1)}, u32[]{:S(2)}, u32[]{:S(2)}) async-start(bf16[16,2,32,544]{3,2,1,0:T(8,128)(2,1)} %broadcast_in_dim.52), calls=%async_computation | async-start | bytes 2621440 | tf_op jit(solution)/shard_map/all_to_all | solution.py:34
  10.5 2.6 %copy.37 = bf16[1,8,2,48,512]{3,1,4,2,0:T(8,128)(2,1)S(1)} copy(bf16[1,8,2,48,512]{4,3,2,1,0:T(8,128)(2,1)} %param.12) | data formatting | bytes 1572864 | tf_op args[2]
  13.1 0.1 bitcast_select_fusion.1
  13.3 0.1 fusion.25
  13.4 1.5 %copy.39 = bf16[8,1,48,512]{3,2,0,1:T(8,128)(2,1)} copy(bf16[8,1,48,512]{2,0,3,1:T(8,128)(2,1)S(1)} %get-tuple-element.12) | data formatting | bytes 786432 | tf_op jit(solution)/shard_map/slice | solution.py:64
  14.9 1.5 %copy.38 = bf16[8,1,48,512]{3,2,0,1:T(8,128)(2,1)} copy(bf16[8,1,48,512]{2,0,3,1:T(8,128)(2,1)S(1)} %get-tuple-element.11) | data formatting | bytes 786432 | tf_op jit(solution)/shard_map/slice | solution.py:63
  16.4 2.6 %copy.42 = bf16[1,8,2,48,512]{3,1,4,2,0:T(8,128)(2,1)S(1)} copy(bf16[1,8,2,48,512]{4,3,2,1,0:T(8,128)(2,1)} %param.13) | data formatting | bytes 1572864 | tf_op args[3]
  19.1 1.5 %bitcast_select_fusion = bf16[8,2,48,512]{2,0,3,1:T(8,128)(2,1)} fusion(bf16[1,8,2,48,512]{3,1,4,2,0:T(8,128)(2,1)S(1)} %copy.42, pred[8,48]{1,0:T(8,128)(4,1)S(1)} %iota_compare_fusion.3), kind=kLoop, calls=%fused_computation.6 | loop fusion | flops 393216 | bytes 1573248 | tf_op jit(solution)/shard_map/jit(_where)/select_n | solution.py:13
  20.6 3.0 %gather_fusion = bf16[512,8,2,48]{3,1,2,0:T(8,128)(2,1)S(1)} fusion(bf16[8,2,48,512]{2,0,3,1:T(8,128)(2,1)} %bitcast_select_fusion, s32[1024]{0:T(1024)S(1)} %pad_clamp_fusion), kind=kCustom, calls=%fused_computation | custom fusion | bytes 1574912 | tf_op jit(solution)/shard_map/jit(_take)/gather | solution.py:58
  23.6 1.9 %select_bitcast_fusion = bf16[8,2,48,512]{2,0,1,3:T(8,128)(2,1)S(1)} fusion(bf16[512,8,2,48]{3,1,2,0:T(8,128)(2,1)S(1)} %gather_fusion, pred[512]{0:T(512)(128)(4,1)S(1)} %compare_and_fusion), kind=kLoop, calls=%fused_computation.8 | loop fusion | flops 393216 | bytes 1573376 | tf_op jit(solution)/shard_map/jit(_take)/select_n | solution.py:58
  25.5 0.1 fusion.24
  25.7 1.5 %copy.44 = bf16[8,1,48,512]{3,2,0,1:T(8,128)(2,1)} copy(bf16[8,1,48,512]{2,0,1,3:T(8,128)(2,1)S(1)} %get-tuple-element.10) | data formatting | bytes 786432 | tf_op jit(solution)/shard_map/slice | solution.py:67
  27.1 0.7 copy.43
  27.9 0.2 convert_reduce_fusion
  28.1 0.1 slice_bitcast_fusion.8
  29.2 0.1 slice.346
  29.3 0.1 slice.347
  29.7 0.1 slice_dynamic-update-slice_fusion
  29.8 0.1 constant_dynamic-update-slice_fusion.14
  29.9 0.1 constant_dynamic-update-slice_fusion.13
  30.0 0.1 constant_dynamic-update-slice_fusion.12
  30.8 0.6 fusion.8
  31.4 0.6 fusion.9
  32.0 0.4 copy-done.2
  32.4 0.6 fusion.6
  33.0 0.6 fusion.7
  33.6 0.4 fusion.3
  34.1 1.0 pad_maximum_fusion.3
  35.0 0.2 pad_slice_fusion
  35.2 0.4 fusion.5
  35.8 1.0 %fusion.27 = f32[768,1024]{1,0:T(8,128)S(1)} fusion(bf16[768,512]{1,0:T(8,128)(2,1)S(1)} %bitcast.116, bf16[1024,512]{1,0:T(8,128)(2,1)S(1)} %bitcast.119), kind=kOutput, calls=%fused_computation.114 | convolution fusion | flops 805306368 | bytes 4980736 | tf_op jit(solution)/shard_map/dot_general | solution.py:94
  36.8 1.0 %fusion.26 = f32[768,1024]{1,0:T(8,128)S(1)} fusion(bf16[768,512]{1,0:T(8,128)(2,1)S(1)} %bitcast.117, bf16[1024,512]{1,0:T(8,128)(2,1)S(1)} %bitcast.118), kind=kOutput, calls=%fused_computation.113 | convolution fusion | flops 805306368 | bytes 4980736 | tf_op jit(solution)/shard_map/dot_general | solution.py:93
  37.8 0.7 fusion.1
  38.5 0.2 copy.50
  38.7 0.1 copy.48
  38.9 0.2 copy.49
  39.0 0.1 copy.47
  39.2 0.1 pad_maximum_fusion
  39.3 0.7 gather_fusion.1
  40.0 1.4 %convert_element_type.93 = bf16[32,4608]{1,0:T(8,128)(2,1)S(1)} reshape(bf16[32,2,48,48]{3,2,1,0:T(8,128)(2,1)S(1)} %bitcast.124) | data formatting | bytes 589824 | tf_op jit(solution)/shard_map/convert_element_type | solution.py:99
  41.4 0.3 convolution_convert_fusion
  41.7 1.0 reshape.192
  42.7 19.3 %all-to-all-start.1 = ((bf16[32,2,2,2304]{3,2,1,0:T(2,128)(2,1)}), bf16[32,2,2,2304]{3,2,1,0:T(2,128)(2,1)S(1)}, u32[]{:S(2)}, u32[]{:S(2)}) async-start(bf16[32,2,2,2304]{3,2,1,0:T(2,128)(2,1)} %reshape.192), calls=%async_computation.1 | async-start | bytes 1179648 | tf_op jit(solution)/shard_map/all_to_all | solution.py:110
  62.0 1.0 maximum_bitcast_fusion
  63.0 35.3 %all-to-all-done.1 = bf16[32,2,2,2304]{3,2,1,0:T(2,128)(2,1)S(1)} async-done(((bf16[32,2,2,2304]{3,2,1,0:T(2,128)(2,1)}), bf16[32,2,2,2304]{3,2,1,0:T(2,128)(2,1)S(1)}, u32[]{:S(2)}, u32[]{:S(2)}) %all-to-all-start.1) | async-done | bytes 589856 | tf_op jit(solution)/shard_map/all_to_all | solution.py:110
  98.3 0.8 copy.82
  (81 shorter events, 2.0 us)
Async XLA Ops:
  2.8 25.2 %all-to-all-start = ((bf16[16,2,32,544]{3,2,1,0:T(8,128)(2,1)}), bf16[16,2,32,544]{3,2,1,0:T(8,128)(2,1)S(1)}, u32[]{:S(2)}, u32[]{:S(2)}) async-start(bf16[16,2,32,544]{3,2,1,0:T(8,128)(2,1)} %broadcast_in_dim.52), calls=%async_computation | async-start | bytes 2621440 | tf_op jit(solution)/shard_map/all_to_all | solution.py:34
  10.4 2.6 %copy-start.4 = (s32[1,8]{1,0:T(1,128)S(1)}, s32[1,8]{1,0:T(1,128)}, u32[]{:S(2)}) copy-start(s32[1,8]{1,0:T(1,128)} %param.14) | copy-start | bytes 100
  16.4 2.6 %copy-start.5 = (s32[1,8]{1,0:T(1,128)S(1)}, s32[1,8]{1,0:T(1,128)}, u32[]{:S(2)}) copy-start(s32[1,8]{1,0:T(1,128)} %param.15) | copy-start | bytes 100
  16.4 2.7 %copy-start.3 = (s32[1,512]{1,0:T(1,128)S(1)}, s32[1,512]{1,0:T(1,128)}, u32[]{:S(2)}) copy-start(s32[1,512]{1,0:T(1,128)} %param.16) | copy-start | bytes 6148
  25.6 2.2 %copy-start.6 = (s32[1,32,1]{1,2,0:T(1,128)S(1)}, s32[1,32,1]{1,2,0:T(1,128)}, u32[]{:S(2)}) copy-start(s32[1,32,1]{1,2,0:T(1,128)} %param.19) | copy-start | bytes 388
  25.7 2.4 %copy-start.7 = (s32[1,32]{1,0:T(1,128)S(1)}, s32[1,32]{1,0:T(1,128)}, u32[]{:S(2)}) copy-start(s32[1,32]{1,0:T(1,128)} %param.18) | copy-start | bytes 388
  25.7 2.4 %copy-start.8 = (s32[1,32]{1,0:T(1,128)S(1)}, s32[1,32]{1,0:T(1,128)}, u32[]{:S(2)}) copy-start(s32[1,32]{1,0:T(1,128)} %param.17) | copy-start | bytes 388
  29.4 1.4 %copy-start = (bf16[8,1,48,512]{3,2,0,1:T(8,128)(2,1)S(1)}, bf16[8,1,48,512]{3,2,0,1:T(8,128)(2,1)}, u32[]{:S(2)}) copy-start(bf16[8,1,48,512]{3,2,0,1:T(8,128)(2,1)} %copy.39) | copy-start | bytes 1179652
  29.5 1.4 %copy-start.1 = (bf16[8,1,48,512]{3,2,0,1:T(8,128)(2,1)S(1)}, bf16[8,1,48,512]{3,2,0,1:T(8,128)(2,1)}, u32[]{:S(2)}) copy-start(bf16[8,1,48,512]{3,2,0,1:T(8,128)(2,1)} %copy.38) | copy-start | bytes 1179652
  31.4 1.0 %copy-start.2 = (bf16[8,1,48,512]{3,2,0,1:T(8,128)(2,1)S(1)}, bf16[8,1,48,512]{3,2,0,1:T(8,128)(2,1)}, u32[]{:S(2)}) copy-start(bf16[8,1,48,512]{3,2,0,1:T(8,128)(2,1)} %copy.44) | copy-start | bytes 1179652
  42.7 55.6 %all-to-all-start.1 = ((bf16[32,2,2,2304]{3,2,1,0:T(2,128)(2,1)}), bf16[32,2,2,2304]{3,2,1,0:T(2,128)(2,1)S(1)}, u32[]{:S(2)}, u32[]{:S(2)}) async-start(bf16[32,2,2,2304]{3,2,1,0:T(2,128)(2,1)} %reshape.192), calls=%async_computation.1 | async-start | bytes 1179648 | tf_op jit(solution)/shard_map/all_to_all | solution.py:110

commit v10 on v7

--- a/solution.py
+++ b/solution.py
@@ -27,14 +27,12 @@
     packed = lax.dynamic_slice_in_dim(both, start, span, axis=2)
     copies = jnp.broadcast_to(packed[None], (groups,) + packed.shape)
     blocks = lax.all_to_all(copies, "grp", split_axis=0, concat_axis=0, tiled=True)
-    upper_blocks, lower_blocks = [], []
+    both_rows = []
     for source in range(groups):
-        block = blocks[source]
-        cut = width - source * rows
-        upper_blocks.append(jnp.pad(block[..., :cut], ((0, 0), (0, 0), (source * rows, 0))))
-        lower_blocks.append(jnp.pad(block[..., cut:], ((0, 0), (0, 0), (0, cut - rows))))
-    return jnp.concatenate(lower_blocks, axis=1), jnp.concatenate(upper_blocks, axis=1)
-
+        offset = source * rows
+        both_rows.append(jnp.pad(blocks[source], ((0, 0), (0, 0), (offset, 2 * width - span - offset))))
+    both_full = jnp.concatenate(both_rows, axis=1)
+    return both_full[..., width:], both_full[..., :width]
 
 def per_device(
     lower_inverse,

time: 98.8 us -> 97.6 us (0.988)
  local copies, waits for them, and re-layouts: 22 us -> 20.9 us
    slice x30 -> x0, local copies, waits for them, and re-layouts: 1 us -> none  [the longest x15 0.92 us: gather_inverses(): block[..., cut:]]
    unnamed x52 -> x38, local copies, waits for them, and re-layouts: 7.64 us -> 7.62 us
where the time goes in v10:
time: 97.6 us; the launch traced here: 97.1 us
  waiting for transfers between devices  35.3 us (36%)
  starting transfers between devices  27 us (28%)
  local copies, waits for them, and re-layouts  20.9 us (21%)
  other arithmetic  6.96 us (7%)
  matrix products  5.85 us (6%)
  between operations  1.13 us (1%)
    all_to_all x1, waiting for transfers between devices, per_device(): lax.all_to_all(buffer, 'clu', split_axis=0, concat_axis=0, tiled=True)  35.3 us
    all_to_all x1, starting transfers between devices, per_device(): lax.all_to_all(buffer, 'clu', split_axis=0, concat_axis=0, tiled=True)  19.4 us
    unnamed x38, local copies, waits for them, and re-layouts  7.62 us
    all_to_all x1, starting transfers between devices, gather_inverses(): lax.all_to_all(copies, 'grp', split_axis=0, concat_axis=0, tiled=True)  7.59 us
    gather x1, local copies, waits for them, and re-layouts, per_device(): upper_pivoted = jnp.take(upper_masked, pivots[0], axis=3)  2.95 us
  transfers between devices with their start and end apart: 2, of which 1 were waited for; matrix products, arithmetic and copies ran while one was open for 19% of the time, Pallas kernels for 0%

profile of v10, /device:TPU:1, one launch (start us, length us, event | category | flops | bytes accessed | tf_op | source)
XLA Modules:
  0.0 97.1 jit_solution(4359584942447912879)
XLA Ops:
  0.6 1.0 fusion.8
  1.6 1.2 %broadcast_in_dim.52 = bf16[16,2,32,544]{3,2,1,0:T(8,128)(2,1)} broadcast(bf16[2,32,544]{2,1,0:T(8,128)(2,1)S(1)} %fusion.8), dimensions={1,2,3} | broadcast | bytes 1183744 | tf_op jit(solution)/shard_map/broadcast_in_dim | solution.py:28
  2.8 7.6 %all-to-all-start = ((bf16[16,2,32,544]{3,2,1,0:T(8,128)(2,1)}), bf16[16,2,32,544]{3,2,1,0:T(8,128)(2,1)S(1)}, u32[]{:S(2)}, u32[]{:S(2)}) async-start(bf16[16,2,32,544]{3,2,1,0:T(8,128)(2,1)} %broadcast_in_dim.52), calls=%async_computation | async-start | bytes 2621440 | tf_op jit(solution)/shard_map/all_to_all | solution.py:29
  10.5 2.6 %copy.37 = bf16[1,8,2,48,512]{3,1,4,2,0:T(8,128)(2,1)S(1)} copy(bf16[1,8,2,48,512]{4,3,2,1,0:T(8,128)(2,1)} %param.12) | data formatting | bytes 1572864 | tf_op args[2]
  13.1 0.1 bitcast_select_fusion.1
  13.3 0.1 fusion.19
  13.4 1.5 %copy.38 = bf16[8,1,48,512]{3,2,0,1:T(8,128)(2,1)} copy(bf16[8,1,48,512]{2,0,3,1:T(8,128)(2,1)S(1)} %get-tuple-element.6) | data formatting | bytes 786432 | tf_op jit(solution)/shard_map/slice | solution.py:55
  14.9 1.5 %copy.39 = bf16[8,1,48,512]{3,2,0,1:T(8,128)(2,1)} copy(bf16[8,1,48,512]{2,0,3,1:T(8,128)(2,1)S(1)} %get-tuple-element.5) | data formatting | bytes 786432 | tf_op jit(solution)/shard_map/slice | solution.py:56
  16.4 2.6 %copy.42 = bf16[1,8,2,48,512]{3,1,4,2,0:T(8,128)(2,1)S(1)} copy(bf16[1,8,2,48,512]{4,3,2,1,0:T(8,128)(2,1)} %param.13) | data formatting | bytes 1572864 | tf_op args[3]
  19.1 1.5 %bitcast_select_fusion = bf16[8,2,48,512]{2,0,3,1:T(8,128)(2,1)} fusion(bf16[1,8,2,48,512]{3,1,4,2,0:T(8,128)(2,1)S(1)} %copy.42, pred[8,48]{1,0:T(8,128)(4,1)S(1)} %iota_compare_fusion.3), kind=kLoop, calls=%fused_computation.6 | loop fusion | flops 393216 | bytes 1573248 | tf_op jit(solution)/shard_map/jit(_where)/select_n | solution.py:13
  20.6 3.0 %gather_fusion = bf16[512,8,2,48]{3,1,2,0:T(8,128)(2,1)S(1)} fusion(bf16[8,2,48,512]{2,0,3,1:T(8,128)(2,1)} %bitcast_select_fusion, s32[1024]{0:T(1024)S(1)} %pad_clamp_fusion), kind=kCustom, calls=%fused_computation | custom fusion | bytes 1574912 | tf_op jit(solution)/shard_map/jit(_take)/gather | solution.py:51
  23.5 1.9 %select_bitcast_fusion = bf16[8,2,48,512]{2,0,1,3:T(8,128)(2,1)S(1)} fusion(bf16[512,8,2,48]{3,1,2,0:T(8,128)(2,1)S(1)} %gather_fusion, pred[512]{0:T(512)(128)(4,1)S(1)} %compare_and_fusion), kind=kLoop, calls=%fused_computation.8 | loop fusion | flops 393216 | bytes 1573376 | tf_op jit(solution)/shard_map/jit(_take)/select_n | solution.py:51
  25.5 0.1 fusion.18
  25.6 1.5 %copy.43 = bf16[8,1,48,512]{3,2,0,1:T(8,128)(2,1)} copy(bf16[8,1,48,512]{2,0,1,3:T(8,128)(2,1)S(1)} %get-tuple-element.4) | data formatting | bytes 786432 | tf_op jit(solution)/shard_map/slice | solution.py:57
  27.1 0.7 copy.44
  27.8 0.2 convert_reduce_fusion
  28.1 0.1 slice_bitcast_fusion.12
  28.4 0.1 pad_dynamic-update-slice_fusion.12
  28.6 0.1 pad_dynamic-update-slice_fusion.9
  29.0 0.1 pad_dynamic-update-slice_fusion.5
  29.5 0.4 fusion.5
  29.9 0.4 fusion.4
  30.3 0.4 fusion.7
  30.7 0.4 fusion.6
  31.1 0.1 copy-done
  31.3 0.4 fusion.1
  31.6 0.4 fusion
  32.0 0.4 fusion.3
  32.4 0.4 fusion.2
  32.8 1.0 %pad_maximum_fusion.1 = (bf16[2,8,48,512]{3,2,0,1:T(8,128)(2,1)S(1)}, bf16[1,8,2,48,512]{4,3,2,1,0:T(8,128)(2,1)}) fusion(bf16[1,8,48,512]{3,2,0,1:T(8,128)(2,1)S(1)} %bitcast.147, bf16[1,8,48,512]{3,2,0,1:T(8,128)(2,1)S(1)} %bitcast.148), kind=kLoop, calls=%fused_computation.21 | loop fusion | flops 393216 | bytes 2359296 | tf_op jit(solution)/shard_map/stack | solution.py:78
  33.8 0.2 pad_slice_fusion.1
  34.0 0.6 fusion.21
  34.6 0.6 fusion.20
  35.3 0.6 add_bitcast_fusion
  35.9 0.2 copy.50
  36.1 0.1 copy.48
  36.2 0.6 subtract_bitcast_fusion
  36.8 0.2 copy.49
  37.0 0.1 copy.47
  37.1 0.1 pad_maximum_fusion
  37.3 0.7 gather_fusion.1
  38.0 1.4 %convert_element_type.50 = bf16[32,4608]{1,0:T(8,128)(2,1)S(1)} reshape(bf16[32,2,48,48]{3,2,1,0:T(8,128)(2,1)S(1)} %bitcast.143) | data formatting | bytes 589824 | tf_op jit(solution)/shard_map/convert_element_type | solution.py:101
  39.4 0.3 convolution_convert_fusion
  39.7 1.0 reshape.181
  40.6 19.4 %all-to-all-start.1 = ((bf16[32,2,2,2304]{3,2,1,0:T(2,128)(2,1)}), bf16[32,2,2,2304]{3,2,1,0:T(2,128)(2,1)S(1)}, u32[]{:S(2)}, u32[]{:S(2)}) async-start(bf16[32,2,2,2304]{3,2,1,0:T(2,128)(2,1)} %reshape.181), calls=%async_computation.1 | async-start | bytes 1179648 | tf_op jit(solution)/shard_map/all_to_all | solution.py:112
  60.0 1.0 maximum_bitcast_fusion
  61.0 35.3 %all-to-all-done.1 = bf16[32,2,2,2304]{3,2,1,0:T(2,128)(2,1)S(1)} async-done(((bf16[32,2,2,2304]{3,2,1,0:T(2,128)(2,1)}), bf16[32,2,2,2304]{3,2,1,0:T(2,128)(2,1)S(1)}, u32[]{:S(2)}, u32[]{:S(2)}) %all-to-all-start.1) | async-done | bytes 589856 | tf_op jit(solution)/shard_map/all_to_all | solution.py:112
  96.3 0.8 copy.67
  (38 shorter events, 1.1 us)
Async XLA Ops:
  2.8 25.2 %all-to-all-start = ((bf16[16,2,32,544]{3,2,1,0:T(8,128)(2,1)}), bf16[16,2,32,544]{3,2,1,0:T(8,128)(2,1)S(1)}, u32[]{:S(2)}, u32[]{:S(2)}) async-start(bf16[16,2,32,544]{3,2,1,0:T(8,128)(2,1)} %broadcast_in_dim.52), calls=%async_computation | async-start | bytes 2621440 | tf_op jit(solution)/shard_map/all_to_all | solution.py:29
  10.4 2.6 %copy-start.4 = (s32[1,8]{1,0:T(1,128)S(1)}, s32[1,8]{1,0:T(1,128)}, u32[]{:S(2)}) copy-start(s32[1,8]{1,0:T(1,128)} %param.14) | copy-start | bytes 100
  14.9 4.1 %copy-start.5 = (s32[1,8]{1,0:T(1,128)S(1)}, s32[1,8]{1,0:T(1,128)}, u32[]{:S(2)}) copy-start(s32[1,8]{1,0:T(1,128)} %param.15) | copy-start | bytes 100
  14.9 4.2 %copy-start.3 = (s32[1,512]{1,0:T(1,128)S(1)}, s32[1,512]{1,0:T(1,128)}, u32[]{:S(2)}) copy-start(s32[1,512]{1,0:T(1,128)} %param.16) | copy-start | bytes 6148
  25.6 2.2 %copy-start.6 = (s32[1,32,1]{1,2,0:T(1,128)S(1)}, s32[1,32,1]{1,2,0:T(1,128)}, u32[]{:S(2)}) copy-start(s32[1,32,1]{1,2,0:T(1,128)} %param.19) | copy-start | bytes 388
  25.6 2.4 %copy-start.7 = (s32[1,32]{1,0:T(1,128)S(1)}, s32[1,32]{1,0:T(1,128)}, u32[]{:S(2)}) copy-start(s32[1,32]{1,0:T(1,128)} %param.18) | copy-start | bytes 388
  25.6 2.4 %copy-start.8 = (s32[1,32]{1,0:T(1,128)S(1)}, s32[1,32]{1,0:T(1,128)}, u32[]{:S(2)}) copy-start(s32[1,32]{1,0:T(1,128)} %param.17) | copy-start | bytes 388
  28.2 1.3 %copy-start.1 = (bf16[8,1,48,512]{3,2,0,1:T(8,128)(2,1)S(1)}, bf16[8,1,48,512]{3,2,0,1:T(8,128)(2,1)}, u32[]{:S(2)}) copy-start(bf16[8,1,48,512]{3,2,0,1:T(8,128)(2,1)} %copy.38) | copy-start | bytes 1179652
  29.2 1.1 %copy-start.2 = (bf16[8,1,48,512]{3,2,0,1:T(8,128)(2,1)S(1)}, bf16[8,1,48,512]{3,2,0,1:T(8,128)(2,1)}, u32[]{:S(2)}) copy-start(bf16[8,1,48,512]{3,2,0,1:T(8,128)(2,1)} %copy.43) | copy-start | bytes 1179652
  30.3 1.0 %copy-start = (bf16[8,1,48,512]{3,2,0,1:T(8,128)(2,1)S(1)}, bf16[8,1,48,512]{3,2,0,1:T(8,128)(2,1)}, u32[]{:S(2)}) copy-start(bf16[8,1,48,512]{3,2,0,1:T(8,128)(2,1)} %copy.39) | copy-start | bytes 1179652
  40.6 55.7 %all-to-all-start.1 = ((bf16[32,2,2,2304]{3,2,1,0:T(2,128)(2,1)}), bf16[32,2,2,2304]{3,2,1,0:T(2,128)(2,1)S(1)}, u32[]{:S(2)}, u32[]{:S(2)}) async-start(bf16[32,2,2,2304]{3,2,1,0:T(2,128)(2,1)} %reshape.181), calls=%async_computation.1 | async-start | bytes 1179648 | tf_op jit(solution)/shard_map/all_to_all | solution.py:112

commit v11 on v10

--- a/solution.py
+++ b/solution.py
@@ -89,12 +89,12 @@
         upper_totals.reshape(2, block_count, rank_width, panel_count),
         ((0, 0), (0, 0), (0, lane_tile - rank_width), (0, 0)),
     ).reshape(2, block_count * lane_tile, panel_count)
-    real_part = lax.dot_general(
-        lower_totals[0], padded[0], contract_last, preferred_element_type=jnp.float32
-    ) - lax.dot_general(lower_totals[1], padded[1], contract_last, preferred_element_type=jnp.float32)
-    imag_part = lax.dot_general(
-        lower_totals[0], padded[1], contract_last, preferred_element_type=jnp.float32
-    ) + lax.dot_general(lower_totals[1], padded[0], contract_last, preferred_element_type=jnp.float32)
+    both_rows = lower_totals.reshape(2 * block_count * rank_width, panel_count)
+    by_real = lax.dot_general(both_rows, padded[0], contract_last, preferred_element_type=jnp.float32)
+    by_imag = lax.dot_general(both_rows, padded[1], contract_last, preferred_element_type=jnp.float32)
+    half = block_count * rank_width
+    real_part = by_real[:half] - by_imag[half:]
+    imag_part = by_imag[:half] + by_real[half:]
     grid = jnp.stack([real_part, imag_part], 0).reshape(2, block_count, rank_width, block_count, lane_tile)
     pair_count = pair_lower.shape[1]
     picked = grid[:, pair_lower[0], :, pair_upper[0], :][..., :rank_width]

time: 97.6 us -> 97.9 us (level)
    dot_general x4 -> x2, matrix products: 2.45 us -> 2.02 us  [the longest x1 1.01 us: per_device(): lax.dot_general(both_rows, padded[1], contract_last, preferred_element_ty...]
where the time goes in v11:
time: 97.9 us; the launch traced here: 97.5 us
  waiting for transfers between devices  35.3 us (36%)
  starting transfers between devices  27 us (28%)
  local copies, waits for them, and re-layouts  20.9 us (21%)
  other arithmetic  7.77 us (8%)
  matrix products  5.42 us (6%)
  between operations  1.13 us (1%)
    all_to_all x1, waiting for transfers between devices, per_device(): lax.all_to_all(buffer, 'clu', split_axis=0, concat_axis=0, tiled=True)  35.3 us
    all_to_all x1, starting transfers between devices, per_device(): lax.all_to_all(buffer, 'clu', split_axis=0, concat_axis=0, tiled=True)  19.4 us
    unnamed x38, local copies, waits for them, and re-layouts  7.62 us
    all_to_all x1, starting transfers between devices, gather_inverses(): lax.all_to_all(copies, 'grp', split_axis=0, concat_axis=0, tiled=True)  7.59 us
    gather x1, local copies, waits for them, and re-layouts, per_device(): upper_pivoted = jnp.take(upper_masked, pivots[0], axis=3)  2.95 us
  transfers between devices with their start and end apart: 2, of which 1 were waited for; matrix products, arithmetic and copies ran while one was open for 19% of the time, Pallas kernels for 0%

profile of v11, /device:TPU:1, one launch (start us, length us, event | category | flops | bytes accessed | tf_op | source)
XLA Modules:
  0.0 97.5 jit_solution(15833489501913473848)
XLA Ops:
  0.6 1.0 fusion.10
  1.6 1.2 %broadcast_in_dim.52 = bf16[16,2,32,544]{3,2,1,0:T(8,128)(2,1)} broadcast(bf16[2,32,544]{2,1,0:T(8,128)(2,1)S(1)} %fusion.10), dimensions={1,2,3} | broadcast | bytes 1183744 | tf_op jit(solution)/shard_map/broadcast_in_dim | solution.py:28
  2.8 7.6 %all-to-all-start = ((bf16[16,2,32,544]{3,2,1,0:T(8,128)(2,1)}), bf16[16,2,32,544]{3,2,1,0:T(8,128)(2,1)S(1)}, u32[]{:S(2)}, u32[]{:S(2)}) async-start(bf16[16,2,32,544]{3,2,1,0:T(8,128)(2,1)} %broadcast_in_dim.52), calls=%async_computation | async-start | bytes 2621440 | tf_op jit(solution)/shard_map/all_to_all | solution.py:29
  10.4 2.6 %copy.37 = bf16[1,8,2,48,512]{3,1,4,2,0:T(8,128)(2,1)S(1)} copy(bf16[1,8,2,48,512]{4,3,2,1,0:T(8,128)(2,1)} %param.12) | data formatting | bytes 1572864 | tf_op args[2]
  13.1 0.1 bitcast_select_fusion.1
  13.3 0.1 fusion.21
  13.4 1.5 %copy.38 = bf16[8,1,48,512]{3,2,0,1:T(8,128)(2,1)} copy(bf16[8,1,48,512]{2,0,3,1:T(8,128)(2,1)S(1)} %get-tuple-element.8) | data formatting | bytes 786432 | tf_op jit(solution)/shard_map/slice | solution.py:55
  14.9 1.5 %copy.39 = bf16[8,1,48,512]{3,2,0,1:T(8,128)(2,1)} copy(bf16[8,1,48,512]{2,0,3,1:T(8,128)(2,1)S(1)} %get-tuple-element.7) | data formatting | bytes 786432 | tf_op jit(solution)/shard_map/slice | solution.py:56
  16.4 2.6 %copy.42 = bf16[1,8,2,48,512]{3,1,4,2,0:T(8,128)(2,1)S(1)} copy(bf16[1,8,2,48,512]{4,3,2,1,0:T(8,128)(2,1)} %param.13) | data formatting | bytes 1572864 | tf_op args[3]
  19.1 1.5 %bitcast_select_fusion = bf16[8,2,48,512]{2,0,3,1:T(8,128)(2,1)} fusion(bf16[1,8,2,48,512]{3,1,4,2,0:T(8,128)(2,1)S(1)} %copy.42, pred[8,48]{1,0:T(8,128)(4,1)S(1)} %iota_compare_fusion.3), kind=kLoop, calls=%fused_computation.6 | loop fusion | flops 393216 | bytes 1573248 | tf_op jit(solution)/shard_map/jit(_where)/select_n | solution.py:13
  20.6 3.0 %gather_fusion = bf16[512,8,2,48]{3,1,2,0:T(8,128)(2,1)S(1)} fusion(bf16[8,2,48,512]{2,0,3,1:T(8,128)(2,1)} %bitcast_select_fusion, s32[1024]{0:T(1024)S(1)} %pad_clamp_fusion), kind=kCustom, calls=%fused_computation | custom fusion | bytes 1574912 | tf_op jit(solution)/shard_map/jit(_take)/gather | solution.py:51
  23.5 1.9 %select_bitcast_fusion = bf16[8,2,48,512]{2,0,1,3:T(8,128)(2,1)S(1)} fusion(bf16[512,8,2,48]{3,1,2,0:T(8,128)(2,1)S(1)} %gather_fusion, pred[512]{0:T(512)(128)(4,1)S(1)} %compare_and_fusion), kind=kLoop, calls=%fused_computation.8 | loop fusion | flops 393216 | bytes 1573376 | tf_op jit(solution)/shard_map/jit(_take)/select_n | solution.py:51
  25.5 0.1 fusion.20
  25.6 1.5 %copy.43 = bf16[8,1,48,512]{3,2,0,1:T(8,128)(2,1)} copy(bf16[8,1,48,512]{2,0,1,3:T(8,128)(2,1)S(1)} %get-tuple-element.6) | data formatting | bytes 786432 | tf_op jit(solution)/shard_map/slice | solution.py:57
  27.1 0.7 copy.44
  27.8 0.2 convert_reduce_fusion
  28.1 0.1 slice_bitcast_fusion.12
  28.2 0.1 pad_dynamic-update-slice_fusion.14
  28.3 0.1 pad_dynamic-update-slice_fusion.13
  28.4 0.1 pad_dynamic-update-slice_fusion.12
  28.5 0.1 pad_dynamic-update-slice_fusion.10
  29.5 0.4 fusion.7
  29.9 0.4 fusion.6
  30.3 0.4 fusion.9
  30.7 0.4 fusion.8
  31.1 0.1 copy-done
  31.3 0.4 fusion.3
  31.6 0.4 fusion.2
  32.0 0.4 fusion.5
  32.4 0.4 fusion.4
  32.8 1.0 %pad_maximum_fusion.1 = (bf16[2,8,48,512]{3,2,0,1:T(8,128)(2,1)S(1)}, bf16[1,8,2,48,512]{4,3,2,1,0:T(8,128)(2,1)}) fusion(bf16[1,8,48,512]{3,2,0,1:T(8,128)(2,1)S(1)} %bitcast.148, bf16[1,8,48,512]{3,2,0,1:T(8,128)(2,1)S(1)} %bitcast.149), kind=kLoop, calls=%fused_computation.23 | loop fusion | flops 393216 | bytes 2359296 | tf_op jit(solution)/shard_map/stack | solution.py:78
  33.8 0.2 pad_slice_fusion
  34.1 1.0 %fusion.23 = f32[768,1024]{1,0:T(8,128)S(1)} fusion(bf16[768,512]{1,0:T(8,128)(2,1)S(1)} %bitcast.128, bf16[1024,512]{1,0:T(8,128)(2,1)S(1)} %bitcast.131), kind=kOutput, calls=%fused_computation.92 | convolution fusion | flops 805306368 | bytes 4980736 | tf_op jit(solution)/shard_map/dot_general | solution.py:94
  35.1 1.0 %fusion.22 = f32[768,1024]{1,0:T(8,128)S(1)} fusion(bf16[768,512]{1,0:T(8,128)(2,1)S(1)} %bitcast.129, bf16[1024,512]{1,0:T(8,128)(2,1)S(1)} %bitcast.130), kind=kOutput, calls=%fused_computation.91 | convolution fusion | flops 805306368 | bytes 4980736 | tf_op jit(solution)/shard_map/dot_general | solution.py:93
  36.1 0.7 fusion.1
  36.9 0.2 copy.50
  37.1 0.1 copy.48
  37.2 0.2 copy.49
  37.4 0.1 copy.47
  37.5 0.1 pad_maximum_fusion
  37.7 0.7 gather_fusion.1
  38.4 1.4 %convert_element_type.65 = bf16[32,4608]{1,0:T(8,128)(2,1)S(1)} reshape(bf16[32,2,48,48]{3,2,1,0:T(8,128)(2,1)S(1)} %bitcast.144) | data formatting | bytes 589824 | tf_op jit(solution)/shard_map/convert_element_type | solution.py:101
  39.8 0.3 convolution_convert_fusion
  40.1 1.0 reshape.192
  41.0 19.4 %all-to-all-start.1 = ((bf16[32,2,2,2304]{3,2,1,0:T(2,128)(2,1)}), bf16[32,2,2,2304]{3,2,1,0:T(2,128)(2,1)S(1)}, u32[]{:S(2)}, u32[]{:S(2)}) async-start(bf16[32,2,2,2304]{3,2,1,0:T(2,128)(2,1)} %reshape.192), calls=%async_computation.1 | async-start | bytes 1179648 | tf_op jit(solution)/shard_map/all_to_all | solution.py:112
  60.4 1.0 maximum_bitcast_fusion
  61.3 35.3 %all-to-all-done.1 = bf16[32,2,2,2304]{3,2,1,0:T(2,128)(2,1)S(1)} async-done(((bf16[32,2,2,2304]{3,2,1,0:T(2,128)(2,1)}), bf16[32,2,2,2304]{3,2,1,0:T(2,128)(2,1)S(1)}, u32[]{:S(2)}, u32[]{:S(2)}) %all-to-all-start.1) | async-done | bytes 589856 | tf_op jit(solution)/shard_map/all_to_all | solution.py:112
  96.7 0.8 copy.67
  (38 shorter events, 1.1 us)
Async XLA Ops:
  2.8 25.2 %all-to-all-start = ((bf16[16,2,32,544]{3,2,1,0:T(8,128)(2,1)}), bf16[16,2,32,544]{3,2,1,0:T(8,128)(2,1)S(1)}, u32[]{:S(2)}, u32[]{:S(2)}) async-start(bf16[16,2,32,544]{3,2,1,0:T(8,128)(2,1)} %broadcast_in_dim.52), calls=%async_computation | async-start | bytes 2621440 | tf_op jit(solution)/shard_map/all_to_all | solution.py:29
  10.4 2.6 %copy-start.4 = (s32[1,8]{1,0:T(1,128)S(1)}, s32[1,8]{1,0:T(1,128)}, u32[]{:S(2)}) copy-start(s32[1,8]{1,0:T(1,128)} %param.14) | copy-start | bytes 100
  14.9 4.1 %copy-start.5 = (s32[1,8]{1,0:T(1,128)S(1)}, s32[1,8]{1,0:T(1,128)}, u32[]{:S(2)}) copy-start(s32[1,8]{1,0:T(1,128)} %param.15) | copy-start | bytes 100
  14.9 4.2 %copy-start.3 = (s32[1,512]{1,0:T(1,128)S(1)}, s32[1,512]{1,0:T(1,128)}, u32[]{:S(2)}) copy-start(s32[1,512]{1,0:T(1,128)} %param.16) | copy-start | bytes 6148
  25.6 2.2 %copy-start.6 = (s32[1,32,1]{1,2,0:T(1,128)S(1)}, s32[1,32,1]{1,2,0:T(1,128)}, u32[]{:S(2)}) copy-start(s32[1,32,1]{1,2,0:T(1,128)} %param.19) | copy-start | bytes 388
  25.6 2.4 %copy-start.7 = (s32[1,32]{1,0:T(1,128)S(1)}, s32[1,32]{1,0:T(1,128)}, u32[]{:S(2)}) copy-start(s32[1,32]{1,0:T(1,128)} %param.18) | copy-start | bytes 388
  25.6 2.4 %copy-start.8 = (s32[1,32]{1,0:T(1,128)S(1)}, s32[1,32]{1,0:T(1,128)}, u32[]{:S(2)}) copy-start(s32[1,32]{1,0:T(1,128)} %param.17) | copy-start | bytes 388
  28.2 1.3 %copy-start.1 = (bf16[8,1,48,512]{3,2,0,1:T(8,128)(2,1)S(1)}, bf16[8,1,48,512]{3,2,0,1:T(8,128)(2,1)}, u32[]{:S(2)}) copy-start(bf16[8,1,48,512]{3,2,0,1:T(8,128)(2,1)} %copy.38) | copy-start | bytes 1179652
  29.2 1.1 %copy-start.2 = (bf16[8,1,48,512]{3,2,0,1:T(8,128)(2,1)S(1)}, bf16[8,1,48,512]{3,2,0,1:T(8,128)(2,1)}, u32[]{:S(2)}) copy-start(bf16[8,1,48,512]{3,2,0,1:T(8,128)(2,1)} %copy.43) | copy-start | bytes 1179652
  30.3 1.0 %copy-start = (bf16[8,1,48,512]{3,2,0,1:T(8,128)(2,1)S(1)}, bf16[8,1,48,512]{3,2,0,1:T(8,128)(2,1)}, u32[]{:S(2)}) copy-start(bf16[8,1,48,512]{3,2,0,1:T(8,128)(2,1)} %copy.39) | copy-start | bytes 1179652
  41.0 55.7 %all-to-all-start.1 = ((bf16[32,2,2,2304]{3,2,1,0:T(2,128)(2,1)}), bf16[32,2,2,2304]{3,2,1,0:T(2,128)(2,1)S(1)}, u32[]{:S(2)}, u32[]{:S(2)}) async-start(bf16[32,2,2,2304]{3,2,1,0:T(2,128)(2,1)} %reshape.192), calls=%async_computation.1 | async-start | bytes 1179648 | tf_op jit(solution)/shard_map/all_to_all | solution.py:112
